TPU v7x, 768 devices: a whole 4x8x12 slice. The times are simulated.
768 devices in a mesh: dp: 24 (over x_hi, z), row: 2 (over x_lo), fsdp: 16 (over y, core).
Axes of the slice: x: 4 (x_hi: 2, x_lo: 2; x = x_hi * 2 + x_lo), y: 8, z: 12, core: 2. Of those that a mesh axis runs over, the one named last changes fastest.
Arguments:
- images: bfloat16 [384, 16, 16, 1536], P(('dp', 'fsdp'), 'row'), may hold values from -6 to 6
- kernel: float32 [7, 7, 1536], replicated, may hold values from -0.875 to 0.875
- conv_bias: float32 [1536], replicated, may hold values from -3 to 3
- ln_gain: float32 [1536], replicated, may hold values from 0.5 to 2
- ln_shift: float32 [1536], replicated, may hold values from -3 to 3
- w_up: bfloat16 [1536, 3072], P('fsdp', 'row'), may hold values from -0.15625 to 0.15625
- cotangent: bfloat16 [384, 16, 16, 3072], P(('dp', 'fsdp'), None, None, 'row'), may hold values from -0.1875 to 0.1875
Outputs:
- hidden: bfloat16 [384, 16, 16, 3072], P(('dp', 'fsdp'), None, None, 'row')
- grad_weight: float32 [24, 1536, 3072], P('dp', 'fsdp', 'row')
- grad_kernel: float32 [7, 7, 1536], replicated
- grad_vectors: float32 [3, 1536], replicated
All inputs are finite; a program needn't handle non-finite values.
Results may differ from a plain program's by a relative error of at most 0.02.
Values may be sent and summed in bfloat16 or wider, within the bound.
No kernel may reach another device: no remote copies, remote signals or barrier semaphores. Data moves between devices by JAX's collectives and lax.ppermute only.
A program may use at most 64 MiB of HBM per device.

v0:
```python
import jax
import jax.numpy as jnp
from jax import lax
from jax.sharding import PartitionSpec as P

norm_epsilon = 1e-06


def gelu_exact(values):
    return jax.nn.gelu(values, approximate=False)


def conv_norm(images, kernel, conv_bias, ln_gain, ln_shift):
    source = images.astype(jnp.float32)
    map_side = source.shape[1]
    padded = jnp.pad(source, ((0, 0), (3, 3), (3, 3), (0, 0)))
    conv_out = jnp.zeros_like(source) + conv_bias
    for tap_row in range(7):
        for tap_col in range(7):
            conv_out = (
                conv_out
                + padded[:, tap_row : tap_row + map_side, tap_col : tap_col + map_side, :]
                * kernel[tap_row, tap_col]
            )
    centre = jnp.mean(conv_out, axis=-1, keepdims=True)
    spread = jnp.mean(jnp.square(conv_out - centre), axis=-1, keepdims=True)
    scale_inv = lax.rsqrt(spread + norm_epsilon)
    unit_field = (conv_out - centre) * scale_inv
    normed = (unit_field * ln_gain + ln_shift).astype(jnp.bfloat16)
    return (padded, unit_field, scale_inv, normed)


def norm_conv_grads(padded, unit_field, scale_inv, grad_normed, ln_gain):
    map_side = unit_field.shape[1]
    grad_gain = jnp.sum(grad_normed * unit_field, axis=(0, 1, 2))
    grad_shift = jnp.sum(grad_normed, axis=(0, 1, 2))
    grad_unit = grad_normed * ln_gain
    mean_one = jnp.mean(grad_unit, axis=-1, keepdims=True)
    mean_two = jnp.mean(grad_unit * unit_field, axis=-1, keepdims=True)
    grad_conv = scale_inv * (grad_unit - mean_one - unit_field * mean_two)
    grad_bias = jnp.sum(grad_conv, axis=(0, 1, 2))
    tap_sums = []
    for tap_row in range(7):
        for tap_col in range(7):
            window = padded[:, tap_row : tap_row + map_side, tap_col : tap_col + map_side, :]
            tap_sums.append(jnp.sum(window * grad_conv, axis=(0, 1, 2)))
    grad_kernel = jnp.stack(tap_sums).reshape(7, 7, unit_field.shape[-1])
    return (grad_kernel, jnp.stack([grad_bias, grad_gain, grad_shift]))


def shards(images, kernel, conv_bias, ln_gain, ln_shift, w_up, cotangent):
    full_maps = lax.all_gather(images, "row", axis=1, tiled=True)
    padded, unit_field, scale_inv, normed = conv_norm(
        full_maps, kernel, conv_bias, ln_gain, ln_shift
    )
    channels = normed.shape[-1]
    hidden_units = w_up.shape[1]
    flat = normed.reshape(-1, channels)
    weights = lax.all_gather(w_up, "fsdp", axis=0, tiled=True)
    pre_act = jnp.dot(flat, weights, preferred_element_type=jnp.float32)
    activated, pullback = jax.vjp(gelu_exact, pre_act)
    hidden = activated.astype(jnp.bfloat16)
    grad_pre = pullback(cotangent.reshape(-1, hidden_units).astype(jnp.float32))[0].astype(
        jnp.bfloat16
    )
    grad_weight = lax.psum_scatter(
        lax.dot_general(
            flat, grad_pre, (((0,), (0,)), ((), ())), preferred_element_type=jnp.float32
        ).astype(jnp.bfloat16),
        "fsdp",
        scatter_dimension=0,
        tiled=True,
    ).astype(jnp.float32)
    grad_normed = lax.dot_general(
        grad_pre, weights, (((1,), (1,)), ((), ())), preferred_element_type=jnp.float32
    )
    kernel_part, vector_part = norm_conv_grads(
        padded, unit_field, scale_inv, grad_normed.reshape(unit_field.shape), ln_gain
    )
    grad_kernel, grad_vectors = lax.psum((kernel_part, vector_part), ("dp", "row", "fsdp"))
    return (hidden.reshape(cotangent.shape), grad_weight[None], grad_kernel, grad_vectors)


def solution(mesh):
    return jax.shard_map(
        shards,
        mesh=mesh,
        in_specs=(
            P(("dp", "fsdp"), "row", None, None),
            P(),
            P(),
            P(),
            P(),
            P("fsdp", "row"),
            P(("dp", "fsdp"), None, None, "row"),
        ),
        out_specs=(P(("dp", "fsdp"), None, None, "row"), P("dp", "fsdp", "row"), P(), P()),
        check_vma=False,
    )
```

profile of v0, /device:TPU:1, one launch (start us, length us, event | category | flops | bytes accessed | tf_op | source)
XLA Modules:
  0.0 715.0 jit_solution(14709917872606870768)
XLA Ops:
  7.2 0.7 all-gather.2.cloned.1.call-update
  8.0 8.3 %all_gather.6 = bf16[1,16,16,1536]{3,2,0,1:T(8,128)(2,1)S(1)} all-gather(bf16[1,8,16,1536]{3,2,0,1:T(8,128)(2,1)} %bitcast.26), channel_id=1, replica_groups=mesh['dp'=24,'row'=2,'fsdp'=16] {'row'}, dimensions={1}, use_global_device_ids=true | all-gather | bytes 1179648 | tf_op jit(solution)/shard_map/all_gather | solution.py:52
  17.3 13.2 %fusion.16 = (f32[16,16]{1,0:T(8,128)S(1)}, f32[1,16,16,1536]{3,2,0,1:T(8,128)S(1)}) fusion(f32[1536]{0:T(1024)S(1)} %get-tuple-element.117, f32[1536]{0:T(1024)S(1)} %get-tuple-element.118, f32[1536]{0:T(1024)S(1)} %get-tuple-element.71, f32[1536]{0:T(1024)S(1)} %get-tuple-element.72, f32[1536]{0:T(1024)S(1)} %get-tuple-element.73, ...), kind=kLoop, calls=%fused_computation.188 | loop fusion | flops 38928128 | bytes 3453952 | tf_op jit(solution)/shard_map/reduce_sum | solution.py:25
  31.3 1.2 add_convert_fusion
  32.5 34.0 %all-gather.2.cloned.1.call-done = bf16[1536,1536]{1,0:T(8,128)(2,1)} async-done(((bf16[96,1536]{1,0:T(8,128)(2,1)}), bf16[1536,1536]{1,0:T(8,128)(2,1)}) %all-gather.2.cloned.1.call-update) | async-done | bytes 4718608 | tf_op jit(solution)/shard_map/all_gather | solution.py:59
  66.5 9.2 %fusion.5 = (bf16[256,1536]{1,0:T(8,128)(2,1)S(1)}, f32[256,1536]{1,0:T(8,128)}, f32[256,1536]{1,0:T(8,128)}) fusion(bf16[1,16,16,1536]{3,2,1,0:T(8,128)(2,1)} %param.13, bf16[256,1536]{1,0:T(8,128)(2,1)} %bitcast.23, bf16[1536,1536]{1,0:T(8,128)(2,1)} %all-gather.2.cloned.1.call-done), kind=kOutput, calls=%fused_computation.57 | convolution fusion | flops 1236664320 | bytes 10223616 | tf_op jit(solution)/shard_map/dot_general | solution.py:60
  75.7 0.9 copy-done.6
  76.6 3.5 convolution_convert_fusion
  80.4 5.2 fusion.14
  85.6 0.6 stack.214
  86.2 2.5 multiply_reduce_fusion
  88.8 0.6 stack.213
  89.4 4.9 multiply_reduce_fusion.1
  94.3 3.7 multiply_reduce_fusion.19
  98.0 2.5 fusion.13
  100.5 0.6 stack.212
  101.2 0.6 stack.203
  101.8 0.6 stack.202
  102.4 0.6 stack.201
  103.0 0.6 stack.200
  103.6 0.6 stack.199
  104.2 0.6 stack.198
  104.8 0.6 stack.197
  105.4 0.6 stack.196
  106.0 0.6 stack.195
  106.6 0.6 stack.194
  107.2 0.6 stack.193
  107.8 0.6 stack.186
  108.4 0.6 stack.162
  109.0 0.6 stack.163
  109.6 0.6 stack.164
  110.2 0.6 stack.165
  110.8 0.6 stack.166
  111.4 0.6 stack.167
  112.0 0.6 stack.168
  113.1 0.6 stack.170
  113.7 0.6 stack.171
  114.3 0.6 stack.172
  114.9 0.6 stack.173
  115.5 0.6 stack.191
  116.1 0.6 stack.190
  116.7 0.6 stack.189
  117.3 0.6 stack.188
  117.9 0.6 stack.187
  118.5 0.6 stack.185
  119.1 0.6 stack.184
  119.7 0.6 stack.183
  120.3 0.6 stack.182
  120.9 0.6 stack.181
  121.5 0.6 stack.180
  122.1 0.6 stack.179
  122.7 0.6 stack.178
  123.3 0.6 stack.177
  123.9 0.6 stack.176
  124.5 0.6 stack.175
  125.1 0.6 stack.174
  125.7 5.2 stack.211
  130.9 0.8 reshape.246
  131.7 0.7 pad_maximum_fusion
  132.4 111.3 %psum.15 = f32[3,1536]{1,0:T(4,128)} all-reduce(f32[3,1536]{1,0:T(4,128)S(1)} %pad_maximum_fusion), channel_id=1, replica_groups=mesh['dp'=24,'row'=2,'fsdp'=16] {'dp','row','fsdp'}, use_global_device_ids=true, to_apply=%region_58.59 | all-reduce | flops 4608 | bytes 36864 | tf_op jit(solution)/shard_map/psum | solution.py:80
  243.7 1.1 multiply_convert_fusion
  244.9 1.8 bitcast_convert_fusion
  246.8 460.0 %all-reduce.3.cloned.1.call-done = f32[7,7,1536]{2,1,0:T(8,128)} async-done(((f32[7,7,1536]{2,1,0:T(8,128)}), f32[7,7,1536]{2,1,0:T(8,128)}) %all-reduce.3.cloned.1.call-update) | async-done | bytes 301072 | tf_op jit(solution)/shard_map/psum | solution.py:80
  706.8 1.7 copy.15
  (44 shorter events, 2.8 us)
Async XLA Ops:
  7.2 59.3 %all-gather.2.cloned.1.call-start = ((), (), s32[]{:S(2)}) async-start(), calls=%async_computation.1 | async-start | bytes 5013504 | tf_op jit(solution)/shard_map/all_gather | solution.py:59
  7.9 237.0 %reduce-scatter.2.cloned.1.call-start = ((), (), s32[]{:S(2)}) async-start(), calls=%async_computation.2 | async-start | bytes 5013504 | tf_op jit(solution)/shard_map/reduce_scatter | solution.py:66
  7.9 8.5 %copy-start.7 = (f32[7,7,1536]{2,1,0:T(8,128)S(1)}, f32[7,7,1536]{2,1,0:T(8,128)}, u32[]{:S(2)}) copy-start(f32[7,7,1536]{2,1,0:T(8,128)} %param.8) | copy-start | bytes 903172
  16.2 1.0 copy-start.1
  30.5 0.7 copy-start.8
  30.5 0.7 copy-start.9
  66.5 10.1 %copy-start.3 = (bf16[1,16,16,1536]{3,2,0,1:T(8,128)(2,1)S(1)}, bf16[1,16,16,1536]{3,2,0,1:T(8,128)(2,1)}, u32[]{:S(2)}) copy-start(bf16[1,16,16,1536]{3,2,0,1:T(8,128)(2,1)} %add_convert_fusion) | copy-start | bytes 2359300
  75.7 0.9 copy-start.6
  80.1 626.6 %all-reduce.3.cloned.1.call-start = ((), (), s32[]{:S(2)}) async-start(), calls=%async_computation.3 | async-start | bytes 688128 | tf_op jit(solution)/shard_map/psum | solution.py:80
  86.2 3.2 copy-start
  94.2 3.8 copy-start.2
  98.0 145.7 %copy-start.5 = (f32[256,1536]{1,0:T(8,128)S(1)}, f32[256,1536]{1,0:T(8,128)}, u32[]{:S(2)}) copy-start(f32[256,1536]{1,0:T(8,128)} %get-tuple-element.124) | copy-start | bytes 4718596
  100.5 143.2 %copy-start.4 = (f32[256,1536]{1,0:T(8,128)S(1)}, f32[256,1536]{1,0:T(8,128)}, u32[]{:S(2)}) copy-start(f32[256,1536]{1,0:T(8,128)} %get-tuple-element.121) | copy-start | bytes 4718596
Sparse Core Ops, SparseCore 0:
  10.4 56.0 all-gather.1
  80.2 66.1 reduce-scatter.1
  245.0 461.6 all-reduce.2
where the time goes:
time: 716 us; the launch traced here: 715 us
  waiting for transfers between devices  495 us (69%)
  blocking collectives  120 us (17%)
  local copies, waits for them, and re-layouts  36.3 us (5%)
  other arithmetic  32.2 us (4%)
  matrix products  17.9 us (2%)
  between operations  14 us (2%)
    psum x1, waiting for transfers between devices, shards(): lax.psum((kernel_part, vector_part), ('dp', 'row', 'fsdp'))  460 us
    psum x1, blocking collectives, shards(): lax.psum((kernel_part, vector_part), ('dp', 'row', 'fsdp'))  111 us
    all_gather x1, waiting for transfers between devices, shards(): weights = lax.all_gather(w_up, 'fsdp', axis=0, tiled=True)  34 us
    another operation x50, local copies, waits for them, and re-layouts, norm_conv_grads(): grad_kernel = jnp.stack(tap_sums).reshape(7, 7, unit_field.shape[-1])  29.7 us
  transfers between devices with their start and end apart: 3, of which 2 were waited for; matrix products, arithmetic and copies ran while one was open for 10% of the time, Pallas kernels for 0%

commit v1 on v0

--- a/solution.py
+++ b/solution.py
@@ -48,6 +48,29 @@
     return (grad_kernel, jnp.stack([grad_bias, grad_gain, grad_shift]))
 
 
+def tree_sum(values, axis):
+    size = lax.axis_size(axis)
+    span = 1
+    while size % (2 * span) == 0:
+        partners = [(i, i ^ span) for i in range(size)]
+        values = values + lax.ppermute(values, axis, partners)
+        span *= 2
+    groups = size // span
+    if groups == 1:
+        return values
+    received = [values]
+    for shift in range(1, groups):
+        pairs = [(i, (i + shift * span) % size) for i in range(size)]
+        received.append(lax.ppermute(values, axis, pairs))
+    group = lax.axis_index(axis) // span
+    stacked = jnp.stack(received)
+    total = None
+    for source in range(groups):
+        term = stacked[(group - source) % groups]
+        total = term if total is None else total + term
+    return total
+
+
 def shards(images, kernel, conv_bias, ln_gain, ln_shift, w_up, cotangent):
     full_maps = lax.all_gather(images, "row", axis=1, tiled=True)
     padded, unit_field, scale_inv, normed = conv_norm(
@@ -77,7 +100,11 @@
     kernel_part, vector_part = norm_conv_grads(
         padded, unit_field, scale_inv, grad_normed.reshape(unit_field.shape), ln_gain
     )
-    grad_kernel, grad_vectors = lax.psum((kernel_part, vector_part), ("dp", "row", "fsdp"))
+    taps = kernel_part.shape[0] * kernel_part.shape[1]
+    packed = jnp.concatenate([kernel_part.reshape(taps, channels), vector_part], axis=0)
+    packed = tree_sum(tree_sum(tree_sum(packed, "row"), "fsdp"), "dp")
+    grad_kernel = packed[:taps].reshape(kernel_part.shape)
+    grad_vectors = packed[taps:]
     return (hidden.reshape(cotangent.shape), grad_weight[None], grad_kernel, grad_vectors)
 
 

time: 716 us -> 298 us (0.42)
  waiting for transfers between devices: 495 us -> 160 us
  blocking collectives: 120 us -> 8.27 us
  starting transfers between devices: 0.3 us -> 58.6 us
  local copies, waits for them, and re-layouts: 36.3 us -> 4.5 us
    psum x1 -> x0, waiting for transfers between devices: 460 us -> none  [shards(): lax.psum((kernel_part, vector_part), ('dp', 'row', 'fsdp'))]
    ppermute x0 -> x10, waiting for transfers between devices: none -> 125 us  [the longest x8 110 us: tree_sum(): values = values + lax.ppermute(values, axis, partners)]
    psum x1 -> x0, blocking collectives: 111 us -> none  [shards(): lax.psum((kernel_part, vector_part), ('dp', 'row', 'fsdp'))]
    ppermute x0 -> x10, starting transfers between devices: none -> 58.5 us  [the longest x8 33.1 us: tree_sum(): values = values + lax.ppermute(values, axis, partners)]
    another operation x50 -> x49, local copies, waits for them, and re-layouts: 29.7 us -> 0.31 us  [norm_conv_grads(): grad_kernel = jnp.stack(tap_sums).reshape(7, 7, unit_field.shape[-1])]
  transfers between devices with their start and end apart: 3 -> 12, of which waited for: 2 -> 11; matrix products, arithmetic and copies ran while one was open for 10% -> 13% of each run, Pallas kernels for 0% -> 0%
where the time goes in v1:
time: 298 us; the launch traced here: 297 us
  waiting for transfers between devices  160 us (54%)
  starting transfers between devices  58.6 us (20%)
  other arithmetic  33.1 us (11%)
  matrix products  17.9 us (6%)
  between operations  14.8 us (5%)
  blocking collectives  8.27 us (3%)
  local copies, waits for them, and re-layouts  4.5 us (2%)
    ppermute x8, waiting for transfers between devices, tree_sum(): values = values + lax.ppermute(values, axis, partners)  110 us
    all_gather x1, waiting for transfers between devices, shards(): weights = lax.all_gather(w_up, 'fsdp', axis=0, tiled=True)  34 us
    ppermute x8, starting transfers between devices, tree_sum(): values = values + lax.ppermute(values, axis, partners)  33.1 us
    ppermute x2, starting transfers between devices, tree_sum(): received.append(lax.ppermute(values, axis, pairs))  25.4 us
    ppermute x2, waiting for transfers between devices, tree_sum(): received.append(lax.ppermute(values, axis, pairs))  15.7 us
    reduce_sum x1, other arithmetic, conv_norm(): centre = jnp.mean(conv_out, axis=-1, keepdims=True)  13.2 us
    dot_general x1, matrix products, shards(): pre_act = jnp.dot(flat, weights, preferred_element_type=jnp.float32)  9.2 us
    reduce_sum x2, other arithmetic, norm_conv_grads(): tap_sums.append(jnp.sum(window * grad_conv, axis=(0, 1, 2)))  8.79 us
  transfers between devices with their start and end apart: 12, of which 11 were waited for; matrix products, arithmetic and copies ran while one was open for 13% of the time, Pallas kernels for 0%

profile of v1, /device:TPU:1, one launch (start us, length us, event | category | flops | bytes accessed | tf_op | source)
XLA Modules:
  0.0 297.3 jit_solution(17479679214116016969)
XLA Ops:
  7.2 0.0 all-gather.2.cloned.1.call-start
  7.2 0.7 all-gather.2.cloned.1.call-update
  7.9 0.0 reduce-scatter.2.cloned.1.call-start
  7.9 0.0 copy-start.7
  8.0 8.3 %all_gather.6 = bf16[1,16,16,1536]{3,2,0,1:T(8,128)(2,1)S(1)} all-gather(bf16[1,8,16,1536]{3,2,0,1:T(8,128)(2,1)} %bitcast.34), channel_id=1, replica_groups=mesh['dp'=24,'row'=2,'fsdp'=16] {'row'}, dimensions={1}, use_global_device_ids=true | all-gather | bytes 1179648 | tf_op jit(solution)/shard_map/all_gather | solution.py:75
  16.2 0.2 convert_element_type.24
  16.4 0.0 copy-done.7
  16.4 0.2 slice_reduce_fusion.46
  16.6 0.3 slice_reduce_fusion.48
  16.9 0.3 slice_reduce_fusion.47
  17.3 0.0 copy-done.1
  17.3 13.2 %fusion.16 = (f32[16,16]{1,0:T(8,128)S(1)}, f32[1,16,16,1536]{3,2,0,1:T(8,128)S(1)}) fusion(f32[1536]{0:T(1024)S(1)} %get-tuple-element.117, f32[1536]{0:T(1024)S(1)} %get-tuple-element.118, f32[1536]{0:T(1024)S(1)} %get-tuple-element.71, f32[1536]{0:T(1024)S(1)} %get-tuple-element.72, f32[1536]{0:T(1024)S(1)} %get-tuple-element.73, ...), kind=kLoop, calls=%fused_computation.190 | loop fusion | flops 38928128 | bytes 3453952 | tf_op jit(solution)/shard_map/reduce_sum | solution.py:25
  30.5 0.0 copy-start.8
  30.5 0.0 copy-start.9
  30.6 0.3 multiply_reduce_fusion.52
  30.9 0.4 copy-done.8
  31.2 0.0 copy-done.9
  31.3 1.2 add_convert_fusion
  32.5 34.0 %all-gather.2.cloned.1.call-done = bf16[1536,1536]{1,0:T(8,128)(2,1)} async-done(((bf16[96,1536]{1,0:T(8,128)(2,1)}), bf16[1536,1536]{1,0:T(8,128)(2,1)}) %all-gather.2.cloned.1.call-update) | async-done | bytes 4718608 | tf_op jit(solution)/shard_map/all_gather | solution.py:82
  66.5 9.2 %fusion.5 = (bf16[256,1536]{1,0:T(8,128)(2,1)S(1)}, f32[256,1536]{1,0:T(8,128)}, f32[256,1536]{1,0:T(8,128)}) fusion(bf16[1,16,16,1536]{3,2,1,0:T(8,128)(2,1)} %param.13, bf16[256,1536]{1,0:T(8,128)(2,1)} %bitcast.29, bf16[1536,1536]{1,0:T(8,128)(2,1)} %all-gather.2.cloned.1.call-done), kind=kOutput, calls=%fused_computation.57 | convolution fusion | flops 1236664320 | bytes 10223616 | tf_op jit(solution)/shard_map/dot_general | solution.py:83
  75.7 0.9 copy-done.6
  76.6 0.0 copy-done.3
  76.6 3.5 %convolution_convert_fusion = bf16[1536,1536]{1,0:T(8,128)(2,1)} fusion(bf16[256,1536]{1,0:T(8,128)(2,1)S(1)} %bitcast.30, bf16[256,1536]{1,0:T(8,128)(2,1)S(1)} %get-tuple-element.120), kind=kOutput, calls=%fused_computation.48 | convolution fusion | flops 1210318848 | bytes 6291456 | tf_op jit(solution)/shard_map/dot_general | solution.py:90
  80.1 0.0 reduce-scatter.2.cloned.1.call-update
  80.1 5.2 %fusion.13 = (f32[1536]{0:T(1024)S(1)}, f32[256]{0:T(256)S(1)}, f32[256,1536]{1,0:T(8,128)}) fusion(f32[1536]{0:T(1024)S(1)} %copy-done.8, bf16[256,1536]{1,0:T(8,128)(2,1)} %copy-done.6, bf16[1536,1536]{1,0:T(8,128)(2,1)} %all-gather.2.cloned.1.call-done), kind=kOutput, calls=%fused_computation.188 | convolution fusion | flops 1209137408 | bytes 7091200 | tf_op jit(solution)/shard_map/dot_general | solution.py:97
  85.4 0.1 div.25
  85.4 2.5 multiply_reduce_fusion
  88.0 0.0 copy-done
  88.0 4.9 %multiply_reduce_fusion.1 = (f32[1536]{0:T(1024)S(1)}, f32[1536]{0:T(1024)S(1)}, f32[1536]{0:T(1024)S(1)}, f32[1536]{0:T(1024)S(1)}, f32[1536]{0:T(1024)S(1)}, /...) fusion(f32[1,16,16,1536]{3,2,0,1:T(8,128)S(1)} %convert_element, ...), kind=kLoop, calls=%fused_computation.61 | loop fusion | flops 16880640 | bytes 6412288 | tf_op jit(solution)/shard_map/reduce_sum | solution.py:46
  92.9 0.0 copy-start.2
  92.9 3.9 %multiply_reduce_fusion.19 = (f32[1536]{0:T(1024)S(1)}, f32[1536]{0:T(1024)S(1)}, f32[1536]{0:T(1024)S(1)}, f32[1536]{0:T(1024)S(1)}, f32[1536]{0:T(1024)S(1)}, ...) fusion(f32[1,16,16,1536]{3,2,0,1:T(8,128)S(1)} %get-tuple-eleme, ...), kind=kLoop, calls=%fused_computation.79 | loop fusion | flops 14128128 | bytes 3256320 | tf_op jit(solution)/shard_map/reduce_sum | solution.py:46
  97.1 0.0 copy-done.2
  97.1 2.5 fusion.14
  100.0 0.5 concatenate.3
  100.6 3.2 %collective-permute-start = (f32[52,1536]{1,0:T(8,128)S(1)}, f32[52,1536]{1,0:T(8,128)S(1)}, u32[]{:S(2)}, u32[]{:S(2)}) collective-permute-start(f32[52,1536]{1,0:T(8,128)S(1)} %concatenate.3), channel_id=1, source_target_pairs={{0,16},{16,0},{1,17},{17,1},{2,18},{18,2},{3,19},{19,3},{4,20},{20... | collective-permute-start | bytes 958472 | tf_op jit(solution)/shard_map/ppermute | solution.py:56
  103.7 8.3 %collective-permute-done = f32[52,1536]{1,0:T(8,128)S(1)} collective-permute-done((f32[52,1536]{1,0:T(8,128)S(1)}, f32[52,1536]{1,0:T(8,128)S(1)}, u32[]{:S(2)}, u32[]{:S(2)}) %collective-permute-start) | collective-permute-done | bytes 319520 | tf_op jit(solution)/shard_map/ppermute | solution.py:56
  112.0 2.9 collective-permute-start.1
  114.9 1.3 collective-permute-done.1
  116.2 2.6 collective-permute-start.2
  118.8 11.0 %collective-permute-done.2 = f32[52,1536]{1,0:T(8,128)S(1)} collective-permute-done((f32[52,1536]{1,0:T(8,128)S(1)}, f32[52,1536]{1,0:T(8,128)S(1)}, u32[]{:S(2)}, u32[]{:S(2)}) %collective-permute-start.2) | collective-permute-done | bytes 319520 | tf_op jit(solution)/shard_map/ppermute | solution.py:56
  129.9 3.9 %collective-permute-start.3 = (f32[52,1536]{1,0:T(8,128)S(1)}, f32[52,1536]{1,0:T(8,128)S(1)}, u32[]{:S(2)}, u32[]{:S(2)}) collective-permute-start(f32[52,1536]{1,0:T(8,128)S(1)} %add.285), channel_id=1, source_target_pairs={{0,4},{1,5},{2,6},{3,7},{4,0},{5,1},{6,2},{7,3},{8,12},{9,13},{10,... | collective-permute-start | bytes 958472 | tf_op jit(solution)/shard_map/ppermute | solution.py:56
  133.7 18.8 %collective-permute-done.3 = f32[52,1536]{1,0:T(8,128)S(1)} collective-permute-done((f32[52,1536]{1,0:T(8,128)S(1)}, f32[52,1536]{1,0:T(8,128)S(1)}, u32[]{:S(2)}, u32[]{:S(2)}) %collective-permute-start.3) | collective-permute-done | bytes 319520 | tf_op jit(solution)/shard_map/ppermute | solution.py:56
  152.5 5.1 %collective-permute-start.4 = (f32[52,1536]{1,0:T(8,128)S(1)}, f32[52,1536]{1,0:T(8,128)S(1)}, u32[]{:S(2)}, u32[]{:S(2)}) collective-permute-start(f32[52,1536]{1,0:T(8,128)S(1)} %add.286), channel_id=1, source_target_pairs={{0,8},{1,9},{2,10},{3,11},{4,12},{5,13},{6,14},{7,15},{8,0},{9,1},... | collective-permute-start | bytes 958472 | tf_op jit(solution)/shard_map/ppermute | solution.py:56
  157.6 18.0 %collective-permute-done.4 = f32[52,1536]{1,0:T(8,128)S(1)} collective-permute-done((f32[52,1536]{1,0:T(8,128)S(1)}, f32[52,1536]{1,0:T(8,128)S(1)}, u32[]{:S(2)}, u32[]{:S(2)}) %collective-permute-start.4) | collective-permute-done | bytes 319520 | tf_op jit(solution)/shard_map/ppermute | solution.py:56
  175.7 0.0 copy-start.4
  175.7 0.0 copy-start.5
  175.7 3.5 %collective-permute-start.5 = (f32[52,1536]{1,0:T(8,128)S(1)}, f32[52,1536]{1,0:T(8,128)S(1)}, u32[]{:S(2)}, u32[]{:S(2)}) collective-permute-start(f32[52,1536]{1,0:T(8,128)S(1)} %add.287), channel_id=1, source_target_pairs={{0,32},{32,0},{64,96},{96,64},{128,160},{160,128},{192,224},{224,1... | collective-permute-start | bytes 958472 | tf_op jit(solution)/shard_map/ppermute | solution.py:56
  179.1 7.7 %collective-permute-done.5 = f32[52,1536]{1,0:T(8,128)S(1)} collective-permute-done((f32[52,1536]{1,0:T(8,128)S(1)}, f32[52,1536]{1,0:T(8,128)S(1)}, u32[]{:S(2)}, u32[]{:S(2)}) %collective-permute-start.5) | collective-permute-done | bytes 319520 | tf_op jit(solution)/shard_map/ppermute | solution.py:56
  186.9 4.1 %collective-permute-start.6 = (f32[52,1536]{1,0:T(8,128)S(1)}, f32[52,1536]{1,0:T(8,128)S(1)}, u32[]{:S(2)}, u32[]{:S(2)}) collective-permute-start(f32[52,1536]{1,0:T(8,128)S(1)} %add.288), channel_id=1, source_target_pairs={{0,64},{32,96},{64,0},{96,32},{128,192},{160,224},{192,128},{224,1... | collective-permute-start | bytes 958472 | tf_op jit(solution)/shard_map/ppermute | solution.py:56
  191.0 15.1 %collective-permute-done.6 = f32[52,1536]{1,0:T(8,128)S(1)} collective-permute-done((f32[52,1536]{1,0:T(8,128)S(1)}, f32[52,1536]{1,0:T(8,128)S(1)}, u32[]{:S(2)}, u32[]{:S(2)}) %collective-permute-start.6) | collective-permute-done | bytes 319520 | tf_op jit(solution)/shard_map/ppermute | solution.py:56
  206.1 8.0 %collective-permute-start.7 = (f32[52,1536]{1,0:T(8,128)S(1)}, f32[52,1536]{1,0:T(8,128)}, u32[]{:S(2)}, u32[]{:S(2)}) collective-permute-start(f32[52,1536]{1,0:T(8,128)S(1)} %add.289), channel_id=1, source_target_pairs={{0,128},{32,160},{64,192},{96,224},{128,0},{160,32},{192,64},{224,... | collective-permute-start | bytes 958472 | tf_op jit(solution)/shard_map/ppermute | solution.py:56
  214.2 29.6 %collective-permute-done.7 = f32[52,1536]{1,0:T(8,128)} collective-permute-done((f32[52,1536]{1,0:T(8,128)S(1)}, f32[52,1536]{1,0:T(8,128)}, u32[]{:S(2)}, u32[]{:S(2)}) %collective-permute-start.7) | collective-permute-done | bytes 319520 | tf_op jit(solution)/shard_map/ppermute | solution.py:56
  243.8 1.0 add.290
  244.9 23.5 %collective-permute-start.8 = (f32[52,1536]{1,0:T(8,128)S(1)}, f32[52,1536]{1,0:T(8,128)S(1)}, u32[]{:S(2)}, u32[]{:S(2)}) collective-permute-start(f32[52,1536]{1,0:T(8,128)S(1)} %add.290), channel_id=1, source_target_pairs={{0,256},{32,288},{64,320},{96,352},{128,384},{160,416},{192,448},{... | collective-permute-start | bytes 958472 | tf_op jit(solution)/shard_map/ppermute | solution.py:64
  268.3 1.9 collective-permute-start.9
  270.2 0.0 copy-done.4
  270.3 1.1 multiply_convert_fusion
  271.4 8.3 %collective-permute-done.8 = f32[52,1536]{1,0:T(8,128)S(1)} collective-permute-done((f32[52,1536]{1,0:T(8,128)S(1)}, f32[52,1536]{1,0:T(8,128)S(1)}, u32[]{:S(2)}, u32[]{:S(2)}) %collective-permute-start.8) | collective-permute-done | bytes 319520 | tf_op jit(solution)/shard_map/ppermute | solution.py:64
  279.7 7.4 %collective-permute-done.9 = f32[52,1536]{1,0:T(8,128)S(1)} collective-permute-done((f32[52,1536]{1,0:T(8,128)S(1)}, f32[52,1536]{1,0:T(8,128)S(1)}, u32[]{:S(2)}, u32[]{:S(2)}) %collective-permute-start.9) | collective-permute-done | bytes 319520 | tf_op jit(solution)/shard_map/ppermute | solution.py:64
  287.1 0.1 pad_maximum_fusion
  287.2 0.1 dynamic-slice_add_fusion
  287.3 0.8 reshape.251
  288.0 0.6 slice_bitcast_fusion
  288.7 1.8 bitcast_convert_fusion
  (69 shorter events, 0.7 us)
Async XLA Ops:
  7.2 59.3 %all-gather.2.cloned.1.call-start = ((), (), s32[]{:S(2)}) async-start(), calls=%async_computation.1 | async-start | bytes 5013504 | tf_op jit(solution)/shard_map/all_gather | solution.py:82
  7.9 280.8 %reduce-scatter.2.cloned.1.call-start = ((), (), s32[]{:S(2)}) async-start(), calls=%async_computation.2 | async-start | bytes 5013504 | tf_op jit(solution)/shard_map/reduce_scatter | solution.py:89
  7.9 8.5 %copy-start.7 = (f32[7,7,1536]{2,1,0:T(8,128)S(1)}, f32[7,7,1536]{2,1,0:T(8,128)}, u32[]{:S(2)}) copy-start(f32[7,7,1536]{2,1,0:T(8,128)} %param.8) | copy-start | bytes 903172
  16.2 1.0 copy-start.1
  30.5 0.7 copy-start.8
  30.5 0.7 copy-start.9
  66.5 10.1 %copy-start.3 = (bf16[1,16,16,1536]{3,2,0,1:T(8,128)(2,1)S(1)}, bf16[1,16,16,1536]{3,2,0,1:T(8,128)(2,1)}, u32[]{:S(2)}) copy-start(bf16[1,16,16,1536]{3,2,0,1:T(8,128)(2,1)} %add_convert_fusion) | copy-start | bytes 2359300
  75.7 0.9 copy-start.6
  85.4 2.5 copy-start
  92.9 4.2 %copy-start.2 = (bf16[1,16,16,1536]{3,2,0,1:T(8,128)(2,1)S(1)}, bf16[1,16,16,1536]{3,2,0,1:T(8,128)(2,1)}, u32[]{:S(2)}) copy-start(bf16[1,16,16,1536]{3,2,0,1:T(8,128)(2,1)} %copy-done.1) | copy-start | bytes 2359300
  100.6 11.4 %collective-permute-start = (f32[52,1536]{1,0:T(8,128)S(1)}, f32[52,1536]{1,0:T(8,128)S(1)}, u32[]{:S(2)}, u32[]{:S(2)}) collective-permute-start(f32[52,1536]{1,0:T(8,128)S(1)} %concatenate.3), channel_id=1, source_target_pairs={{0,16},{16,0},{1,17},{17,1},{2,18},{18,2},{3,19},{19,3},{4,20},{20... | collective-permute-start | bytes 958472 | tf_op jit(solution)/shard_map/ppermute | solution.py:56
  112.0 4.1 %collective-permute-start.1 = (f32[52,1536]{1,0:T(8,128)S(1)}, f32[52,1536]{1,0:T(8,128)S(1)}, u32[]{:S(2)}, u32[]{:S(2)}) collective-permute-start(f32[52,1536]{1,0:T(8,128)S(1)} %add.283), channel_id=1, source_target_pairs={{0,1},{1,0},{2,3},{3,2},{4,5},{5,4},{6,7},{7,6},{8,9},{9,8},{10,11... | collective-permute-start | bytes 958472 | tf_op jit(solution)/shard_map/ppermute | solution.py:56
  116.2 13.6 %collective-permute-start.2 = (f32[52,1536]{1,0:T(8,128)S(1)}, f32[52,1536]{1,0:T(8,128)S(1)}, u32[]{:S(2)}, u32[]{:S(2)}) collective-permute-start(f32[52,1536]{1,0:T(8,128)S(1)} %add.284), channel_id=1, source_target_pairs={{0,2},{1,3},{2,0},{3,1},{4,6},{5,7},{6,4},{7,5},{8,10},{9,11},{10,... | collective-permute-start | bytes 958472 | tf_op jit(solution)/shard_map/ppermute | solution.py:56
  129.9 22.6 %collective-permute-start.3 = (f32[52,1536]{1,0:T(8,128)S(1)}, f32[52,1536]{1,0:T(8,128)S(1)}, u32[]{:S(2)}, u32[]{:S(2)}) collective-permute-start(f32[52,1536]{1,0:T(8,128)S(1)} %add.285), channel_id=1, source_target_pairs={{0,4},{1,5},{2,6},{3,7},{4,0},{5,1},{6,2},{7,3},{8,12},{9,13},{10,... | collective-permute-start | bytes 958472 | tf_op jit(solution)/shard_map/ppermute | solution.py:56
  152.5 23.1 %collective-permute-start.4 = (f32[52,1536]{1,0:T(8,128)S(1)}, f32[52,1536]{1,0:T(8,128)S(1)}, u32[]{:S(2)}, u32[]{:S(2)}) collective-permute-start(f32[52,1536]{1,0:T(8,128)S(1)} %add.286), channel_id=1, source_target_pairs={{0,8},{1,9},{2,10},{3,11},{4,12},{5,13},{6,14},{7,15},{8,0},{9,1},... | collective-permute-start | bytes 958472 | tf_op jit(solution)/shard_map/ppermute | solution.py:56
  175.7 94.6 %copy-start.4 = (f32[256,1536]{1,0:T(8,128)S(1)}, f32[256,1536]{1,0:T(8,128)}, u32[]{:S(2)}) copy-start(f32[256,1536]{1,0:T(8,128)} %get-tuple-element.121) | copy-start | bytes 4718596
  175.7 94.6 %copy-start.5 = (f32[256,1536]{1,0:T(8,128)S(1)}, f32[256,1536]{1,0:T(8,128)}, u32[]{:S(2)}) copy-start(f32[256,1536]{1,0:T(8,128)} %get-tuple-element.124) | copy-start | bytes 4718596
  175.7 11.2 %collective-permute-start.5 = (f32[52,1536]{1,0:T(8,128)S(1)}, f32[52,1536]{1,0:T(8,128)S(1)}, u32[]{:S(2)}, u32[]{:S(2)}) collective-permute-start(f32[52,1536]{1,0:T(8,128)S(1)} %add.287), channel_id=1, source_target_pairs={{0,32},{32,0},{64,96},{96,64},{128,160},{160,128},{192,224},{224,1... | collective-permute-start | bytes 958472 | tf_op jit(solution)/shard_map/ppermute | solution.py:56
  186.9 19.1 %collective-permute-start.6 = (f32[52,1536]{1,0:T(8,128)S(1)}, f32[52,1536]{1,0:T(8,128)S(1)}, u32[]{:S(2)}, u32[]{:S(2)}) collective-permute-start(f32[52,1536]{1,0:T(8,128)S(1)} %add.288), channel_id=1, source_target_pairs={{0,64},{32,96},{64,0},{96,32},{128,192},{160,224},{192,128},{224,1... | collective-permute-start | bytes 958472 | tf_op jit(solution)/shard_map/ppermute | solution.py:56
  206.1 37.7 %collective-permute-start.7 = (f32[52,1536]{1,0:T(8,128)S(1)}, f32[52,1536]{1,0:T(8,128)}, u32[]{:S(2)}, u32[]{:S(2)}) collective-permute-start(f32[52,1536]{1,0:T(8,128)S(1)} %add.289), channel_id=1, source_target_pairs={{0,128},{32,160},{64,192},{96,224},{128,0},{160,32},{192,64},{224,... | collective-permute-start | bytes 958472 | tf_op jit(solution)/shard_map/ppermute | solution.py:56
  244.9 34.9 %collective-permute-start.8 = (f32[52,1536]{1,0:T(8,128)S(1)}, f32[52,1536]{1,0:T(8,128)S(1)}, u32[]{:S(2)}, u32[]{:S(2)}) collective-permute-start(f32[52,1536]{1,0:T(8,128)S(1)} %add.290), channel_id=1, source_target_pairs={{0,256},{32,288},{64,320},{96,352},{128,384},{160,416},{192,448},{... | collective-permute-start | bytes 958472 | tf_op jit(solution)/shard_map/ppermute | solution.py:64
  268.3 18.8 %collective-permute-start.9 = (f32[52,1536]{1,0:T(8,128)S(1)}, f32[52,1536]{1,0:T(8,128)S(1)}, u32[]{:S(2)}, u32[]{:S(2)}) collective-permute-start(f32[52,1536]{1,0:T(8,128)S(1)} %add.290), channel_id=1, source_target_pairs={{0,512},{32,544},{64,576},{96,608},{128,640},{160,672},{192,704},{... | collective-permute-start | bytes 958472 | tf_op jit(solution)/shard_map/ppermute | solution.py:64
Sparse Core Ops, SparseCore 0:
  10.4 56.0 all-gather.1
  80.3 73.9 reduce-scatter.1

commit v2 on v0

--- a/solution.py
+++ b/solution.py
@@ -48,6 +48,50 @@
     return (grad_kernel, jnp.stack([grad_bias, grad_gain, grad_shift]))
 
 
+def halving_sum(values, stages):
+    kept = []
+    for axis, span in stages:
+        size = lax.axis_size(axis)
+        bit = (lax.axis_index(axis) // span) % 2
+        half = values.shape[0] // 2
+        keep = lax.dynamic_slice_in_dim(values, bit * half, half)
+        send = lax.dynamic_slice_in_dim(values, (1 - bit) * half, half)
+        values = keep + lax.ppermute(send, axis, [(i, i ^ span) for i in range(size)])
+        kept.append((axis, span, size, bit))
+    axis, span = "dp", 1
+    while lax.axis_size(axis) % (2 * span) == 0 and ("dp", span) in stages:
+        span *= 2
+    size = lax.axis_size(axis)
+    groups = size // span
+    if groups > 1:
+        group = lax.axis_index(axis) // span
+        parts = values.reshape(groups, -1)
+        received = [parts[group]]
+        for shift in range(1, groups):
+            pairs = [(i, (i + shift * span) % size) for i in range(size)]
+            received.append(lax.ppermute(parts[(group + shift) % groups], axis, pairs))
+        stacked = jnp.stack(received)
+        total = None
+        for source in range(groups):
+            term = stacked[(group - source) % groups]
+            total = term if total is None else total + term
+        received = [total]
+        for shift in range(1, groups):
+            pairs = [(i, (i + shift * span) % size) for i in range(size)]
+            received.append(lax.ppermute(total, axis, pairs))
+        stacked = jnp.stack(received)
+        values = jnp.concatenate([stacked[(group - source) % groups] for source in range(groups)])
+    for axis, span, size, bit in reversed(kept):
+        other = lax.ppermute(values, axis, [(i, i ^ span) for i in range(size)])
+        values = jnp.where(bit == 0, jnp.concatenate([values, other]), jnp.concatenate([other, values]))
+    return values
+
+
+HALVING_STAGES = (
+    ("fsdp", 1), ("row", 1), ("fsdp", 2), ("dp", 1), ("fsdp", 4), ("dp", 2), ("fsdp", 8), ("dp", 4),
+)
+
+
 def shards(images, kernel, conv_bias, ln_gain, ln_shift, w_up, cotangent):
     full_maps = lax.all_gather(images, "row", axis=1, tiled=True)
     padded, unit_field, scale_inv, normed = conv_norm(
@@ -77,7 +121,11 @@
     kernel_part, vector_part = norm_conv_grads(
         padded, unit_field, scale_inv, grad_normed.reshape(unit_field.shape), ln_gain
     )
-    grad_kernel, grad_vectors = lax.psum((kernel_part, vector_part), ("dp", "row", "fsdp"))
+    taps = kernel_part.shape[0] * kernel_part.shape[1]
+    packed = jnp.concatenate([kernel_part.reshape(taps, channels), vector_part], axis=0)
+    packed = halving_sum(packed.reshape(-1), HALVING_STAGES).reshape(packed.shape)
+    grad_kernel = packed[:taps].reshape(kernel_part.shape)
+    grad_vectors = packed[taps:]
     return (hidden.reshape(cotangent.shape), grad_weight[None], grad_kernel, grad_vectors)
 
 

time: 716 us -> 258 us (0.36)
  waiting for transfers between devices: 495 us -> 77.4 us
  blocking collectives: 120 us -> 8.27 us
  starting transfers between devices: 0.3 us -> 96.9 us
  local copies, waits for them, and re-layouts: 36.3 us -> 7.3 us
    psum x1 -> x0, waiting for transfers between devices: 460 us -> none  [shards(): lax.psum((kernel_part, vector_part), ('dp', 'row', 'fsdp'))]
    psum x1 -> x0, blocking collectives: 111 us -> none  [shards(): lax.psum((kernel_part, vector_part), ('dp', 'row', 'fsdp'))]
    ppermute x0 -> x20, starting transfers between devices: none -> 96.8 us  [the longest x8 42.4 us: halving_sum(): other = lax.ppermute(values, axis, [(i, i ^ span) for i in range(size)])]
    ppermute x0 -> x20, waiting for transfers between devices: none -> 43.6 us  [the longest x8 18.2 us: halving_sum(): other = lax.ppermute(values, axis, [(i, i ^ span) for i in range(size)])]
    another operation x50 -> x49, local copies, waits for them, and re-layouts: 29.7 us -> 0.31 us  [norm_conv_grads(): grad_kernel = jnp.stack(tap_sums).reshape(7, 7, unit_field.shape[-1])]
  transfers between devices with their start and end apart: 3 -> 22, of which waited for: 2 -> 19; matrix products, arithmetic and copies ran while one was open for 10% -> 14% of each run, Pallas kernels for 0% -> 0%
where the time goes in v2:
time: 258 us; the launch traced here: 257 us
  starting transfers between devices  96.9 us (38%)
  waiting for transfers between devices  77.4 us (30%)
  other arithmetic  33.3 us (13%)
  matrix products  18.2 us (7%)
  between operations  15.4 us (6%)
  blocking collectives  8.27 us (3%)
  local copies, waits for them, and re-layouts  7.3 us (3%)
    ppermute x8, starting transfers between devices, halving_sum(): other = lax.ppermute(values, axis, [(i, i ^ span) for i in range(size)])  42.4 us
    all_gather x1, waiting for transfers between devices, shards(): weights = lax.all_gather(w_up, 'fsdp', axis=0, tiled=True)  33.1 us
    ppermute x8, starting transfers between devices, halving_sum(): lax.ppermute(send, axis, [(i, i ^ span) for i in range(size)])  30.5 us
    ppermute x8, waiting for transfers between devices, halving_sum(): other = lax.ppermute(values, axis, [(i, i ^ span) for i in range(size)])  18.2 us
    ppermute x8, waiting for transfers between devices, halving_sum(): lax.ppermute(send, axis, [(i, i ^ span) for i in range(size)])  16.2 us
    reduce_sum x1, other arithmetic, conv_norm(): centre = jnp.mean(conv_out, axis=-1, keepdims=True)  13.2 us
    ppermute x2, starting transfers between devices, halving_sum(): received.append(lax.ppermute(parts[(group + shift) % groups], axis, pairs))  12.4 us
    ppermute x2, starting transfers between devices, halving_sum(): received.append(lax.ppermute(total, axis, pairs))  11.6 us
  transfers between devices with their start and end apart: 22, of which 19 were waited for; matrix products, arithmetic and copies ran while one was open for 14% of the time, Pallas kernels for 0%

profile of v2, /device:TPU:1, one launch (start us, length us, event | category | flops | bytes accessed | tf_op | source)
XLA Modules:
  0.0 256.9 jit_solution(16190937541670780108)
XLA Ops:
  7.2 0.7 all-gather.2.cloned.1.call-update
  8.0 8.3 %all_gather.6 = bf16[1,16,16,1536]{3,2,0,1:T(8,128)(2,1)S(1)} all-gather(bf16[1,8,16,1536]{3,2,0,1:T(8,128)(2,1)} %bitcast.42), channel_id=1, replica_groups=mesh['dp'=24,'row'=2,'fsdp'=16] {'row'}, dimensions={1}, use_global_device_ids=true | all-gather | bytes 1179648 | tf_op jit(solution)/shard_map/all_gather | solution.py:96
  16.2 0.9 copy-done.1
  17.6 0.3 slice_reduce_fusion.48
  17.9 0.3 slice_reduce_fusion.47
  18.2 13.2 %fusion.25 = (f32[16,16]{1,0:T(8,128)S(1)}, f32[1,16,16,1536]{3,2,0,1:T(8,128)S(1)}) fusion(f32[1536]{0:T(1024)S(1)} %get-tuple-element.117, f32[1536]{0:T(1024)S(1)} %get-tuple-element.118, f32[1536]{0:T(1024)S(1)} %get-tuple-element.71, f32[1536]{0:T(1024)S(1)} %get-tuple-element.72, f32[1536]{0:T(1024)S(1)} %get-tuple-element.73, ...), kind=kLoop, calls=%fused_computation.228 | loop fusion | flops 38928128 | bytes 3453952 | tf_op jit(solution)/shard_map/reduce_sum | solution.py:25
  31.5 0.3 multiply_reduce_fusion.52
  31.8 0.4 copy-done.7
  32.2 1.2 add_convert_fusion
  33.4 33.1 %all-gather.2.cloned.1.call-done = bf16[1536,1536]{1,0:T(8,128)(2,1)} async-done(((bf16[96,1536]{1,0:T(8,128)(2,1)}), bf16[1536,1536]{1,0:T(8,128)(2,1)}) %all-gather.2.cloned.1.call-update) | async-done | bytes 4718608 | tf_op jit(solution)/shard_map/all_gather | solution.py:103
  66.5 9.5 %fusion.5 = (bf16[256,1536]{1,0:T(8,128)(2,1)}, f32[256,1536]{1,0:T(8,128)}, f32[256,1536]{1,0:T(8,128)}) fusion(bf16[1,16,16,1536]{3,2,1,0:T(8,128)(2,1)} %param.13, bf16[256,1536]{1,0:T(8,128)(2,1)} %bitcast.39, bf16[1536,1536]{1,0:T(8,128)(2,1)} %all-gather.2.cloned.1.call-done), kind=kOutput, calls=%fused_computation.57 | convolution fusion | flops 1236664320 | bytes 10223616 | tf_op jit(solution)/shard_map/dot_general | solution.py:104
  76.0 4.7 %convolution_convert_fusion = bf16[1536,1536]{1,0:T(8,128)(2,1)} fusion(bf16[256,1536]{1,0:T(8,128)(2,1)S(1)} %bitcast.40, bf16[256,1536]{1,0:T(8,128)(2,1)} %get-tuple-element.120), kind=kOutput, calls=%fused_computation.48 | convolution fusion | flops 1210318848 | bytes 6291456 | tf_op jit(solution)/shard_map/dot_general | solution.py:111
  80.7 4.1 %fusion.22 = (f32[1536]{0:T(1024)S(1)}, f32[256]{0:T(256)S(1)}, f32[256,1536]{1,0:T(8,128)S(1)}) fusion(f32[1536]{0:T(1024)S(1)} %copy-done.7, bf16[256,1536]{1,0:T(8,128)(2,1)} %get-tuple-element.120, bf16[1536,1536]{1,0:T(8,128)(2,1)} %all-gather.2.cloned.1.call-done), kind=kOutput, calls=%fused_computation.226 | convolution fusion | flops 1209137408 | bytes 7091200 | tf_op jit(solution)/shard_map/dot_general | solution.py:118
  84.8 0.5 multiply_reduce_fusion
  85.3 0.7 copy-done
  86.1 5.9 %multiply_reduce_fusion.1 = (f32[1536]{0:T(1024)S(1)}, f32[1536]{0:T(1024)S(1)}, f32[1536]{0:T(1024)S(1)}, f32[1536]{0:T(1024)S(1)}, f32[1536]{0:T(1024)S(1)}, /...) fusion(f32[1,16,16,1536]{3,2,0,1:T(8,128)S(1)} %convert_element, ...), kind=kLoop, calls=%fused_computation.61 | loop fusion | flops 16880640 | bytes 6412288 | tf_op jit(solution)/shard_map/reduce_sum | solution.py:46
  92.0 3.9 %multiply_reduce_fusion.19 = (f32[1536]{0:T(1024)S(1)}, f32[1536]{0:T(1024)S(1)}, f32[1536]{0:T(1024)S(1)}, f32[1536]{0:T(1024)S(1)}, f32[1536]{0:T(1024)S(1)}, ...) fusion(f32[1,16,16,1536]{3,2,0,1:T(8,128)S(1)} %get-tuple-eleme, ...), kind=kLoop, calls=%fused_computation.79 | loop fusion | flops 14128128 | bytes 3256320 | tf_op jit(solution)/shard_map/reduce_sum | solution.py:46
  96.2 2.5 fusion.23
  99.1 0.5 concatenate.72
  99.7 0.7 reshape.271
  100.4 1.2 dynamic_slice.76
  101.7 2.1 collective-permute-start
  103.9 1.1 collective-permute-done
  105.0 0.9 dynamic-slice_add_fusion
  106.0 3.1 %collective-permute-start.1 = (f32[19968]{0:T(1024)S(1)}, f32[19968]{0:T(1024)S(1)}, u32[]{:S(2)}, u32[]{:S(2)}) collective-permute-start(f32[19968]{0:T(1024)S(1)} %dynamic_slice.78), channel_id=1, source_target_pairs={{0,16},{16,0},{1,17},{17,1},{2,18},{18,2},{3,19},{19,3},{4,20},{20... | collective-permute-start | bytes 239624 | tf_op jit(solution)/shard_map/ppermute | solution.py:59
  109.1 2.7 %collective-permute-done.1 = f32[19968]{0:T(1024)S(1)} collective-permute-done((f32[19968]{0:T(1024)S(1)}, f32[19968]{0:T(1024)S(1)}, u32[]{:S(2)}, u32[]{:S(2)}) %collective-permute-start.1) | collective-permute-done | bytes 79904 | tf_op jit(solution)/shard_map/ppermute | solution.py:59
  112.0 2.3 collective-permute-start.2
  114.4 2.7 %collective-permute-done.2 = f32[9984]{0:T(1024)S(1)} collective-permute-done((f32[9984]{0:T(1024)S(1)}, f32[9984]{0:T(1024)S(1)}, u32[]{:S(2)}, u32[]{:S(2)}) %collective-permute-start.2) | collective-permute-done | bytes 39968 | tf_op jit(solution)/shard_map/ppermute | solution.py:59
  117.2 3.3 %collective-permute-start.3 = (f32[4992]{0:T(1024)S(1)}, f32[4992]{0:T(1024)S(1)}, u32[]{:S(2)}, u32[]{:S(2)}) collective-permute-start(f32[4992]{0:T(1024)S(1)} %dynamic_slice.82), channel_id=1, source_target_pairs={{0,32},{32,0},{64,96},{96,64},{128,160},{160,128},{192,224},{224,1... | collective-permute-start | bytes 59912 | tf_op jit(solution)/shard_map/ppermute | solution.py:59
  120.6 1.6 collective-permute-done.3
  122.3 2.7 %collective-permute-start.4 = (f32[2496]{0:T(1024)S(1)}, f32[2496]{0:T(1024)S(1)}, u32[]{:S(2)}, u32[]{:S(2)}) collective-permute-start(f32[2496]{0:T(1024)S(1)} %dynamic_slice.84), channel_id=1, source_target_pairs={{0,4},{1,5},{2,6},{3,7},{4,0},{5,1},{6,2},{7,3},{8,12},{9,13},{10,... | collective-permute-start | bytes 29960 | tf_op jit(solution)/shard_map/ppermute | solution.py:59
  125.0 2.7 %collective-permute-done.4 = f32[2496]{0:T(1024)S(1)} collective-permute-done((f32[2496]{0:T(1024)S(1)}, f32[2496]{0:T(1024)S(1)}, u32[]{:S(2)}, u32[]{:S(2)}) %collective-permute-start.4) | collective-permute-done | bytes 10016 | tf_op jit(solution)/shard_map/ppermute | solution.py:59
  127.9 4.4 %collective-permute-start.5 = (f32[1248]{0:T(1024)S(1)}, f32[1248]{0:T(1024)S(1)}, u32[]{:S(2)}, u32[]{:S(2)}) collective-permute-start(f32[1248]{0:T(1024)S(1)} %dynamic_slice.86), channel_id=1, source_target_pairs={{0,64},{32,96},{64,0},{96,32},{128,192},{160,224},{192,128},{224,1... | collective-permute-start | bytes 14984 | tf_op jit(solution)/shard_map/ppermute | solution.py:59
  132.4 1.0 collective-permute-done.5
  133.5 4.5 %collective-permute-start.6 = (f32[624]{0:T(1024)S(1)}, f32[624]{0:T(1024)S(1)}, u32[]{:S(2)}, u32[]{:S(2)}) collective-permute-start(f32[624]{0:T(1024)S(1)} %dynamic_slice.88), channel_id=1, source_target_pairs={{0,8},{1,9},{2,10},{3,11},{4,12},{5,13},{6,14},{7,15},{8,0},{9,1},... | collective-permute-start | bytes 7496 | tf_op jit(solution)/shard_map/ppermute | solution.py:59
  138.1 3.7 %collective-permute-done.6 = f32[624]{0:T(1024)S(1)} collective-permute-done((f32[624]{0:T(1024)S(1)}, f32[624]{0:T(1024)S(1)}, u32[]{:S(2)}, u32[]{:S(2)}) %collective-permute-start.6) | collective-permute-done | bytes 2528 | tf_op jit(solution)/shard_map/ppermute | solution.py:59
  141.9 8.0 %collective-permute-start.7 = (f32[312]{0:T(512)S(1)}, f32[312]{0:T(512)S(1)}, u32[]{:S(2)}, u32[]{:S(2)}) collective-permute-start(f32[312]{0:T(512)S(1)} %dynamic_slice.90), channel_id=1, source_target_pairs={{0,128},{32,160},{64,192},{96,224},{128,0},{160,32},{192,64},{224,... | collective-permute-start | bytes 3752 | tf_op jit(solution)/shard_map/ppermute | solution.py:59
  150.0 0.9 collective-permute-done.7
  151.1 10.4 %collective-permute-start.8 = (f32[104]{0:T(128)S(1)}, f32[104]{0:T(128)S(1)}, u32[]{:S(2)}, u32[]{:S(2)}) collective-permute-start(f32[104]{0:T(128)S(1)} %get-tuple-element.129), channel_id=1, source_target_pairs={{0,256},{32,288},{64,320},{96,352},{128,384},{160,416},{192,448},{... | collective-permute-start | bytes 1256 | tf_op jit(solution)/shard_map/ppermute | solution.py:72
  161.6 1.9 collective-permute-start.9
  163.5 6.2 %collective-permute-done.9 = f32[104]{0:T(128)S(1)} collective-permute-done((f32[104]{0:T(128)S(1)}, f32[104]{0:T(128)S(1)}, u32[]{:S(2)}, u32[]{:S(2)}) %collective-permute-start.9) | collective-permute-done | bytes 448 | tf_op jit(solution)/shard_map/ppermute | solution.py:72
  169.8 6.3 %collective-permute-start.10 = (f32[104]{0:T(128)S(1)}, f32[104]{0:T(128)S(1)}, u32[]{:S(2)}, u32[]{:S(2)}) collective-permute-start(f32[104]{0:T(128)S(1)} %fusion.32), channel_id=1, source_target_pairs={{0,256},{32,288},{64,320},{96,352},{128,384},{160,416},{192,448},{... | collective-permute-start | bytes 1256 | tf_op jit(solution)/shard_map/ppermute | solution.py:81
  176.1 5.3 %collective-permute-start.11 = (f32[104]{0:T(128)S(1)}, f32[104]{0:T(128)S(1)}, u32[]{:S(2)}, u32[]{:S(2)}) collective-permute-start(f32[104]{0:T(128)S(1)} %fusion.32), channel_id=1, source_target_pairs={{0,512},{32,544},{64,576},{96,608},{128,640},{160,672},{192,704},{... | collective-permute-start | bytes 1256 | tf_op jit(solution)/shard_map/ppermute | solution.py:81
  181.4 2.9 %collective-permute-done.11 = f32[104]{0:T(128)S(1)} collective-permute-done((f32[104]{0:T(128)S(1)}, f32[104]{0:T(128)S(1)}, u32[]{:S(2)}, u32[]{:S(2)}) %collective-permute-start.11) | collective-permute-done | bytes 448 | tf_op jit(solution)/shard_map/ppermute | solution.py:81
  184.4 5.2 %collective-permute-start.12 = (f32[312]{0:T(512)S(1)}, f32[312]{0:T(512)S(1)}, u32[]{:S(2)}, u32[]{:S(2)}) collective-permute-start(f32[312]{0:T(512)S(1)} %pad_maximum_fusion.6), channel_id=1, source_target_pairs={{0,128},{32,160},{64,192},{96,224},{128,0},{160,32},{192,64},{224,... | collective-permute-start | bytes 3752 | tf_op jit(solution)/shard_map/ppermute | solution.py:85
  189.7 3.0 %collective-permute-done.12 = f32[312]{0:T(512)S(1)} collective-permute-done((f32[312]{0:T(512)S(1)}, f32[312]{0:T(512)S(1)}, u32[]{:S(2)}, u32[]{:S(2)}) %collective-permute-start.12) | collective-permute-done | bytes 1280 | tf_op jit(solution)/shard_map/ppermute | solution.py:85
  192.7 4.3 %collective-permute-start.13 = (f32[624]{0:T(1024)S(1)}, f32[624]{0:T(1024)S(1)}, u32[]{:S(2)}, u32[]{:S(2)}) collective-permute-start(f32[624]{0:T(1024)S(1)} %maximum_select_fusion.7), channel_id=1, source_target_pairs={{0,8},{1,9},{2,10},{3,11},{4,12},{5,13},{6,14},{7,15},{8,0},{9,1},... | collective-permute-start | bytes 7496 | tf_op jit(solution)/shard_map/ppermute | solution.py:85
  197.0 3.9 %collective-permute-done.13 = f32[624]{0:T(1024)S(1)} collective-permute-done((f32[624]{0:T(1024)S(1)}, f32[624]{0:T(1024)S(1)}, u32[]{:S(2)}, u32[]{:S(2)}) %collective-permute-start.13) | collective-permute-done | bytes 2528 | tf_op jit(solution)/shard_map/ppermute | solution.py:85
  201.1 4.3 %collective-permute-start.14 = (f32[1248]{0:T(1024)S(1)}, f32[1248]{0:T(1024)S(1)}, u32[]{:S(2)}, u32[]{:S(2)}) collective-permute-start(f32[1248]{0:T(1024)S(1)} %maximum_select_fusion.6), channel_id=1, source_target_pairs={{0,64},{32,96},{64,0},{96,32},{128,192},{160,224},{192,128},{224,1... | collective-permute-start | bytes 14984 | tf_op jit(solution)/shard_map/ppermute | solution.py:85
  205.4 1.0 collective-permute-done.14
  206.5 2.3 collective-permute-start.15
  208.8 3.4 %collective-permute-done.15 = f32[2496]{0:T(1024)S(1)} collective-permute-done((f32[2496]{0:T(1024)S(1)}, f32[2496]{0:T(1024)S(1)}, u32[]{:S(2)}, u32[]{:S(2)}) %collective-permute-start.15) | collective-permute-done | bytes 10016 | tf_op jit(solution)/shard_map/ppermute | solution.py:85
  212.3 3.2 %collective-permute-start.16 = (f32[4992]{0:T(1024)S(1)}, f32[4992]{0:T(1024)S(1)}, u32[]{:S(2)}, u32[]{:S(2)}) collective-permute-start(f32[4992]{0:T(1024)S(1)} %maximum_select_fusion.4), channel_id=1, source_target_pairs={{0,32},{32,0},{64,96},{96,64},{128,160},{160,128},{192,224},{224,1... | collective-permute-start | bytes 59912 | tf_op jit(solution)/shard_map/ppermute | solution.py:85
  215.5 1.3 collective-permute-done.16
  216.8 2.1 collective-permute-start.17
  218.9 2.7 %collective-permute-done.17 = f32[9984]{0:T(1024)S(1)} collective-permute-done((f32[9984]{0:T(1024)S(1)}, f32[9984]{0:T(1024)S(1)}, u32[]{:S(2)}, u32[]{:S(2)}) %collective-permute-start.17) | collective-permute-done | bytes 39968 | tf_op jit(solution)/shard_map/ppermute | solution.py:85
  221.6 2.1 collective-permute-start.18
  223.7 1.1 multiply_convert_fusion
  224.9 1.9 collective-permute-done.18
  226.8 18.9 %collective-permute-start.19 = (f32[39936]{0:T(1024)S(1)}, f32[39936]{0:T(1024)S(1)}, u32[]{:S(2)}, u32[]{:S(2)}) collective-permute-start(f32[39936]{0:T(1024)S(1)} %maximum_select_fusion.1), channel_id=1, source_target_pairs={{0,1},{1,0},{2,3},{3,2},{4,5},{5,4},{6,7},{7,6},{8,9},{9,8},{10,11... | collective-permute-start | bytes 479240 | tf_op jit(solution)/shard_map/ppermute | solution.py:85
  245.8 0.9 collective-permute-done.19
  246.8 0.8 reshape.273
  247.6 0.6 fusion.14
  248.2 1.8 bitcast_convert_fusion
  (114 shorter events, 2.8 us)
Async XLA Ops:
  7.2 59.4 %all-gather.2.cloned.1.call-start = ((), (), s32[]{:S(2)}) async-start(), calls=%async_computation.1 | async-start | bytes 5013504 | tf_op jit(solution)/shard_map/all_gather | solution.py:103
  7.9 240.3 %reduce-scatter.2.cloned.1.call-start = ((), (), s32[]{:S(2)}) async-start(), calls=%async_computation.2 | async-start | bytes 5013504 | tf_op jit(solution)/shard_map/reduce_scatter | solution.py:110
  8.0 9.4 %copy-start.6 = (f32[7,7,1536]{2,1,0:T(8,128)S(1)}, f32[7,7,1536]{2,1,0:T(8,128)}, u32[]{:S(2)}) copy-start(f32[7,7,1536]{2,1,0:T(8,128)} %param.8) | copy-start | bytes 903172
  16.2 0.9 copy-start.1
  31.4 0.7 copy-start.7
  31.5 0.7 copy-start.8
  66.5 9.5 %copy-start.3 = (bf16[1,16,16,1536]{3,2,0,1:T(8,128)(2,1)S(1)}, bf16[1,16,16,1536]{3,2,0,1:T(8,128)(2,1)}, u32[]{:S(2)}) copy-start(bf16[1,16,16,1536]{3,2,0,1:T(8,128)(2,1)} %add_convert_fusion) | copy-start | bytes 2359300
  84.8 1.2 copy-start
  92.0 4.2 %copy-start.2 = (bf16[1,16,16,1536]{3,2,0,1:T(8,128)(2,1)S(1)}, bf16[1,16,16,1536]{3,2,0,1:T(8,128)(2,1)}, u32[]{:S(2)}) copy-start(bf16[1,16,16,1536]{3,2,0,1:T(8,128)(2,1)} %copy-done.1) | copy-start | bytes 2359300
  99.7 124.0 %copy-start.4 = (f32[256,1536]{1,0:T(8,128)S(1)}, f32[256,1536]{1,0:T(8,128)}, u32[]{:S(2)}) copy-start(f32[256,1536]{1,0:T(8,128)} %get-tuple-element.121) | copy-start | bytes 4718596
  99.7 124.0 %copy-start.5 = (f32[256,1536]{1,0:T(8,128)S(1)}, f32[256,1536]{1,0:T(8,128)}, u32[]{:S(2)}) copy-start(f32[256,1536]{1,0:T(8,128)} %get-tuple-element.130) | copy-start | bytes 4718596
  101.7 3.3 %collective-permute-start = (f32[39936]{0:T(1024)S(1)}, f32[39936]{0:T(1024)S(1)}, u32[]{:S(2)}, u32[]{:S(2)}) collective-permute-start(f32[39936]{0:T(1024)S(1)} %dynamic_slice.76), channel_id=1, source_target_pairs={{0,1},{1,0},{2,3},{3,2},{4,5},{5,4},{6,7},{7,6},{8,9},{9,8},{10,11... | collective-permute-start | bytes 479240 | tf_op jit(solution)/shard_map/ppermute | solution.py:59
  106.0 5.8 %collective-permute-start.1 = (f32[19968]{0:T(1024)S(1)}, f32[19968]{0:T(1024)S(1)}, u32[]{:S(2)}, u32[]{:S(2)}) collective-permute-start(f32[19968]{0:T(1024)S(1)} %dynamic_slice.78), channel_id=1, source_target_pairs={{0,16},{16,0},{1,17},{17,1},{2,18},{18,2},{3,19},{19,3},{4,20},{20... | collective-permute-start | bytes 239624 | tf_op jit(solution)/shard_map/ppermute | solution.py:59
  112.0 5.1 %collective-permute-start.2 = (f32[9984]{0:T(1024)S(1)}, f32[9984]{0:T(1024)S(1)}, u32[]{:S(2)}, u32[]{:S(2)}) collective-permute-start(f32[9984]{0:T(1024)S(1)} %dynamic_slice.80), channel_id=1, source_target_pairs={{0,2},{1,3},{2,0},{3,1},{4,6},{5,7},{6,4},{7,5},{8,10},{9,11},{10,... | collective-permute-start | bytes 119816 | tf_op jit(solution)/shard_map/ppermute | solution.py:59
  117.2 4.9 %collective-permute-start.3 = (f32[4992]{0:T(1024)S(1)}, f32[4992]{0:T(1024)S(1)}, u32[]{:S(2)}, u32[]{:S(2)}) collective-permute-start(f32[4992]{0:T(1024)S(1)} %dynamic_slice.82), channel_id=1, source_target_pairs={{0,32},{32,0},{64,96},{96,64},{128,160},{160,128},{192,224},{224,1... | collective-permute-start | bytes 59912 | tf_op jit(solution)/shard_map/ppermute | solution.py:59
  122.3 5.4 %collective-permute-start.4 = (f32[2496]{0:T(1024)S(1)}, f32[2496]{0:T(1024)S(1)}, u32[]{:S(2)}, u32[]{:S(2)}) collective-permute-start(f32[2496]{0:T(1024)S(1)} %dynamic_slice.84), channel_id=1, source_target_pairs={{0,4},{1,5},{2,6},{3,7},{4,0},{5,1},{6,2},{7,3},{8,12},{9,13},{10,... | collective-permute-start | bytes 29960 | tf_op jit(solution)/shard_map/ppermute | solution.py:59
  127.9 5.4 %collective-permute-start.5 = (f32[1248]{0:T(1024)S(1)}, f32[1248]{0:T(1024)S(1)}, u32[]{:S(2)}, u32[]{:S(2)}) collective-permute-start(f32[1248]{0:T(1024)S(1)} %dynamic_slice.86), channel_id=1, source_target_pairs={{0,64},{32,96},{64,0},{96,32},{128,192},{160,224},{192,128},{224,1... | collective-permute-start | bytes 14984 | tf_op jit(solution)/shard_map/ppermute | solution.py:59
  133.5 8.3 %collective-permute-start.6 = (f32[624]{0:T(1024)S(1)}, f32[624]{0:T(1024)S(1)}, u32[]{:S(2)}, u32[]{:S(2)}) collective-permute-start(f32[624]{0:T(1024)S(1)} %dynamic_slice.88), channel_id=1, source_target_pairs={{0,8},{1,9},{2,10},{3,11},{4,12},{5,13},{6,14},{7,15},{8,0},{9,1},... | collective-permute-start | bytes 7496 | tf_op jit(solution)/shard_map/ppermute | solution.py:59
  141.9 9.0 %collective-permute-start.7 = (f32[312]{0:T(512)S(1)}, f32[312]{0:T(512)S(1)}, u32[]{:S(2)}, u32[]{:S(2)}) collective-permute-start(f32[312]{0:T(512)S(1)} %dynamic_slice.90), channel_id=1, source_target_pairs={{0,128},{32,160},{64,192},{96,224},{128,0},{160,32},{192,64},{224,... | collective-permute-start | bytes 3752 | tf_op jit(solution)/shard_map/ppermute | solution.py:59
  151.1 12.4 %collective-permute-start.8 = (f32[104]{0:T(128)S(1)}, f32[104]{0:T(128)S(1)}, u32[]{:S(2)}, u32[]{:S(2)}) collective-permute-start(f32[104]{0:T(128)S(1)} %get-tuple-element.129), channel_id=1, source_target_pairs={{0,256},{32,288},{64,320},{96,352},{128,384},{160,416},{192,448},{... | collective-permute-start | bytes 1256 | tf_op jit(solution)/shard_map/ppermute | solution.py:72
  161.6 8.2 %collective-permute-start.9 = (f32[104]{0:T(128)S(1)}, f32[104]{0:T(128)S(1)}, u32[]{:S(2)}, u32[]{:S(2)}) collective-permute-start(f32[104]{0:T(128)S(1)} %get-tuple-element.128), channel_id=1, source_target_pairs={{0,512},{32,544},{64,576},{96,608},{128,640},{160,672},{192,704},{... | collective-permute-start | bytes 1256 | tf_op jit(solution)/shard_map/ppermute | solution.py:72
  169.8 11.6 %collective-permute-start.10 = (f32[104]{0:T(128)S(1)}, f32[104]{0:T(128)S(1)}, u32[]{:S(2)}, u32[]{:S(2)}) collective-permute-start(f32[104]{0:T(128)S(1)} %fusion.32), channel_id=1, source_target_pairs={{0,256},{32,288},{64,320},{96,352},{128,384},{160,416},{192,448},{... | collective-permute-start | bytes 1256 | tf_op jit(solution)/shard_map/ppermute | solution.py:81
  176.1 8.2 %collective-permute-start.11 = (f32[104]{0:T(128)S(1)}, f32[104]{0:T(128)S(1)}, u32[]{:S(2)}, u32[]{:S(2)}) collective-permute-start(f32[104]{0:T(128)S(1)} %fusion.32), channel_id=1, source_target_pairs={{0,512},{32,544},{64,576},{96,608},{128,640},{160,672},{192,704},{... | collective-permute-start | bytes 1256 | tf_op jit(solution)/shard_map/ppermute | solution.py:81
  184.4 8.2 %collective-permute-start.12 = (f32[312]{0:T(512)S(1)}, f32[312]{0:T(512)S(1)}, u32[]{:S(2)}, u32[]{:S(2)}) collective-permute-start(f32[312]{0:T(512)S(1)} %pad_maximum_fusion.6), channel_id=1, source_target_pairs={{0,128},{32,160},{64,192},{96,224},{128,0},{160,32},{192,64},{224,... | collective-permute-start | bytes 3752 | tf_op jit(solution)/shard_map/ppermute | solution.py:85
  192.7 8.2 %collective-permute-start.13 = (f32[624]{0:T(1024)S(1)}, f32[624]{0:T(1024)S(1)}, u32[]{:S(2)}, u32[]{:S(2)}) collective-permute-start(f32[624]{0:T(1024)S(1)} %maximum_select_fusion.7), channel_id=1, source_target_pairs={{0,8},{1,9},{2,10},{3,11},{4,12},{5,13},{6,14},{7,15},{8,0},{9,1},... | collective-permute-start | bytes 7496 | tf_op jit(solution)/shard_map/ppermute | solution.py:85
  201.1 5.3 %collective-permute-start.14 = (f32[1248]{0:T(1024)S(1)}, f32[1248]{0:T(1024)S(1)}, u32[]{:S(2)}, u32[]{:S(2)}) collective-permute-start(f32[1248]{0:T(1024)S(1)} %maximum_select_fusion.6), channel_id=1, source_target_pairs={{0,64},{32,96},{64,0},{96,32},{128,192},{160,224},{192,128},{224,1... | collective-permute-start | bytes 14984 | tf_op jit(solution)/shard_map/ppermute | solution.py:85
  206.5 5.8 %collective-permute-start.15 = (f32[2496]{0:T(1024)S(1)}, f32[2496]{0:T(1024)S(1)}, u32[]{:S(2)}, u32[]{:S(2)}) collective-permute-start(f32[2496]{0:T(1024)S(1)} %maximum_select_fusion.5), channel_id=1, source_target_pairs={{0,4},{1,5},{2,6},{3,7},{4,0},{5,1},{6,2},{7,3},{8,12},{9,13},{10,... | collective-permute-start | bytes 29960 | tf_op jit(solution)/shard_map/ppermute | solution.py:85
  212.3 4.5 %collective-permute-start.16 = (f32[4992]{0:T(1024)S(1)}, f32[4992]{0:T(1024)S(1)}, u32[]{:S(2)}, u32[]{:S(2)}) collective-permute-start(f32[4992]{0:T(1024)S(1)} %maximum_select_fusion.4), channel_id=1, source_target_pairs={{0,32},{32,0},{64,96},{96,64},{128,160},{160,128},{192,224},{224,1... | collective-permute-start | bytes 59912 | tf_op jit(solution)/shard_map/ppermute | solution.py:85
  216.8 4.7 %collective-permute-start.17 = (f32[9984]{0:T(1024)S(1)}, f32[9984]{0:T(1024)S(1)}, u32[]{:S(2)}, u32[]{:S(2)}) collective-permute-start(f32[9984]{0:T(1024)S(1)} %maximum_select_fusion.3), channel_id=1, source_target_pairs={{0,2},{1,3},{2,0},{3,1},{4,6},{5,7},{6,4},{7,5},{8,10},{9,11},{10,... | collective-permute-start | bytes 119816 | tf_op jit(solution)/shard_map/ppermute | solution.py:85
  221.6 5.2 %collective-permute-start.18 = (f32[19968]{0:T(1024)S(1)}, f32[19968]{0:T(1024)S(1)}, u32[]{:S(2)}, u32[]{:S(2)}) collective-permute-start(f32[19968]{0:T(1024)S(1)} %maximum_select_fusion.2), channel_id=1, source_target_pairs={{0,16},{16,0},{1,17},{17,1},{2,18},{18,2},{3,19},{19,3},{4,20},{20... | collective-permute-start | bytes 239624 | tf_op jit(solution)/shard_map/ppermute | solution.py:85
  226.8 19.9 %collective-permute-start.19 = (f32[39936]{0:T(1024)S(1)}, f32[39936]{0:T(1024)S(1)}, u32[]{:S(2)}, u32[]{:S(2)}) collective-permute-start(f32[39936]{0:T(1024)S(1)} %maximum_select_fusion.1), channel_id=1, source_target_pairs={{0,1},{1,0},{2,3},{3,2},{4,5},{5,4},{6,7},{7,6},{8,9},{9,8},{10,11... | collective-permute-start | bytes 479240 | tf_op jit(solution)/shard_map/ppermute | solution.py:85
Sparse Core Ops, SparseCore 0:
  10.4 56.0 all-gather.1
  86.2 66.2 reduce-scatter.1

commit v3 on v0

--- a/solution.py
+++ b/solution.py
@@ -48,6 +48,23 @@
     return (grad_kernel, jnp.stack([grad_bias, grad_gain, grad_shift]))
 
 
+def exchange_sum(values, axes):
+    count = lax.axis_size(axes)
+    return lax.all_to_all(values.reshape(count, -1), axes, 0, 0, tiled=True).sum(0)
+
+
+def exchange_gather(values, axes):
+    count = lax.axis_size(axes)
+    copies = jnp.broadcast_to(values[None], (count,) + values.shape)
+    return lax.all_to_all(copies, axes, 0, 0, tiled=True).reshape(-1)
+
+
+def packed_sum(values):
+    inner, outer = ("row", "fsdp"), "dp"
+    values = exchange_sum(exchange_sum(values, inner), outer)
+    return exchange_gather(exchange_gather(values, outer), inner)
+
+
 def shards(images, kernel, conv_bias, ln_gain, ln_shift, w_up, cotangent):
     full_maps = lax.all_gather(images, "row", axis=1, tiled=True)
     padded, unit_field, scale_inv, normed = conv_norm(
@@ -77,7 +94,11 @@
     kernel_part, vector_part = norm_conv_grads(
         padded, unit_field, scale_inv, grad_normed.reshape(unit_field.shape), ln_gain
     )
-    grad_kernel, grad_vectors = lax.psum((kernel_part, vector_part), ("dp", "row", "fsdp"))
+    taps = kernel_part.shape[0] * kernel_part.shape[1]
+    packed = jnp.concatenate([kernel_part.reshape(taps, channels), vector_part], axis=0)
+    packed = packed_sum(packed.reshape(-1)).reshape(packed.shape)
+    grad_kernel = packed[:taps].reshape(kernel_part.shape)
+    grad_vectors = packed[taps:]
     return (hidden.reshape(cotangent.shape), grad_weight[None], grad_kernel, grad_vectors)
 
 

time: 716 us -> 194 us (0.27)
  waiting for transfers between devices: 495 us -> 46.7 us
  blocking collectives: 120 us -> 66.6 us
  local copies, waits for them, and re-layouts: 36.3 us -> 7.51 us
    psum x1 -> x0, waiting for transfers between devices: 460 us -> none  [shards(): lax.psum((kernel_part, vector_part), ('dp', 'row', 'fsdp'))]
    psum x1 -> x0, blocking collectives: 111 us -> none  [shards(): lax.psum((kernel_part, vector_part), ('dp', 'row', 'fsdp'))]
    all_to_all x0 -> x3, blocking collectives: none -> 58.3 us  [the longest x2 44.2 us: exchange_sum(): lax.all_to_all(values.reshape(count, -1), axes, 0, 0, tiled=True).sum(0)]
    another operation x50 -> x49, local copies, waits for them, and re-layouts: 29.7 us -> 0.31 us  [norm_conv_grads(): grad_kernel = jnp.stack(tap_sums).reshape(7, 7, unit_field.shape[-1])]
    all_to_all x0 -> x1, waiting for transfers between devices: none -> 12 us  [exchange_gather(): return lax.all_to_all(copies, axes, 0, 0, tiled=True).reshape(-1)]
  transfers between devices with their start and end apart: 3 -> 3, of which waited for: 2 -> 2; matrix products, arithmetic and copies ran while one was open for 10% -> 21% of each run, Pallas kernels for 0% -> 0%
where the time goes in v3:
time: 194 us
  blocking collectives  66.6 us (34%)
  waiting for transfers between devices  46.7 us (24%)
  other arithmetic  33.4 us (17%)
  matrix products  17.9 us (9%)
  between operations  14.7 us (8%)
  local copies, waits for them, and re-layouts  7.51 us (4%)
  starting transfers between devices  7.02 us (4%)
    all_to_all x2, blocking collectives, exchange_sum(): lax.all_to_all(values.reshape(count, -1), axes, 0, 0, tiled=True).sum(0)  44.2 us
    all_gather x1, waiting for transfers between devices, shards(): weights = lax.all_gather(w_up, 'fsdp', axis=0, tiled=True)  34 us
    all_to_all x1, blocking collectives, exchange_gather(): return lax.all_to_all(copies, axes, 0, 0, tiled=True).reshape(-1)  14 us
    reduce_sum x1, other arithmetic, conv_norm(): centre = jnp.mean(conv_out, axis=-1, keepdims=True)  13.2 us
    all_to_all x1, waiting for transfers between devices, exchange_gather(): return lax.all_to_all(copies, axes, 0, 0, tiled=True).reshape(-1)  12 us
    dot_general x1, matrix products, shards(): pre_act = jnp.dot(flat, weights, preferred_element_type=jnp.float32)  9.2 us
    reduce_sum x2, other arithmetic, norm_conv_grads(): tap_sums.append(jnp.sum(window * grad_conv, axis=(0, 1, 2)))  8.79 us
    all_gather x1, blocking collectives, shards(): full_maps = lax.all_gather(images, 'row', axis=1, tiled=True)  8.27 us
  transfers between devices with their start and end apart: 3, of which 2 were waited for; matrix products, arithmetic and copies ran while one was open for 21% of the time, Pallas kernels for 0%

profile of v3, /device:TPU:1, one launch (start us, length us, event | category | flops | bytes accessed | tf_op | source)
XLA Modules:
  0.0 193.7 jit_solution(16047381718693045372)
XLA Ops:
  7.2 0.0 all-gather.2.cloned.1.call-start
  7.2 0.7 all-gather.2.cloned.1.call-update
  7.9 0.0 reduce-scatter.2.cloned.1.call-start
  7.9 0.0 copy-start.7
  8.0 8.3 %all_gather.6 = bf16[1,16,16,1536]{3,2,0,1:T(8,128)(2,1)S(1)} all-gather(bf16[1,8,16,1536]{3,2,0,1:T(8,128)(2,1)} %bitcast.29), channel_id=1, replica_groups=mesh['dp'=24,'row'=2,'fsdp'=16] {'row'}, dimensions={1}, use_global_device_ids=true | all-gather | bytes 1179648 | tf_op jit(solution)/shard_map/all_gather | solution.py:69
  16.2 0.0 copy-start.1
  16.2 0.2 convert_element_type.24
  16.4 0.0 copy-done.7
  16.4 0.2 slice_reduce_fusion.46
  16.6 0.3 slice_reduce_fusion.48
  16.9 0.3 slice_reduce_fusion.47
  17.3 0.0 copy-done.1
  17.3 13.2 %fusion.16 = (f32[16,16]{1,0:T(8,128)S(1)}, f32[1,16,16,1536]{3,2,0,1:T(8,128)S(1)}) fusion(f32[1536]{0:T(1024)S(1)} %get-tuple-element.117, f32[1536]{0:T(1024)S(1)} %get-tuple-element.118, f32[1536]{0:T(1024)S(1)} %get-tuple-element.71, f32[1536]{0:T(1024)S(1)} %get-tuple-element.72, f32[1536]{0:T(1024)S(1)} %get-tuple-element.73, ...), kind=kLoop, calls=%fused_computation.187 | loop fusion | flops 38928128 | bytes 3453952 | tf_op jit(solution)/shard_map/reduce_sum | solution.py:25
  30.5 0.0 copy-start.8
  30.5 0.0 copy-start.9
  30.6 0.3 multiply_reduce_fusion.52
  30.9 0.4 copy-done.8
  31.2 0.0 copy-done.9
  31.3 1.2 add_convert_fusion
  32.5 34.0 %all-gather.2.cloned.1.call-done = bf16[1536,1536]{1,0:T(8,128)(2,1)} async-done(((bf16[96,1536]{1,0:T(8,128)(2,1)}), bf16[1536,1536]{1,0:T(8,128)(2,1)}) %all-gather.2.cloned.1.call-update) | async-done | bytes 4718608 | tf_op jit(solution)/shard_map/all_gather | solution.py:76
  66.5 0.0 copy-start.3
  66.5 9.2 %fusion.5 = (bf16[256,1536]{1,0:T(8,128)(2,1)S(1)}, f32[256,1536]{1,0:T(8,128)}, f32[256,1536]{1,0:T(8,128)}) fusion(bf16[1,16,16,1536]{3,2,1,0:T(8,128)(2,1)} %param.13, bf16[256,1536]{1,0:T(8,128)(2,1)} %bitcast.25, bf16[1536,1536]{1,0:T(8,128)(2,1)} %all-gather.2.cloned.1.call-done), kind=kOutput, calls=%fused_computation.57 | convolution fusion | flops 1236664320 | bytes 10223616 | tf_op jit(solution)/shard_map/dot_general | solution.py:77
  75.7 0.0 copy-start.6
  75.7 0.9 copy-done.6
  76.6 0.0 copy-done.3
  76.6 3.5 %convolution_convert_fusion = bf16[1536,1536]{1,0:T(8,128)(2,1)} fusion(bf16[256,1536]{1,0:T(8,128)(2,1)S(1)} %bitcast.26, bf16[256,1536]{1,0:T(8,128)(2,1)S(1)} %get-tuple-element.120), kind=kOutput, calls=%fused_computation.48 | convolution fusion | flops 1210318848 | bytes 6291456 | tf_op jit(solution)/shard_map/dot_general | solution.py:84
  80.1 0.0 reduce-scatter.2.cloned.1.call-update
  80.1 5.2 %fusion.13 = (f32[1536]{0:T(1024)S(1)}, f32[256]{0:T(256)S(1)}, f32[256,1536]{1,0:T(8,128)}) fusion(f32[1536]{0:T(1024)S(1)} %copy-done.8, bf16[256,1536]{1,0:T(8,128)(2,1)} %copy-done.6, bf16[1536,1536]{1,0:T(8,128)(2,1)} %all-gather.2.cloned.1.call-done), kind=kOutput, calls=%fused_computation.185 | convolution fusion | flops 1209137408 | bytes 7091200 | tf_op jit(solution)/shard_map/dot_general | solution.py:91
  85.4 0.1 div.17
  85.4 0.0 copy-start
  85.4 2.5 %multiply_reduce_fusion = (f32[1536]{0:T(1024)S(1)}, f32[16,16]{1,0:T(8,128)S(1)}) fusion(f32[1,16,16,1536]{3,2,0,1:T(8,128)S(1)} %get-tuple-element.123, f32[16,16]{1,0:T(8,128)S(1)} %add_rsqrt_fusion, f32[16,16]{1,0:T(8,128)S(1)} %broadcast_multiply_fusion.1, f32[256,1536]{1,0:T(8,128)} %get-tuple-element.125, f32[1,16,16,1536]{3,2,0,1:T(8,128)} %bitcast.24, ...), kind=kLoop, calls=%fused_computation.60 | loop fusion | flops 2750720 | bytes 4733952 | tf_op jit(solution)/shard_map/reduce_sum | solution.py:35
  88.0 0.0 copy-done
  88.0 4.9 %multiply_reduce_fusion.1 = (f32[1536]{0:T(1024)S(1)}, f32[1536]{0:T(1024)S(1)}, f32[1536]{0:T(1024)S(1)}, f32[1536]{0:T(1024)S(1)}, f32[1536]{0:T(1024)S(1)}, /...) fusion(f32[1,16,16,1536]{3,2,0,1:T(8,128)S(1)} %convert_element, ...), kind=kLoop, calls=%fused_computation.61 | loop fusion | flops 16880640 | bytes 6412288 | tf_op jit(solution)/shard_map/reduce_sum | solution.py:46
  92.9 0.0 copy-start.2
  92.9 3.9 %multiply_reduce_fusion.19 = (f32[1536]{0:T(1024)S(1)}, f32[1536]{0:T(1024)S(1)}, f32[1536]{0:T(1024)S(1)}, f32[1536]{0:T(1024)S(1)}, f32[1536]{0:T(1024)S(1)}, ...) fusion(f32[1,16,16,1536]{3,2,0,1:T(8,128)S(1)} %get-tuple-eleme, ...), kind=kLoop, calls=%fused_computation.79 | loop fusion | flops 14128128 | bytes 3256320 | tf_op jit(solution)/shard_map/reduce_sum | solution.py:46
  97.1 0.0 copy-done.2
  97.1 2.5 %fusion.14 = (f32[1536]{0:T(1024)S(1)}, f32[1536]{0:T(1024)S(1)}, f32[1536]{0:T(1024)S(1)}, f32[1536]{0:T(1024)S(1)}, f32[1536]{0:T(1024)S(1)}, /*index=5*/f32[1...) fusion(f32[1,16,16,1536]{3,2,0,1:T(8,128)S(1)} %get-tuple-eleme, ...), kind=kLoop, calls=%fused_computation.186 | loop fusion | flops 10988544 | bytes 4018176 | tf_op jit(solution)/shard_map/reduce_sum | solution.py:41
  100.0 0.0 copy-start.5
  100.0 0.5 concatenate.3
  100.6 0.0 copy-start.4
  100.6 1.2 all_to_all.20
  101.8 19.9 %all_to_all.30 = f32[32,1,2496]{2,1,0:T(1,128)S(1)} all-to-all(f32[32,1,2496]{2,1,0:T(1,128)} %all_to_all.20), channel_id=1, replica_groups=mesh['dp'=24,'row'=2,'fsdp'=16] {'row','fsdp'}, dimensions={0} | all-to-all | bytes 638976 | tf_op jit(solution)/shard_map/all_to_all | solution.py:53
  121.7 0.2 reduce_sum.578
  121.9 0.1 all_to_all.22
  122.0 24.3 %all_to_all.31 = f32[24,1,104]{2,1,0:T(1,128)S(1)} all-to-all(f32[24,1,104]{2,1,0:T(1,128)S(1)} %all_to_all.22), channel_id=1, replica_groups=mesh['dp'=24,'row'=2,'fsdp'=16] {'dp'}, dimensions={0} | all-to-all | bytes 19968 | tf_op jit(solution)/shard_map/all_to_all | solution.py:53
  146.4 14.0 %all_to_all.32 = f32[24,1,104]{2,1,0:T(1,128)S(1)} all-to-all(f32[24,1,104]{2,1,0:T(1,128)S(1)} %broadcast_in_dim.13), channel_id=1, replica_groups=mesh['dp'=24,'row'=2,'fsdp'=16] {'dp'}, dimensions={0} | all-to-all | bytes 19968 | tf_op jit(solution)/shard_map/all_to_all | solution.py:59
  160.4 0.5 broadcast.200
  160.9 0.7 reduce.109
  161.6 0.1 broadcast_in_dim.14
  161.7 0.9 broadcast_in_dim.15
  162.6 6.9 %all-to-all-start.3 = ((f32[32,1,2496]{2,1,0:T(1,128)}), f32[32,1,2496]{2,1,0:T(1,128)S(1)}, u32[]{:S(2)}, u32[]{:S(2)}) async-start(f32[32,1,2496]{2,1,0:T(1,128)} %broadcast_in_dim.15), calls=%async_computation.4 | async-start | bytes 655360 | tf_op jit(solution)/shard_map/all_to_all | solution.py:59
  169.5 0.0 copy-done.5
  169.5 0.0 copy-done.4
  169.6 1.1 multiply_convert_fusion
  170.7 12.0 %all-to-all-done.3 = f32[32,1,2496]{2,1,0:T(1,128)S(1)} async-done(((f32[32,1,2496]{2,1,0:T(1,128)}), f32[32,1,2496]{2,1,0:T(1,128)S(1)}, u32[]{:S(2)}, u32[]{:S(2)}) %all-to-all-start.3) | async-done | bytes 319520 | tf_op jit(solution)/shard_map/all_to_all | solution.py:59
  182.7 0.8 reduce.57
  183.4 0.2 reshape_reshape.4
  183.7 0.6 slice.447
  184.3 0.8 reshape.269
  185.1 0.0 reduce-scatter.2.cloned.1.call-done
  185.1 1.8 bitcast_convert_fusion
  (58 shorter events, 0.4 us)
Async XLA Ops:
  7.2 59.3 %all-gather.2.cloned.1.call-start = ((), (), s32[]{:S(2)}) async-start(), calls=%async_computation.5 | async-start | bytes 5013504 | tf_op jit(solution)/shard_map/all_gather | solution.py:76
  7.9 177.2 %reduce-scatter.2.cloned.1.call-start = ((), (), s32[]{:S(2)}) async-start(), calls=%async_computation.6 | async-start | bytes 5013504 | tf_op jit(solution)/shard_map/reduce_scatter | solution.py:83
  7.9 8.5 %copy-start.7 = (f32[7,7,1536]{2,1,0:T(8,128)S(1)}, f32[7,7,1536]{2,1,0:T(8,128)}, u32[]{:S(2)}) copy-start(f32[7,7,1536]{2,1,0:T(8,128)} %param.8) | copy-start | bytes 903172
  16.2 1.0 copy-start.1
  30.5 0.7 copy-start.8
  30.5 0.7 copy-start.9
  66.5 10.1 %copy-start.3 = (bf16[1,16,16,1536]{3,2,0,1:T(8,128)(2,1)S(1)}, bf16[1,16,16,1536]{3,2,0,1:T(8,128)(2,1)}, u32[]{:S(2)}) copy-start(bf16[1,16,16,1536]{3,2,0,1:T(8,128)(2,1)} %add_convert_fusion) | copy-start | bytes 2359300
  75.7 0.9 copy-start.6
  85.4 2.5 %copy-start = (f32[256,1536]{1,0:T(8,128)S(1)}, f32[256,1536]{1,0:T(8,128)}, u32[]{:S(2)}) copy-start(f32[256,1536]{1,0:T(8,128)} %get-tuple-element.125) | copy-start | bytes 4718596
  92.9 4.2 %copy-start.2 = (bf16[1,16,16,1536]{3,2,0,1:T(8,128)(2,1)S(1)}, bf16[1,16,16,1536]{3,2,0,1:T(8,128)(2,1)}, u32[]{:S(2)}) copy-start(bf16[1,16,16,1536]{3,2,0,1:T(8,128)(2,1)} %copy-done.1) | copy-start | bytes 2359300
  100.0 69.5 %copy-start.5 = (f32[256,1536]{1,0:T(8,128)S(1)}, f32[256,1536]{1,0:T(8,128)}, u32[]{:S(2)}) copy-start(f32[256,1536]{1,0:T(8,128)} %get-tuple-element.124) | copy-start | bytes 4718596
  100.6 69.0 %copy-start.4 = (f32[256,1536]{1,0:T(8,128)S(1)}, f32[256,1536]{1,0:T(8,128)}, u32[]{:S(2)}) copy-start(f32[256,1536]{1,0:T(8,128)} %get-tuple-element.121) | copy-start | bytes 4718596
  162.6 20.1 %all-to-all-start.3 = ((f32[32,1,2496]{2,1,0:T(1,128)}), f32[32,1,2496]{2,1,0:T(1,128)S(1)}, u32[]{:S(2)}, u32[]{:S(2)}) async-start(f32[32,1,2496]{2,1,0:T(1,128)} %broadcast_in_dim.15), calls=%async_computation.4 | async-start | bytes 655360 | tf_op jit(solution)/shard_map/all_to_all | solution.py:59
Sparse Core Ops, SparseCore 0:
  10.4 56.0 all-gather.1
  80.3 70.8 reduce-scatter.1

commit v4 on v3

--- a/solution.py
+++ b/solution.py
@@ -61,8 +61,9 @@
 
 def packed_sum(values):
     inner, outer = ("row", "fsdp"), "dp"
-    values = exchange_sum(exchange_sum(values, inner), outer)
-    return exchange_gather(exchange_gather(values, outer), inner)
+    values = exchange_sum(values, inner)
+    values = exchange_gather(values, outer).reshape(lax.axis_size(outer), -1).sum(0)
+    return exchange_gather(values, inner)
 
 
 def shards(images, kernel, conv_bias, ln_gain, ln_shift, w_up, cotangent):

time: 194 us -> 183 us (0.943)
  blocking collectives: 66.6 us -> 56.1 us
    all_to_all x2 -> x1, blocking collectives: 44.2 us -> 20 us  [exchange_sum(): lax.all_to_all(values.reshape(count, -1), axes, 0, 0, tiled=True).sum(0)]
    all_to_all x1, blocking collectives: 14 us -> 27.8 us  [exchange_gather(): return lax.all_to_all(copies, axes, 0, 0, tiled=True).reshape(-1)]
  transfers between devices with their start and end apart: 3 -> 3, of which waited for: 2 -> 2; matrix products, arithmetic and copies ran while one was open for 21% -> 23% of each run, Pallas kernels for 0% -> 0%
where the time goes in v4:
time: 183 us; the launch traced here: 182 us
  blocking collectives  56.1 us (31%)
  waiting for transfers between devices  46.6 us (25%)
  other arithmetic  33.8 us (18%)
  matrix products  17.9 us (10%)
  between operations  14.7 us (8%)
  starting transfers between devices  7.06 us (4%)
  local copies, waits for them, and re-layouts  6.21 us (3%)
    all_gather x1, waiting for transfers between devices, shards(): weights = lax.all_gather(w_up, 'fsdp', axis=0, tiled=True)  34 us
    all_to_all x1, blocking collectives, exchange_gather(): return lax.all_to_all(copies, axes, 0, 0, tiled=True).reshape(-1)  27.8 us
    all_to_all x1, blocking collectives, exchange_sum(): lax.all_to_all(values.reshape(count, -1), axes, 0, 0, tiled=True).sum(0)  20 us
    reduce_sum x1, other arithmetic, conv_norm(): centre = jnp.mean(conv_out, axis=-1, keepdims=True)  13.2 us
    all_to_all x1, waiting for transfers between devices, exchange_gather(): return lax.all_to_all(copies, axes, 0, 0, tiled=True).reshape(-1)  12 us
    dot_general x1, matrix products, shards(): pre_act = jnp.dot(flat, weights, preferred_element_type=jnp.float32)  9.2 us
    reduce_sum x2, other arithmetic, norm_conv_grads(): tap_sums.append(jnp.sum(window * grad_conv, axis=(0, 1, 2)))  8.78 us
    all_gather x1, blocking collectives, shards(): full_maps = lax.all_gather(images, 'row', axis=1, tiled=True)  8.27 us
  transfers between devices with their start and end apart: 3, of which 2 were waited for; matrix products, arithmetic and copies ran while one was open for 23% of the time, Pallas kernels for 0%

profile of v4, /device:TPU:1, one launch (start us, length us, event | category | flops | bytes accessed | tf_op | source)
XLA Modules:
  0.0 182.4 jit_solution(11079543469418801425)
XLA Ops:
  7.2 0.0 all-gather.2.cloned.1.call-start
  7.2 0.7 all-gather.2.cloned.1.call-update
  7.9 0.0 reduce-scatter.2.cloned.1.call-start
  7.9 0.0 copy-start.7
  8.0 8.3 %all_gather.6 = bf16[1,16,16,1536]{3,2,0,1:T(8,128)(2,1)S(1)} all-gather(bf16[1,8,16,1536]{3,2,0,1:T(8,128)(2,1)} %bitcast.28), channel_id=1, replica_groups=mesh['dp'=24,'row'=2,'fsdp'=16] {'row'}, dimensions={1}, use_global_device_ids=true | all-gather | bytes 1179648 | tf_op jit(solution)/shard_map/all_gather | solution.py:70
  16.2 0.0 copy-start.1
  16.2 0.2 convert_element_type.24
  16.4 0.0 copy-done.7
  16.4 0.2 slice_reduce_fusion.46
  16.6 0.3 slice_reduce_fusion.48
  16.9 0.3 slice_reduce_fusion.47
  17.3 0.0 copy-done.1
  17.3 13.2 %fusion.16 = (f32[16,16]{1,0:T(8,128)S(1)}, f32[1,16,16,1536]{3,2,0,1:T(8,128)S(1)}) fusion(f32[1536]{0:T(1024)S(1)} %get-tuple-element.117, f32[1536]{0:T(1024)S(1)} %get-tuple-element.118, f32[1536]{0:T(1024)S(1)} %get-tuple-element.71, f32[1536]{0:T(1024)S(1)} %get-tuple-element.72, f32[1536]{0:T(1024)S(1)} %get-tuple-element.73, ...), kind=kLoop, calls=%fused_computation.187 | loop fusion | flops 38928128 | bytes 3453952 | tf_op jit(solution)/shard_map/reduce_sum | solution.py:25
  30.5 0.0 copy-start.8
  30.5 0.0 copy-start.9
  30.6 0.3 multiply_reduce_fusion.52
  30.9 0.4 copy-done.8
  31.2 0.0 copy-done.9
  31.3 1.2 add_convert_fusion
  32.5 34.0 %all-gather.2.cloned.1.call-done = bf16[1536,1536]{1,0:T(8,128)(2,1)} async-done(((bf16[96,1536]{1,0:T(8,128)(2,1)}), bf16[1536,1536]{1,0:T(8,128)(2,1)}) %all-gather.2.cloned.1.call-update) | async-done | bytes 4718608 | tf_op jit(solution)/shard_map/all_gather | solution.py:77
  66.5 0.0 copy-start.3
  66.5 9.2 %fusion.5 = (bf16[256,1536]{1,0:T(8,128)(2,1)S(1)}, f32[256,1536]{1,0:T(8,128)}, f32[256,1536]{1,0:T(8,128)}) fusion(bf16[1,16,16,1536]{3,2,1,0:T(8,128)(2,1)} %param.13, bf16[256,1536]{1,0:T(8,128)(2,1)} %bitcast.24, bf16[1536,1536]{1,0:T(8,128)(2,1)} %all-gather.2.cloned.1.call-done), kind=kOutput, calls=%fused_computation.57 | convolution fusion | flops 1236664320 | bytes 10223616 | tf_op jit(solution)/shard_map/dot_general | solution.py:78
  75.7 0.0 copy-start.6
  75.7 0.9 copy-done.6
  76.6 0.0 copy-done.3
  76.6 3.5 %convolution_convert_fusion = bf16[1536,1536]{1,0:T(8,128)(2,1)} fusion(bf16[256,1536]{1,0:T(8,128)(2,1)S(1)} %bitcast.25, bf16[256,1536]{1,0:T(8,128)(2,1)S(1)} %get-tuple-element.120), kind=kOutput, calls=%fused_computation.48 | convolution fusion | flops 1210318848 | bytes 6291456 | tf_op jit(solution)/shard_map/dot_general | solution.py:85
  80.1 0.0 reduce-scatter.2.cloned.1.call-update
  80.1 5.2 %fusion.13 = (f32[1536]{0:T(1024)S(1)}, f32[256]{0:T(256)S(1)}, f32[256,1536]{1,0:T(8,128)}) fusion(f32[1536]{0:T(1024)S(1)} %copy-done.8, bf16[256,1536]{1,0:T(8,128)(2,1)} %copy-done.6, bf16[1536,1536]{1,0:T(8,128)(2,1)} %all-gather.2.cloned.1.call-done), kind=kOutput, calls=%fused_computation.185 | convolution fusion | flops 1209137408 | bytes 7091200 | tf_op jit(solution)/shard_map/dot_general | solution.py:92
  85.3 0.1 div.17
  85.4 0.0 copy-start
  85.4 2.5 %multiply_reduce_fusion = (f32[1536]{0:T(1024)S(1)}, f32[16,16]{1,0:T(8,128)S(1)}) fusion(f32[1,16,16,1536]{3,2,0,1:T(8,128)S(1)} %get-tuple-element.123, f32[16,16]{1,0:T(8,128)S(1)} %add_rsqrt_fusion, f32[16,16]{1,0:T(8,128)S(1)} %broadcast_multiply_fusion.1, f32[256,1536]{1,0:T(8,128)} %get-tuple-element.125, f32[1,16,16,1536]{3,2,0,1:T(8,128)} %bitcast.23, ...), kind=kLoop, calls=%fused_computation.60 | loop fusion | flops 2750720 | bytes 4733952 | tf_op jit(solution)/shard_map/reduce_sum | solution.py:35
  88.0 0.0 copy-done
  88.0 4.9 %multiply_reduce_fusion.1 = (f32[1536]{0:T(1024)S(1)}, f32[1536]{0:T(1024)S(1)}, f32[1536]{0:T(1024)S(1)}, f32[1536]{0:T(1024)S(1)}, f32[1536]{0:T(1024)S(1)}, /...) fusion(f32[1,16,16,1536]{3,2,0,1:T(8,128)S(1)} %convert_element, ...), kind=kLoop, calls=%fused_computation.61 | loop fusion | flops 16880640 | bytes 6412288 | tf_op jit(solution)/shard_map/reduce_sum | solution.py:46
  92.9 0.0 copy-start.2
  92.9 3.9 %multiply_reduce_fusion.19 = (f32[1536]{0:T(1024)S(1)}, f32[1536]{0:T(1024)S(1)}, f32[1536]{0:T(1024)S(1)}, f32[1536]{0:T(1024)S(1)}, f32[1536]{0:T(1024)S(1)}, ...) fusion(f32[1,16,16,1536]{3,2,0,1:T(8,128)S(1)} %get-tuple-eleme, ...), kind=kLoop, calls=%fused_computation.79 | loop fusion | flops 14128128 | bytes 3256320 | tf_op jit(solution)/shard_map/reduce_sum | solution.py:46
  96.8 0.0 copy-done.2
  96.8 2.5 %fusion.14 = (f32[1536]{0:T(1024)S(1)}, f32[1536]{0:T(1024)S(1)}, f32[1536]{0:T(1024)S(1)}, f32[1536]{0:T(1024)S(1)}, f32[1536]{0:T(1024)S(1)}, /*index=5*/f32[1...) fusion(f32[1,16,16,1536]{3,2,0,1:T(8,128)S(1)} %get-tuple-eleme, ...), kind=kLoop, calls=%fused_computation.186 | loop fusion | flops 10988544 | bytes 4018176 | tf_op jit(solution)/shard_map/reduce_sum | solution.py:41
  100.0 0.5 concatenate.3
  100.5 0.0 copy-start.5
  100.6 0.5 all_to_all.14
  101.0 0.0 copy-start.4
  101.0 20.0 %all_to_all.21 = f32[32,1,2496]{2,1,0:T(1,128)} all-to-all(f32[32,1,2496]{2,1,0:T(1,128)S(1)} %all_to_all.14), channel_id=1, replica_groups=mesh['dp'=24,'row'=2,'fsdp'=16] {'row','fsdp'}, dimensions={0} | all-to-all | bytes 638976 | tf_op jit(solution)/shard_map/all_to_all | solution.py:53
  121.1 1.2 reduce_sum.578
  122.2 0.1 broadcast_in_dim.11
  122.4 27.8 %all_to_all.22 = f32[24,1,2496]{2,1,0:T(1,128)S(1)} all-to-all(f32[24,1,2496]{2,1,0:T(1,128)S(1)} %broadcast_in_dim.11), channel_id=1, replica_groups=mesh['dp'=24,'row'=2,'fsdp'=16] {'dp'}, dimensions={0} | all-to-all | bytes 479232 | tf_op jit(solution)/shard_map/all_to_all | solution.py:59
  150.2 0.2 reduce_sum.579
  150.3 0.9 broadcast_in_dim.12
  151.2 7.0 %all-to-all-start.2 = ((f32[32,1,2496]{2,1,0:T(1,128)}), f32[32,1,2496]{2,1,0:T(1,128)S(1)}, u32[]{:S(2)}, u32[]{:S(2)}) async-start(f32[32,1,2496]{2,1,0:T(1,128)} %broadcast_in_dim.12), calls=%async_computation.3 | async-start | bytes 655360 | tf_op jit(solution)/shard_map/all_to_all | solution.py:59
  158.2 0.0 copy-done.5
  158.2 0.0 copy-done.4
  158.2 1.1 multiply_convert_fusion
  159.4 12.0 %all-to-all-done.2 = f32[32,1,2496]{2,1,0:T(1,128)S(1)} async-done(((f32[32,1,2496]{2,1,0:T(1,128)}), f32[32,1,2496]{2,1,0:T(1,128)S(1)}, u32[]{:S(2)}, u32[]{:S(2)}) %all-to-all-start.2) | async-done | bytes 319520 | tf_op jit(solution)/shard_map/all_to_all | solution.py:59
  171.3 0.8 reduce.56
  172.1 0.2 reshape_reshape.4
  172.3 0.6 slice.447
  172.9 0.8 reshape.262
  173.7 0.0 reduce-scatter.2.cloned.1.call-done
  173.7 1.8 %bitcast_convert_fusion = f32[1,96,1536]{2,1,0:T(8,128)} fusion(bf16[96,1536]{1,0:T(8,128)(2,1)} %reduce-scatter.2.cloned.1.call-done), kind=kLoop, calls=%fused_computation.131 | loop fusion | flops 147456 | bytes 884736 | tf_op jit(solution)/shard_map/broadcast_in_dim | solution.py:103
  (56 shorter events, 0.4 us)
Async XLA Ops:
  7.2 59.3 %all-gather.2.cloned.1.call-start = ((), (), s32[]{:S(2)}) async-start(), calls=%async_computation.4 | async-start | bytes 5013504 | tf_op jit(solution)/shard_map/all_gather | solution.py:77
  7.9 165.8 %reduce-scatter.2.cloned.1.call-start = ((), (), s32[]{:S(2)}) async-start(), calls=%async_computation.5 | async-start | bytes 5013504 | tf_op jit(solution)/shard_map/reduce_scatter | solution.py:84
  7.9 8.5 %copy-start.7 = (f32[7,7,1536]{2,1,0:T(8,128)S(1)}, f32[7,7,1536]{2,1,0:T(8,128)}, u32[]{:S(2)}) copy-start(f32[7,7,1536]{2,1,0:T(8,128)} %param.8) | copy-start | bytes 903172
  16.2 1.0 copy-start.1
  30.5 0.7 copy-start.8
  30.5 0.7 copy-start.9
  66.5 10.1 %copy-start.3 = (bf16[1,16,16,1536]{3,2,0,1:T(8,128)(2,1)S(1)}, bf16[1,16,16,1536]{3,2,0,1:T(8,128)(2,1)}, u32[]{:S(2)}) copy-start(bf16[1,16,16,1536]{3,2,0,1:T(8,128)(2,1)} %add_convert_fusion) | copy-start | bytes 2359300
  75.7 0.9 copy-start.6
  85.4 2.6 %copy-start = (f32[256,1536]{1,0:T(8,128)S(1)}, f32[256,1536]{1,0:T(8,128)}, u32[]{:S(2)}) copy-start(f32[256,1536]{1,0:T(8,128)} %get-tuple-element.125) | copy-start | bytes 4718596
  92.9 4.0 %copy-start.2 = (bf16[1,16,16,1536]{3,2,0,1:T(8,128)(2,1)S(1)}, bf16[1,16,16,1536]{3,2,0,1:T(8,128)(2,1)}, u32[]{:S(2)}) copy-start(bf16[1,16,16,1536]{3,2,0,1:T(8,128)(2,1)} %copy-done.1) | copy-start | bytes 2359300
  100.5 57.7 %copy-start.5 = (f32[256,1536]{1,0:T(8,128)S(1)}, f32[256,1536]{1,0:T(8,128)}, u32[]{:S(2)}) copy-start(f32[256,1536]{1,0:T(8,128)} %get-tuple-element.124) | copy-start | bytes 4718596
  101.0 57.2 %copy-start.4 = (f32[256,1536]{1,0:T(8,128)S(1)}, f32[256,1536]{1,0:T(8,128)}, u32[]{:S(2)}) copy-start(f32[256,1536]{1,0:T(8,128)} %get-tuple-element.121) | copy-start | bytes 4718596
  151.2 20.1 %all-to-all-start.2 = ((f32[32,1,2496]{2,1,0:T(1,128)}), f32[32,1,2496]{2,1,0:T(1,128)S(1)}, u32[]{:S(2)}, u32[]{:S(2)}) async-start(f32[32,1,2496]{2,1,0:T(1,128)} %broadcast_in_dim.12), calls=%async_computation.3 | async-start | bytes 655360 | tf_op jit(solution)/shard_map/all_to_all | solution.py:59
Sparse Core Ops, SparseCore 0:
  10.4 56.0 all-gather.1
  80.2 70.9 reduce-scatter.1

commit v5 on v4

--- a/solution.py
+++ b/solution.py
@@ -74,24 +74,33 @@
     channels = normed.shape[-1]
     hidden_units = w_up.shape[1]
     flat = normed.reshape(-1, channels)
-    weights = lax.all_gather(w_up, "fsdp", axis=0, tiled=True)
-    pre_act = jnp.dot(flat, weights, preferred_element_type=jnp.float32)
-    activated, pullback = jax.vjp(gelu_exact, pre_act)
-    hidden = activated.astype(jnp.bfloat16)
-    grad_pre = pullback(cotangent.reshape(-1, hidden_units).astype(jnp.float32))[0].astype(
-        jnp.bfloat16
-    )
-    grad_weight = lax.psum_scatter(
-        lax.dot_general(
-            flat, grad_pre, (((0,), (0,)), ((), ())), preferred_element_type=jnp.float32
-        ).astype(jnp.bfloat16),
-        "fsdp",
-        scatter_dimension=0,
-        tiled=True,
-    ).astype(jnp.float32)
-    grad_normed = lax.dot_general(
-        grad_pre, weights, (((1,), (1,)), ((), ())), preferred_element_type=jnp.float32
-    )
+    cot_flat = cotangent.reshape(-1, hidden_units)
+    pieces = 2
+    width = hidden_units // pieces
+    hidden_parts, weight_parts, grad_normed = [], [], None
+    for piece in range(pieces):
+        columns = slice(piece * width, (piece + 1) * width)
+        weights = lax.all_gather(w_up[:, columns], "fsdp", axis=0, tiled=True)
+        pre_act = jnp.dot(flat, weights, preferred_element_type=jnp.float32)
+        activated, pullback = jax.vjp(gelu_exact, pre_act)
+        hidden_parts.append(activated.astype(jnp.bfloat16))
+        grad_pre = pullback(cot_flat[:, columns].astype(jnp.float32))[0].astype(jnp.bfloat16)
+        weight_parts.append(
+            lax.psum_scatter(
+                lax.dot_general(
+                    flat, grad_pre, (((0,), (0,)), ((), ())), preferred_element_type=jnp.float32
+                ).astype(jnp.bfloat16),
+                "fsdp",
+                scatter_dimension=0,
+                tiled=True,
+            ).astype(jnp.float32)
+        )
+        part = lax.dot_general(
+            grad_pre, weights, (((1,), (1,)), ((), ())), preferred_element_type=jnp.float32
+        )
+        grad_normed = part if grad_normed is None else grad_normed + part
+    hidden = jnp.concatenate(hidden_parts, axis=1)
+    grad_weight = jnp.concatenate(weight_parts, axis=1)
     kernel_part, vector_part = norm_conv_grads(
         padded, unit_field, scale_inv, grad_normed.reshape(unit_field.shape), ln_gain
     )

time: 183 us -> 265 us (1.45)
  waiting for transfers between devices: 46.6 us -> 124 us
    reduce_scatter x1 -> x2, waiting for transfers between devices: 0.01 us -> 39.2 us  [shards(): lax.psum_scatter(lax.dot_general(flat, grad_pre, (((0,), (0,)), ((), ()))...]
    all_gather x1 -> x2, waiting for transfers between devices: 34 us -> 73.1 us  [shards(): weights = lax.all_gather(w_up[:, columns], 'fsdp', axis=0, tiled=True)]
    dot_general x1 -> x2, matrix products: 9.2 us -> 11.2 us  [shards(): pre_act = jnp.dot(flat, weights, preferred_element_type=jnp.float32)]
  transfers between devices with their start and end apart: 3 -> 5, of which waited for: 2 -> 4; matrix products, arithmetic and copies ran while one was open for 23% -> 18% of each run, Pallas kernels for 0% -> 0%
where the time goes in v5:
time: 265 us; the launch traced here: 264 us
  waiting for transfers between devices  124 us (47%)
  blocking collectives  55.7 us (21%)
  other arithmetic  34.3 us (13%)
  matrix products  19.8 us (7%)
  between operations  14.5 us (5%)
  local copies, waits for them, and re-layouts  8.54 us (3%)
  starting transfers between devices  7.5 us (3%)
    all_gather x2, waiting for transfers between devices, shards(): weights = lax.all_gather(w_up[:, columns], 'fsdp', axis=0, tiled=True)  73.1 us
    reduce_scatter x2, waiting for transfers between devices, shards(): lax.psum_scatter(lax.dot_general(flat, grad_pre, (((0,), (0,)), ((), ()))...  39.2 us
    all_to_all x1, blocking collectives, exchange_gather(): return lax.all_to_all(copies, axes, 0, 0, tiled=True).reshape(-1)  26.8 us
    all_to_all x1, blocking collectives, exchange_sum(): lax.all_to_all(values.reshape(count, -1), axes, 0, 0, tiled=True).sum(0)  20.6 us
    reduce_sum x1, other arithmetic, conv_norm(): centre = jnp.mean(conv_out, axis=-1, keepdims=True)  13.1 us
    dot_general x2, matrix products, shards(): pre_act = jnp.dot(flat, weights, preferred_element_type=jnp.float32)  11.2 us
    all_to_all x1, waiting for transfers between devices, exchange_gather(): return lax.all_to_all(copies, axes, 0, 0, tiled=True).reshape(-1)  10.6 us
    reduce_sum x2, other arithmetic, norm_conv_grads(): tap_sums.append(jnp.sum(window * grad_conv, axis=(0, 1, 2)))  9.68 us
  transfers between devices with their start and end apart: 5, of which 4 were waited for; matrix products, arithmetic and copies ran while one was open for 18% of the time, Pallas kernels for 0%

profile of v5, /device:TPU:1, one launch (start us, length us, event | category | flops | bytes accessed | tf_op | source)
XLA Modules:
  0.0 264.0 jit_solution(3105239125809699201)
XLA Ops:
  7.2 0.0 all-gather.5.cloned.1.call-start
  7.2 1.7 fusion.32
  8.9 0.0 all-gather.5.cloned.1.call-update
  8.9 0.0 all-gather.3.cloned.1.call-start
  9.0 0.7 all-gather.3.cloned.1.call-update
  9.7 0.0 reduce-scatter.5.cloned.1.call-start
  9.7 0.0 copy-start.10
  9.8 8.3 %all_gather.9 = bf16[1,16,16,1536]{3,2,0,1:T(8,128)(2,1)S(1)} all-gather(bf16[1,8,16,1536]{3,2,0,1:T(8,128)(2,1)} %bitcast.36), channel_id=1, replica_groups=mesh['dp'=24,'row'=2,'fsdp'=16] {'row'}, dimensions={1}, use_global_device_ids=true | all-gather | bytes 1179648 | tf_op jit(solution)/shard_map/all_gather | solution.py:70
  18.0 0.2 convert_element_type.34
  18.2 0.2 slice_reduce_fusion.46
  18.4 0.3 slice_reduce_fusion.48
  18.7 0.3 slice_reduce_fusion.47
  19.1 0.0 copy-done.3
  19.1 0.0 copy-done.18
  19.1 13.1 %fusion.31 = (f32[16,16]{1,0:T(8,128)}, f32[1,16,16,1536]{3,2,0,1:T(8,128)S(1)}) fusion(f32[1536]{0:T(1024)S(1)} %get-tuple-element.117, f32[1536]{0:T(1024)S(1)} %get-tuple-element.118, f32[1536]{0:T(1024)S(1)} %get-tuple-element.71, f32[1536]{0:T(1024)S(1)} %get-tuple-element.72, f32[1536]{0:T(1024)S(1)} %get-tuple-element.73, ...), kind=kLoop, calls=%fused_computation.216 | loop fusion | flops 38928128 | bytes 3453952 | tf_op jit(solution)/shard_map/reduce_sum | solution.py:25
  32.2 0.7 broadcast_multiply_fusion.1
  32.9 0.3 multiply_reduce_fusion.52
  33.2 0.0 copy-start.12
  33.3 1.2 add_convert_fusion
  34.5 29.6 %all-gather.5.cloned.1.call-done = bf16[1536,768]{1,0:T(8,128)(2,1)} async-done(((bf16[96,768]{1,0:T(8,128)(2,1)}), bf16[1536,768]{1,0:T(8,128)(2,1)}) %all-gather.5.cloned.1.call-update) | async-done | bytes 2359312 | tf_op jit(solution)/shard_map/all_gather | solution.py:83
  64.1 3.6 %fusion.33 = f32[256,768]{1,0:T(8,128)} fusion(bf16[256,1536]{1,0:T(8,128)(2,1)} %bitcast.30, bf16[1536,768]{1,0:T(8,128)(2,1)} %all-gather.5.cloned.1.call-done), kind=kOutput, calls=%fused_computation.218 | convolution fusion | flops 603979776 | bytes 3932160 | tf_op jit(solution)/shard_map/dot_general | solution.py:84
  67.7 0.0 copy-done.12
  67.7 43.4 %all-gather.3.cloned.1.call-done = bf16[1536,768]{1,0:T(8,128)(2,1)} async-done(((bf16[96,768]{1,0:T(8,128)(2,1)}), bf16[1536,768]{1,0:T(8,128)(2,1)}) %all-gather.3.cloned.1.call-update) | async-done | bytes 2359312 | tf_op jit(solution)/shard_map/all_gather | solution.py:83
  111.1 7.7 %fusion.5 = (bf16[256,768]{1,0:T(8,128)(2,1)S(1)}, f32[256,768]{1,0:T(8,128)}, bf16[256,768]{1,0:T(8,128)(2,1)S(1)}, f32[256,768]{1,0:T(8,128)}, f32[256,768]{1,0:T(8,128)}) fusion(bf16[256,1536]{1,0:T(8,128)(2,1)} %bitcast.37, f32[256,768]{1,0:T(8,128)} %fusion.33, bf16[256,1536]{1,0:T(8,128)(2,1)} %bitcast.31, ...), kind=kOutput, calls=%fused_computation.119 | convolution fusion | flops 632684544 | bytes 7864320 | tf_op jit(solution)/shard_map/dot_general | solution.py:84
  118.8 0.7 copy-done.6
  119.5 2.2 convolution_convert_fusion
  121.8 0.0 reduce-scatter.5.cloned.1.call-update
  121.8 0.2 reduce-scatter.3.cloned.1.call-start
  122.0 0.0 copy-start.7
  122.0 2.6 fusion.34
  124.7 0.0 copy-start.13
  124.7 1.5 fusion.27
  126.2 0.0 copy-done.13
  126.2 1.2 multiply_reduce_fusion
  127.3 0.5 copy-done.2
  127.9 2.2 convolution_convert_fusion.1
  130.1 0.0 reduce-scatter.3.cloned.1.call-update
  130.1 0.6 copy-done.20
  130.7 0.1 div.17
  130.8 0.0 copy-done.14
  130.8 5.9 %multiply_reduce_fusion.1 = (f32[1536]{0:T(1024)S(1)}, f32[1536]{0:T(1024)S(1)}, f32[1536]{0:T(1024)S(1)}, f32[1536]{0:T(1024)S(1)}, f32[1536]{0:T(1024)S(1)}, /...) fusion(f32[1,16,16,1536]{3,2,0,1:T(8,128)S(1)} %convert_element, ...), kind=kLoop, calls=%fused_computation.52 | loop fusion | flops 16880640 | bytes 6412288 | tf_op jit(solution)/shard_map/reduce_sum | solution.py:46
  136.8 2.5 fusion.28
  139.4 0.0 copy-start.16
  139.4 0.0 copy-start.15
  139.4 3.7 %multiply_reduce_fusion.19 = (f32[1536]{0:T(1024)S(1)}, f32[1536]{0:T(1024)S(1)}, f32[1536]{0:T(1024)S(1)}, f32[1536]{0:T(1024)S(1)}, f32[1536]{0:T(1024)S(1)}, ...) fusion(f32[1,16,16,1536]{3,2,0,1:T(8,128)S(1)} %get-tuple-eleme, ...), kind=kLoop, calls=%fused_computation.70 | loop fusion | flops 14128128 | bytes 3256320 | tf_op jit(solution)/shard_map/reduce_sum | solution.py:46
  143.8 0.5 concatenate.12
  144.3 0.5 all_to_all.14
  144.8 20.6 %all_to_all.21 = f32[32,1,2496]{2,1,0:T(1,128)S(1)} all-to-all(f32[32,1,2496]{2,1,0:T(1,128)S(1)} %all_to_all.14), channel_id=1, replica_groups=mesh['dp'=24,'row'=2,'fsdp'=16] {'row','fsdp'}, dimensions={0} | all-to-all | bytes 638976 | tf_op jit(solution)/shard_map/all_to_all | solution.py:53
  165.5 0.2 reduce_sum.578
  165.7 0.1 broadcast_in_dim.11
  165.8 26.8 %all_to_all.22 = f32[24,1,2496]{2,1,0:T(1,128)S(1)} all-to-all(f32[24,1,2496]{2,1,0:T(1,128)S(1)} %broadcast_in_dim.11), channel_id=1, replica_groups=mesh['dp'=24,'row'=2,'fsdp'=16] {'dp'}, dimensions={0} | all-to-all | bytes 479232 | tf_op jit(solution)/shard_map/all_to_all | solution.py:59
  192.6 0.2 reduce_sum.579
  192.8 0.9 broadcast_in_dim.12
  193.7 7.2 %all-to-all-start.2 = ((f32[32,1,2496]{2,1,0:T(1,128)}), f32[32,1,2496]{2,1,0:T(1,128)S(1)}, u32[]{:S(2)}, u32[]{:S(2)}) async-start(f32[32,1,2496]{2,1,0:T(1,128)} %broadcast_in_dim.12), calls=%async_computation.4 | async-start | bytes 655360 | tf_op jit(solution)/shard_map/all_to_all | solution.py:59
  200.8 0.0 copy-done.8
  200.8 1.6 multiply_convert_fusion
  202.4 0.9 pad_maximum_fusion
  203.4 10.6 %all-to-all-done.2 = f32[32,1,2496]{2,1,0:T(1,128)S(1)} async-done(((f32[32,1,2496]{2,1,0:T(1,128)}), f32[32,1,2496]{2,1,0:T(1,128)S(1)}, u32[]{:S(2)}, u32[]{:S(2)}) %all-to-all-start.2) | async-done | bytes 319520 | tf_op jit(solution)/shard_map/all_to_all | solution.py:59
  213.9 0.8 reduce.56
  214.7 0.2 reshape_reshape.4
  215.0 0.6 slice.465
  215.6 0.8 reshape.263
  216.3 39.2 %reduce-scatter.3.cloned.1.call-done = bf16[96,768]{1,0:T(8,128)(2,1)} async-done(((bf16[1536,768]{1,0:T(8,128)(2,1)}), bf16[96,768]{1,0:T(8,128)(2,1)}) %reduce-scatter.3.cloned.1.call-update) | async-done | bytes 147472 | tf_op jit(solution)/shard_map/reduce_scatter | solution.py:89
  255.6 1.8 fusion.26
  (83 shorter events, 0.4 us)
Async XLA Ops:
  7.2 56.9 %all-gather.5.cloned.1.call-start = ((), (), s32[]{:S(2)}) async-start(), calls=%async_computation.6 | async-start | bytes 2506752 | tf_op jit(solution)/shard_map/all_gather | solution.py:83
  8.9 102.2 %all-gather.3.cloned.1.call-start = ((), (), s32[]{:S(2)}) async-start(), calls=%async_computation.5 | async-start | bytes 2506752 | tf_op jit(solution)/shard_map/all_gather | solution.py:83
  9.7 206.6 %reduce-scatter.5.cloned.1.call-start = ((), (), s32[]{:S(2)}) async-start(), calls=%async_computation.8 | async-start | bytes 2506752 | tf_op jit(solution)/shard_map/reduce_scatter | solution.py:89
  9.7 8.5 %copy-start.10 = (f32[7,7,1536]{2,1,0:T(8,128)S(1)}, f32[7,7,1536]{2,1,0:T(8,128)}, u32[]{:S(2)}) copy-start(f32[7,7,1536]{2,1,0:T(8,128)} %param.8) | copy-start | bytes 903172
  18.0 1.0 copy-start.3
  18.0 1.0 copy-start.18
  32.2 1.0 copy-start.11
  32.2 1.0 copy-start.19
  33.2 34.4 %copy-start.12 = (f32[16,16]{1,0:T(8,128)}, f32[16,16]{1,0:T(8,128)S(1)}, u32[]{:S(2)}) copy-start(f32[16,16]{1,0:T(8,128)S(1)} %add_rsqrt_fusion) | copy-start | bytes 3076
  111.1 8.4 %copy-start.1 = (bf16[1,16,16,1536]{3,2,0,1:T(8,128)(2,1)S(1)}, bf16[1,16,16,1536]{3,2,0,1:T(8,128)(2,1)}, u32[]{:S(2)}) copy-start(bf16[1,16,16,1536]{3,2,0,1:T(8,128)(2,1)} %add_convert_fusion) | copy-start | bytes 2359300
  118.8 0.7 copy-start.6
  121.8 133.8 %reduce-scatter.3.cloned.1.call-start = ((), (), s32[]{:S(2)}) async-start(), calls=%async_computation.7 | async-start | bytes 2506752 | tf_op jit(solution)/shard_map/reduce_scatter | solution.py:89
  122.0 2.6 %copy-start.5 = (bf16[1536,768]{1,0:T(8,128)(2,1)S(1)}, bf16[1536,768]{1,0:T(8,128)(2,1)}, u32[]{:S(2)}) copy-start(bf16[1536,768]{1,0:T(8,128)(2,1)} %all-gather.5.cloned.1.call-done) | copy-start | bytes 7077892
  122.0 2.6 %copy-start.7 = (bf16[256,768]{1,0:T(8,128)(2,1)S(1)}, bf16[256,768]{1,0:T(8,128)(2,1)}, u32[]{:S(2)}) copy-start(bf16[256,768]{1,0:T(8,128)(2,1)} %copy-done.6) | copy-start | bytes 1179652
  124.7 1.5 copy-start.13
  126.2 1.2 copy-start
  126.2 1.7 copy-start.2
  130.1 0.6 copy-start.20
  130.1 0.7 copy-start.17
  130.1 0.7 copy-start.14
  130.8 6.0 %copy-start.4 = (bf16[1,16,16,1536]{3,2,0,1:T(8,128)(2,1)S(1)}, bf16[1,16,16,1536]{3,2,0,1:T(8,128)(2,1)}, u32[]{:S(2)}) copy-start(bf16[1,16,16,1536]{3,2,0,1:T(8,128)(2,1)} %copy-done.3) | copy-start | bytes 2359300
  139.4 4.3 %copy-start.16 = (f32[1536]{0:T(1024)S(1)}, f32[1536]{0:T(1024)}, u32[]{:S(2)}) copy-start(f32[1536]{0:T(1024)} %get-tuple-element.52) | copy-start | bytes 18436
  139.4 4.3 %copy-start.15 = (f32[1536]{0:T(1024)S(1)}, f32[1536]{0:T(1024)}, u32[]{:S(2)}) copy-start(f32[1536]{0:T(1024)} %get-tuple-element.54) | copy-start | bytes 18436
  144.8 56.0 %copy-start.8 = (f32[256,768]{1,0:T(8,128)S(1)}, f32[256,768]{1,0:T(8,128)}, u32[]{:S(2)}) copy-start(f32[256,768]{1,0:T(8,128)} %fusion.33) | copy-start | bytes 2359300
  144.8 56.0 %copy-start.9 = (f32[256,768]{1,0:T(8,128)S(1)}, f32[256,768]{1,0:T(8,128)}, u32[]{:S(2)}) copy-start(f32[256,768]{1,0:T(8,128)} %get-tuple-element.121) | copy-start | bytes 2359300
  193.7 20.3 %all-to-all-start.2 = ((f32[32,1,2496]{2,1,0:T(1,128)}), f32[32,1,2496]{2,1,0:T(1,128)S(1)}, u32[]{:S(2)}, u32[]{:S(2)}) async-start(f32[32,1,2496]{2,1,0:T(1,128)} %broadcast_in_dim.12), calls=%async_computation.4 | async-start | bytes 655360 | tf_op jit(solution)/shard_map/all_to_all | solution.py:59
Sparse Core Ops, SparseCore 0:
  11.0 53.0 all-gather.4
  67.1 43.9 all-gather.2
  121.9 65.6 reduce-scatter.4
  190.6 64.9 reduce-scatter.2

commit v6 on v4

--- a/solution.py
+++ b/solution.py
@@ -60,10 +60,14 @@
 
 
 def packed_sum(values):
-    inner, outer = ("row", "fsdp"), "dp"
+    inner, outer = ("dp_hi", "row") + FSDP, "z"
     values = exchange_sum(values, inner)
     values = exchange_gather(values, outer).reshape(lax.axis_size(outer), -1).sum(0)
     return exchange_gather(values, inner)
+
+
+DP = ("dp_hi", "z")
+FSDP = ("y", "core")
 
 
 def shards(images, kernel, conv_bias, ln_gain, ln_shift, w_up, cotangent):
@@ -74,7 +78,7 @@
     channels = normed.shape[-1]
     hidden_units = w_up.shape[1]
     flat = normed.reshape(-1, channels)
-    weights = lax.all_gather(w_up, "fsdp", axis=0, tiled=True)
+    weights = lax.all_gather(w_up, FSDP, axis=0, tiled=True)
     pre_act = jnp.dot(flat, weights, preferred_element_type=jnp.float32)
     activated, pullback = jax.vjp(gelu_exact, pre_act)
     hidden = activated.astype(jnp.bfloat16)
@@ -85,7 +89,7 @@
         lax.dot_general(
             flat, grad_pre, (((0,), (0,)), ((), ())), preferred_element_type=jnp.float32
         ).astype(jnp.bfloat16),
-        "fsdp",
+        FSDP,
         scatter_dimension=0,
         tiled=True,
     ).astype(jnp.float32)
@@ -104,18 +108,22 @@
 
 
 def solution(mesh):
+    replicas, rows, fsdp = (mesh.shape[name] for name in ("dp", "row", "fsdp"))
+    fine = jax.sharding.Mesh(
+        mesh.devices.reshape(2, replicas // 2, rows, fsdp // 2, 2), ("dp_hi", "z", "row") + FSDP
+    )
     return jax.shard_map(
         shards,
-        mesh=mesh,
+        mesh=fine,
         in_specs=(
-            P(("dp", "fsdp"), "row", None, None),
+            P(DP + FSDP, "row", None, None),
             P(),
             P(),
             P(),
             P(),
-            P("fsdp", "row"),
-            P(("dp", "fsdp"), None, None, "row"),
+            P(FSDP, "row"),
+            P(DP + FSDP, None, None, "row"),
         ),
-        out_specs=(P(("dp", "fsdp"), None, None, "row"), P("dp", "fsdp", "row"), P(), P()),
+        out_specs=(P(DP + FSDP, None, None, "row"), P(DP, FSDP, "row"), P(), P()),
         check_vma=False,
     )

time: 183 us -> 178 us (0.973)
  blocking collectives: 56.1 us -> 50.1 us
    all_to_all x1, blocking collectives: 27.8 us -> 19.2 us  [exchange_gather(): return lax.all_to_all(copies, axes, 0, 0, tiled=True).reshape(-1)]
    all_to_all x1, blocking collectives: 20 us -> 22.6 us  [exchange_sum(): lax.all_to_all(values.reshape(count, -1), axes, 0, 0, tiled=True).sum(0)]
where the time goes in v6:
time: 178 us; the launch traced here: 177 us
  blocking collectives  50.1 us (28%)
  waiting for transfers between devices  46.8 us (26%)
  other arithmetic  32.7 us (18%)
  matrix products  17.9 us (10%)
  between operations  14.7 us (8%)
  starting transfers between devices  7.93 us (4%)
  local copies, waits for them, and re-layouts  7.05 us (4%)
    all_gather x1, waiting for transfers between devices, shards(): weights = lax.all_gather(w_up, FSDP, axis=0, tiled=True)  34 us
    all_to_all x1, blocking collectives, exchange_sum(): lax.all_to_all(values.reshape(count, -1), axes, 0, 0, tiled=True).sum(0)  22.6 us
    all_to_all x1, blocking collectives, exchange_gather(): return lax.all_to_all(copies, axes, 0, 0, tiled=True).reshape(-1)  19.2 us
    reduce_sum x1, other arithmetic, conv_norm(): centre = jnp.mean(conv_out, axis=-1, keepdims=True)  13.2 us
    all_to_all x1, waiting for transfers between devices, exchange_gather(): return lax.all_to_all(copies, axes, 0, 0, tiled=True).reshape(-1)  12.1 us
    dot_general x1, matrix products, shards(): pre_act = jnp.dot(flat, weights, preferred_element_type=jnp.float32)  9.2 us
    reduce_sum x2, other arithmetic, norm_conv_grads(): tap_sums.append(jnp.sum(window * grad_conv, axis=(0, 1, 2)))  8.78 us
    all_gather x1, blocking collectives, shards(): full_maps = lax.all_gather(images, 'row', axis=1, tiled=True)  8.27 us
  transfers between devices with their start and end apart: 3, of which 2 were waited for; matrix products, arithmetic and copies ran while one was open for 23% of the time, Pallas kernels for 0%

profile of v6, /device:TPU:1, one launch (start us, length us, event | category | flops | bytes accessed | tf_op | source)
XLA Modules:
  0.0 177.2 jit_solution(9235593374017545456)
XLA Ops:
  7.2 0.0 all-gather.2.cloned.1.call-start
  7.2 0.7 all-gather.2.cloned.1.call-update
  7.9 0.0 reduce-scatter.2.cloned.1.call-start
  7.9 0.0 copy-start.7
  8.0 8.3 %all_gather.6 = bf16[1,16,16,1536]{3,2,0,1:T(8,128)(2,1)S(1)} all-gather(bf16[1,8,16,1536]{3,2,0,1:T(8,128)(2,1)} %bitcast.28), channel_id=1, replica_groups=mesh['dp_hi'=2,'z'=12,'row'=2,'y'=8,'core'=2] {'row'}, dimensions={1}, use_global_device_ids=true | all-gather | bytes 1179648 | tf_op jit(solution)/shard_map/all_gather | solution.py:74
  16.2 0.0 copy-start.1
  16.2 0.2 convert_element_type.24
  16.4 0.0 copy-done.7
  16.4 0.2 slice_reduce_fusion.46
  16.6 0.3 slice_reduce_fusion.48
  16.9 0.3 slice_reduce_fusion.47
  17.3 0.0 copy-done.1
  17.3 13.2 %fusion.16 = (f32[16,16]{1,0:T(8,128)S(1)}, f32[1,16,16,1536]{3,2,0,1:T(8,128)S(1)}) fusion(f32[1536]{0:T(1024)S(1)} %get-tuple-element.117, f32[1536]{0:T(1024)S(1)} %get-tuple-element.118, f32[1536]{0:T(1024)S(1)} %get-tuple-element.71, f32[1536]{0:T(1024)S(1)} %get-tuple-element.72, f32[1536]{0:T(1024)S(1)} %get-tuple-element.73, ...), kind=kLoop, calls=%fused_computation.187 | loop fusion | flops 38928128 | bytes 3453952 | tf_op jit(solution)/shard_map/reduce_sum | solution.py:25
  30.5 0.0 copy-start.8
  30.5 0.0 copy-start.9
  30.6 0.3 multiply_reduce_fusion.52
  30.9 0.4 copy-done.8
  31.2 0.0 copy-done.9
  31.3 1.2 add_convert_fusion
  32.5 34.0 %all-gather.2.cloned.1.call-done = bf16[1536,1536]{1,0:T(8,128)(2,1)} async-done(((bf16[96,1536]{1,0:T(8,128)(2,1)}), bf16[1536,1536]{1,0:T(8,128)(2,1)}) %all-gather.2.cloned.1.call-update) | async-done | bytes 4718608 | tf_op jit(solution)/shard_map/all_gather | solution.py:81
  66.5 0.0 copy-start.3
  66.5 9.2 %fusion.5 = (bf16[256,1536]{1,0:T(8,128)(2,1)S(1)}, f32[256,1536]{1,0:T(8,128)}, f32[256,1536]{1,0:T(8,128)}) fusion(bf16[1,16,16,1536]{3,2,1,0:T(8,128)(2,1)} %param.13, bf16[256,1536]{1,0:T(8,128)(2,1)} %bitcast.24, bf16[1536,1536]{1,0:T(8,128)(2,1)} %all-gather.2.cloned.1.call-done), kind=kOutput, calls=%fused_computation.57 | convolution fusion | flops 1236664320 | bytes 10223616 | tf_op jit(solution)/shard_map/dot_general | solution.py:82
  75.7 0.0 copy-start.6
  75.7 0.9 copy-done.6
  76.6 0.0 copy-done.3
  76.6 3.5 %convolution_convert_fusion = bf16[1536,1536]{1,0:T(8,128)(2,1)} fusion(bf16[256,1536]{1,0:T(8,128)(2,1)S(1)} %bitcast.25, bf16[256,1536]{1,0:T(8,128)(2,1)S(1)} %get-tuple-element.120), kind=kOutput, calls=%fused_computation.48 | convolution fusion | flops 1210318848 | bytes 6291456 | tf_op jit(solution)/shard_map/dot_general | solution.py:89
  80.1 0.0 reduce-scatter.2.cloned.1.call-update
  80.1 5.2 %fusion.13 = (f32[1536]{0:T(1024)S(1)}, f32[256]{0:T(256)S(1)}, f32[256,1536]{1,0:T(8,128)}) fusion(f32[1536]{0:T(1024)S(1)} %copy-done.8, bf16[256,1536]{1,0:T(8,128)(2,1)} %copy-done.6, bf16[1536,1536]{1,0:T(8,128)(2,1)} %all-gather.2.cloned.1.call-done), kind=kOutput, calls=%fused_computation.185 | convolution fusion | flops 1209137408 | bytes 7091200 | tf_op jit(solution)/shard_map/dot_general | solution.py:96
  85.3 0.1 div.17
  85.4 0.0 copy-start
  85.4 2.5 %multiply_reduce_fusion = (f32[1536]{0:T(1024)S(1)}, f32[16,16]{1,0:T(8,128)S(1)}) fusion(f32[1,16,16,1536]{3,2,0,1:T(8,128)S(1)} %get-tuple-element.123, f32[16,16]{1,0:T(8,128)S(1)} %add_rsqrt_fusion, f32[16,16]{1,0:T(8,128)S(1)} %broadcast_multiply_fusion.1, f32[256,1536]{1,0:T(8,128)} %get-tuple-element.125, f32[1,16,16,1536]{3,2,0,1:T(8,128)} %bitcast.23, ...), kind=kLoop, calls=%fused_computation.60 | loop fusion | flops 2750720 | bytes 4733952 | tf_op jit(solution)/shard_map/reduce_sum | solution.py:35
  88.0 0.0 copy-done
  88.0 4.9 %multiply_reduce_fusion.1 = (f32[1536]{0:T(1024)S(1)}, f32[1536]{0:T(1024)S(1)}, f32[1536]{0:T(1024)S(1)}, f32[1536]{0:T(1024)S(1)}, f32[1536]{0:T(1024)S(1)}, /...) fusion(f32[1,16,16,1536]{3,2,0,1:T(8,128)S(1)} %convert_element, ...), kind=kLoop, calls=%fused_computation.61 | loop fusion | flops 16880640 | bytes 6412288 | tf_op jit(solution)/shard_map/reduce_sum | solution.py:46
  92.9 0.0 copy-start.2
  92.9 3.9 %multiply_reduce_fusion.19 = (f32[1536]{0:T(1024)S(1)}, f32[1536]{0:T(1024)S(1)}, f32[1536]{0:T(1024)S(1)}, f32[1536]{0:T(1024)S(1)}, f32[1536]{0:T(1024)S(1)}, ...) fusion(f32[1,16,16,1536]{3,2,0,1:T(8,128)S(1)} %get-tuple-eleme, ...), kind=kLoop, calls=%fused_computation.79 | loop fusion | flops 14128128 | bytes 3256320 | tf_op jit(solution)/shard_map/reduce_sum | solution.py:46
  96.8 0.0 copy-done.2
  96.8 2.5 %fusion.14 = (f32[1536]{0:T(1024)S(1)}, f32[1536]{0:T(1024)S(1)}, f32[1536]{0:T(1024)S(1)}, f32[1536]{0:T(1024)S(1)}, f32[1536]{0:T(1024)S(1)}, /*index=5*/f32[1...) fusion(f32[1,16,16,1536]{3,2,0,1:T(8,128)S(1)} %get-tuple-eleme, ...), kind=kLoop, calls=%fused_computation.186 | loop fusion | flops 10988544 | bytes 4018176 | tf_op jit(solution)/shard_map/reduce_sum | solution.py:41
  100.0 0.0 copy-start.5
  100.0 0.5 concatenate.3
  100.6 0.0 copy-start.4
  100.6 1.3 all_to_all.14
  101.8 22.6 %all_to_all.21 = f32[64,1,1248]{2,1,0:T(1,128)S(1)} all-to-all(f32[64,1,1248]{2,1,0:T(1,128)} %all_to_all.14), channel_id=1, replica_groups=mesh['dp_hi'=2,'z'=12,'row'=2,'y'=8,'core'=2] {'dp_hi','row','y','core'}, dimensions={0} | all-to-all | bytes 638976 | tf_op jit(solution)/shard_map/all_to_all | solution.py:53
  124.5 0.2 reduce_sum.578
  124.7 19.2 %all_to_all.22 = f32[12,1,1248]{2,1,0:T(1,128)S(1)} all-to-all(f32[12,1,1248]{2,1,0:T(1,128)S(1)} %broadcast_in_dim.11), channel_id=1, replica_groups=mesh['dp_hi'=2,'z'=12,'row'=2,'y'=8,'core'=2] {'z'}, dimensions={0} | all-to-all | bytes 119808 | tf_op jit(solution)/shard_map/all_to_all | solution.py:59
  144.0 0.9 broadcast_in_dim.12
  144.9 7.9 %all-to-all-start.2 = ((f32[64,1,1248]{2,1,0:T(1,128)}), f32[64,1,1248]{2,1,0:T(1,128)S(1)}, u32[]{:S(2)}, u32[]{:S(2)}) async-start(f32[64,1,1248]{2,1,0:T(1,128)} %broadcast_in_dim.12), calls=%async_computation.3 | async-start | bytes 655360 | tf_op jit(solution)/shard_map/all_to_all | solution.py:59
  152.8 0.0 copy-done.5
  152.8 0.0 copy-done.4
  152.8 1.1 multiply_convert_fusion
  153.9 12.1 %all-to-all-done.2 = f32[64,1,1248]{2,1,0:T(1,128)S(1)} async-done(((f32[64,1,1248]{2,1,0:T(1,128)}), f32[64,1,1248]{2,1,0:T(1,128)S(1)}, u32[]{:S(2)}, u32[]{:S(2)}) %all-to-all-start.2) | async-done | bytes 319520 | tf_op jit(solution)/shard_map/all_to_all | solution.py:59
  166.0 0.8 reduce.56
  166.8 0.4 reshape_reshape.4
  167.2 0.6 slice.447
  167.8 0.8 reshape.262
  168.5 0.0 reduce-scatter.2.cloned.1.call-done
  168.5 1.8 %bitcast_convert_fusion = f32[1,96,1536]{2,1,0:T(8,128)} fusion(bf16[96,1536]{1,0:T(8,128)(2,1)} %reduce-scatter.2.cloned.1.call-done), kind=kLoop, calls=%fused_computation.131 | loop fusion | flops 147456 | bytes 884736 | tf_op jit(solution)/shard_map/broadcast_in_dim | solution.py:107
  (58 shorter events, 0.5 us)
Async XLA Ops:
  7.2 59.3 %all-gather.2.cloned.1.call-start = ((), (), s32[]{:S(2)}) async-start(), calls=%async_computation.4 | async-start | bytes 5013504 | tf_op jit(solution)/shard_map/all_gather | solution.py:81
  7.9 160.6 %reduce-scatter.2.cloned.1.call-start = ((), (), s32[]{:S(2)}) async-start(), calls=%async_computation.5 | async-start | bytes 5013504 | tf_op jit(solution)/shard_map/reduce_scatter | solution.py:88
  7.9 8.5 %copy-start.7 = (f32[7,7,1536]{2,1,0:T(8,128)S(1)}, f32[7,7,1536]{2,1,0:T(8,128)}, u32[]{:S(2)}) copy-start(f32[7,7,1536]{2,1,0:T(8,128)} %param.8) | copy-start | bytes 903172
  16.2 1.0 copy-start.1
  30.5 0.7 copy-start.8
  30.5 0.7 copy-start.9
  66.5 10.1 %copy-start.3 = (bf16[1,16,16,1536]{3,2,0,1:T(8,128)(2,1)S(1)}, bf16[1,16,16,1536]{3,2,0,1:T(8,128)(2,1)}, u32[]{:S(2)}) copy-start(bf16[1,16,16,1536]{3,2,0,1:T(8,128)(2,1)} %add_convert_fusion) | copy-start | bytes 2359300
  75.7 0.9 copy-start.6
  85.4 2.6 %copy-start = (f32[256,1536]{1,0:T(8,128)S(1)}, f32[256,1536]{1,0:T(8,128)}, u32[]{:S(2)}) copy-start(f32[256,1536]{1,0:T(8,128)} %get-tuple-element.125) | copy-start | bytes 4718596
  92.9 4.0 %copy-start.2 = (bf16[1,16,16,1536]{3,2,0,1:T(8,128)(2,1)S(1)}, bf16[1,16,16,1536]{3,2,0,1:T(8,128)(2,1)}, u32[]{:S(2)}) copy-start(bf16[1,16,16,1536]{3,2,0,1:T(8,128)(2,1)} %copy-done.1) | copy-start | bytes 2359300
  100.0 52.8 %copy-start.5 = (f32[256,1536]{1,0:T(8,128)S(1)}, f32[256,1536]{1,0:T(8,128)}, u32[]{:S(2)}) copy-start(f32[256,1536]{1,0:T(8,128)} %get-tuple-element.124) | copy-start | bytes 4718596
  100.6 52.2 %copy-start.4 = (f32[256,1536]{1,0:T(8,128)S(1)}, f32[256,1536]{1,0:T(8,128)}, u32[]{:S(2)}) copy-start(f32[256,1536]{1,0:T(8,128)} %get-tuple-element.121) | copy-start | bytes 4718596
  144.9 21.1 %all-to-all-start.2 = ((f32[64,1,1248]{2,1,0:T(1,128)}), f32[64,1,1248]{2,1,0:T(1,128)S(1)}, u32[]{:S(2)}, u32[]{:S(2)}) async-start(f32[64,1,1248]{2,1,0:T(1,128)} %broadcast_in_dim.12), calls=%async_computation.3 | async-start | bytes 655360 | tf_op jit(solution)/shard_map/all_to_all | solution.py:59
Sparse Core Ops, SparseCore 0:
  10.4 56.0 all-gather.1
  80.2 70.9 reduce-scatter.1

commit v7 on v6

--- a/solution.py
+++ b/solution.py
@@ -71,7 +71,14 @@
 
 
 def shards(images, kernel, conv_bias, ln_gain, ln_shift, w_up, cotangent):
-    full_maps = lax.all_gather(images, "row", axis=1, tiled=True)
+    rows = lax.axis_size("row")
+    others = lax.ppermute(images, "row", [(i, (i + 1) % rows) for i in range(rows)])
+    first = lax.axis_index("row") == 0
+    full_maps = jnp.where(
+        first,
+        jnp.concatenate([images, others], axis=1),
+        jnp.concatenate([others, images], axis=1),
+    )
     padded, unit_field, scale_inv, normed = conv_norm(
         full_maps, kernel, conv_bias, ln_gain, ln_shift
     )

time: 178 us -> 181 us (1.017)
  blocking collectives: 50.1 us -> 41.6 us
  local copies, waits for them, and re-layouts: 7.05 us -> 15 us
  waiting for transfers between devices: 46.8 us -> 42 us
  other arithmetic: 32.7 us -> 37.1 us
  starting transfers between devices: 7.93 us -> 12 us
    all_gather x1 -> x0, blocking collectives: 8.27 us -> none  [shards(): full_maps = lax.all_gather(images, 'row', axis=1, tiled=True)]
    slice x3, local copies, waits for them, and re-layouts: 0.82 us -> 6.69 us  [conv_norm(): kernel[tap_row, tap_col]]
    all_gather x1, waiting for transfers between devices: 34 us -> 29.2 us  [shards(): weights = lax.all_gather(w_up, FSDP, axis=0, tiled=True)]
    ppermute x0 -> x1, starting transfers between devices: none -> 3.95 us  [shards(): lax.ppermute(images, 'row', [(i, (i + 1) % rows) for i in range(rows)])]
    reduce_sum x1, other arithmetic: 13.2 us -> 15.2 us  [conv_norm(): centre = jnp.mean(conv_out, axis=-1, keepdims=True)]
  transfers between devices with their start and end apart: 3 -> 4, of which waited for: 2 -> 2; matrix products, arithmetic and copies ran while one was open for 23% -> 30% of each run, Pallas kernels for 0% -> 0%
where the time goes in v7:
time: 181 us; the launch traced here: 180 us
  waiting for transfers between devices  42 us (23%)
  blocking collectives  41.6 us (23%)
  other arithmetic  37.1 us (20%)
  matrix products  18 us (10%)
  local copies, waits for them, and re-layouts  15 us (8%)
  between operations  14.6 us (8%)
  starting transfers between devices  12 us (7%)
    all_gather x1, waiting for transfers between devices, shards(): weights = lax.all_gather(w_up, FSDP, axis=0, tiled=True)  29.2 us
    all_to_all x1, blocking collectives, exchange_sum(): lax.all_to_all(values.reshape(count, -1), axes, 0, 0, tiled=True).sum(0)  22.3 us
    all_to_all x1, blocking collectives, exchange_gather(): return lax.all_to_all(copies, axes, 0, 0, tiled=True).reshape(-1)  19.3 us
    reduce_sum x1, other arithmetic, conv_norm(): centre = jnp.mean(conv_out, axis=-1, keepdims=True)  15.2 us
    all_to_all x1, waiting for transfers between devices, exchange_gather(): return lax.all_to_all(copies, axes, 0, 0, tiled=True).reshape(-1)  12.1 us
    dot_general x1, matrix products, shards(): pre_act = jnp.dot(flat, weights, preferred_element_type=jnp.float32)  9.19 us
    reduce_sum x2, other arithmetic, norm_conv_grads(): tap_sums.append(jnp.sum(window * grad_conv, axis=(0, 1, 2)))  8.78 us
    all_to_all x1, starting transfers between devices, exchange_gather(): return lax.all_to_all(copies, axes, 0, 0, tiled=True).reshape(-1)  7.99 us
  transfers between devices with their start and end apart: 4, of which 2 were waited for; matrix products, arithmetic and copies ran while one was open for 30% of the time, Pallas kernels for 0%

profile of v7, /device:TPU:1, one launch (start us, length us, event | category | flops | bytes accessed | tf_op | source)
XLA Modules:
  0.0 180.3 jit_solution(2565992335653837518)
XLA Ops:
  7.2 0.0 all-gather.2.cloned.1.call-start
  7.2 0.7 all-gather.2.cloned.1.call-update
  7.9 0.0 reduce-scatter.2.cloned.1.call-start
  7.9 4.0 %collective-permute-start = (bf16[1,8,16,1536]{3,2,1,0:T(8,128)(2,1)}, bf16[1,8,16,1536]{3,2,1,0:T(8,128)(2,1)S(1)}, u32[]{:S(2)}, u32[]{:S(2)}) collective-permute-start(bf16[1,8,16,1536]{3,2,1,0:T(8,128)(2,1)} %param.7), channel_id=1, source_target_pairs={{0,16},{16,0},{1,17},{17,1},{2,18},{18,2},{3,19},{19,3},{4,20},{20... | collective-permute-start | bytes 1179656 | tf_op jit(solution)/shard_map/ppermute | solution.py:75
  11.9 1.9 %slice_reduce_fusion.46 = (f32[1536]{0:T(1024)S(1)}, f32[1536]{0:T(1024)S(1)}, f32[1536]{0:T(1024)}, f32[1536]{0:T(1024)}, f32[1536]{0:T(1024)}, /*index=5*/f32[...) fusion(f32[7,7,1536]{2,1,0:T(8,128)} %param.8), kind=kLoop, calls=%fused_computation.181 | loop fusion | bytes 135168 | tf_op jit(solution)/shard_map/slice | solution.py:23
  13.8 2.5 %slice_reduce_fusion.48 = (f32[1536]{0:T(1024)}, f32[1536]{0:T(1024)}, f32[1536]{0:T(1024)}, f32[1536]{0:T(1024)}, f32[1536]{0:T(1024)}, /*index=5*/f32[1536]{0:...) fusion(f32[7,7,1536]{2,1,0:T(8,128)} %param.8), kind=kLoop, calls=%fused_computation.183 | loop fusion | bytes 233472 | tf_op jit(solution)/shard_map/slice | solution.py:23
  16.3 2.3 %slice_reduce_fusion.47 = (f32[1536]{0:T(1024)}, f32[1536]{0:T(1024)}, f32[1536]{0:T(1024)}, f32[1536]{0:T(1024)}, f32[1536]{0:T(1024)}, /*index=5*/f32[1536]{0:...) fusion(f32[7,7,1536]{2,1,0:T(8,128)} %param.8), kind=kLoop, calls=%fused_computation.182 | loop fusion | bytes 233472 | tf_op jit(solution)/shard_map/slice | solution.py:23
  18.6 0.0 collective-permute-done
  18.6 1.3 fusion.13
  19.9 15.2 %fusion.17 = (f32[16,16]{1,0:T(8,128)}, f32[1,16,16,1536]{3,2,1,0:T(8,128)S(1)}) fusion(f32[1536]{0:T(1024)} %get-tuple-element.117, f32[1536]{0:T(1024)} %get-tuple-element.118, f32[1536]{0:T(1024)} %get-tuple-element.71, f32[1536]{0:T(1024)} %get-tuple-element.72, f32[1536]{0:T(1024)} %get-tuple-element.73, f32[1536]{0:T(1024)} %get-tuple-element.74, ...), kind=kLoop, calls=%fused_computation.189 | loop fusion | flops 38928128 | bytes 3453952 | tf_op jit(solution)/shard_map/reduce_sum | solution.py:25
  35.0 0.0 copy-start.6
  35.0 0.0 copy-start.11
  35.0 0.7 broadcast_multiply_fusion.1
  35.8 0.3 multiply_reduce_fusion.52
  36.1 0.0 copy-done.6
  36.1 0.0 copy-done.11
  36.1 1.2 add_convert_fusion
  37.3 29.2 %all-gather.2.cloned.1.call-done = bf16[1536,1536]{1,0:T(8,128)(2,1)} async-done(((bf16[96,1536]{1,0:T(8,128)(2,1)}), bf16[1536,1536]{1,0:T(8,128)(2,1)}) %all-gather.2.cloned.1.call-update) | async-done | bytes 4718608 | tf_op jit(solution)/shard_map/all_gather | solution.py:88
  66.6 0.0 copy-start.1
  66.6 9.2 %fusion.5 = (bf16[256,1536]{1,0:T(8,128)(2,1)S(1)}, f32[256,1536]{1,0:T(8,128)}, f32[256,1536]{1,0:T(8,128)}) fusion(bf16[1,16,16,1536]{3,2,1,0:T(8,128)(2,1)} %param.13, bf16[256,1536]{1,0:T(8,128)(2,1)} %bitcast.20, bf16[1536,1536]{1,0:T(8,128)(2,1)} %all-gather.2.cloned.1.call-done), kind=kOutput, calls=%fused_computation.57 | convolution fusion | flops 1236664320 | bytes 10223616 | tf_op jit(solution)/shard_map/dot_general | solution.py:89
  75.8 0.0 copy-start.5
  75.8 0.9 copy-done.5
  76.6 0.0 copy-done.1
  76.6 3.6 %convolution_convert_fusion = bf16[1536,1536]{1,0:T(8,128)(2,1)} fusion(bf16[256,1536]{1,0:T(8,128)(2,1)S(1)} %bitcast.21, bf16[256,1536]{1,0:T(8,128)(2,1)S(1)} %get-tuple-element.120), kind=kOutput, calls=%fused_computation.48 | convolution fusion | flops 1210318848 | bytes 6291456 | tf_op jit(solution)/shard_map/dot_general | solution.py:96
  80.2 0.0 reduce-scatter.2.cloned.1.call-update
  80.2 5.2 %fusion.14 = (f32[1536]{0:T(1024)S(1)}, f32[256]{0:T(256)S(1)}, f32[256,1536]{1,0:T(8,128)}) fusion(f32[1536]{0:T(1024)} %param.10, bf16[256,1536]{1,0:T(8,128)(2,1)} %copy-done.5, bf16[1536,1536]{1,0:T(8,128)(2,1)} %all-gather.2.cloned.1.call-done), kind=kOutput, calls=%fused_computation.187 | convolution fusion | flops 1209137408 | bytes 7091200 | tf_op jit(solution)/shard_map/dot_general | solution.py:103
  85.4 0.6 stack.207
  86.0 0.6 broadcast_multiply_fusion.2
  86.6 1.4 div.17
  87.9 0.0 copy-start
  87.9 0.0 copy-start.7
  87.9 0.0 copy-start.8
  87.9 2.5 %multiply_reduce_fusion = (f32[1536]{0:T(1024)S(1)}, f32[16,16]{1,0:T(8,128)S(1)}) fusion(f32[1,16,16,1536]{3,2,1,0:T(8,128)S(1)} %get-tuple-element.123, f32[16,16]{1,0:T(8,128)S(1)} %add_rsqrt_fusion, f32[16,16]{1,0:T(8,128)S(1)} %broadcast_multiply_fusion.1, f32[256,1536]{1,0:T(8,128)} %get-tuple-element.125, f32[1,16,16,1536]{3,2,1,0:T(8,128)} %bitcast.19, ...), kind=kLoop, calls=%fused_computation.60 | loop fusion | flops 2750720 | bytes 4733952 | tf_op jit(solution)/shard_map/reduce_sum | solution.py:35
  90.5 0.6 stack.206
  91.1 0.0 copy-done
  91.1 0.0 copy-done.7
  91.1 0.0 copy-done.8
  91.1 4.9 %multiply_reduce_fusion.1 = (f32[1536]{0:T(1024)S(1)}, f32[1536]{0:T(1024)S(1)}, f32[1536]{0:T(1024)S(1)}, f32[1536]{0:T(1024)S(1)}, f32[1536]{0:T(1024)S(1)}, /...) fusion(f32[1,16,16,1536]{3,2,1,0:T(8,128)S(1)} %fusion.13, ...), kind=kLoop, calls=%fused_computation.61 | loop fusion | flops 16880640 | bytes 6412288 | tf_op jit(solution)/shard_map/reduce_sum | solution.py:46
  96.0 0.0 copy-start.2
  96.0 3.9 %multiply_reduce_fusion.19 = (f32[1536]{0:T(1024)S(1)}, f32[1536]{0:T(1024)S(1)}, f32[1536]{0:T(1024)S(1)}, f32[1536]{0:T(1024)S(1)}, f32[1536]{0:T(1024)S(1)}, ...) fusion(f32[1,16,16,1536]{3,2,1,0:T(8,128)S(1)} %get-tuple-eleme, ...), kind=kLoop, calls=%fused_computation.79 | loop fusion | flops 14128128 | bytes 3256320 | tf_op jit(solution)/shard_map/reduce_sum | solution.py:46
  99.9 0.0 copy-done.2
  99.9 0.0 copy-start.9
  99.9 0.0 copy-start.10
  100.0 2.6 %fusion.15 = (f32[1536]{0:T(1024)S(1)}, f32[1536]{0:T(1024)S(1)}, f32[1536]{0:T(1024)S(1)}, f32[1536]{0:T(1024)S(1)}, f32[1536]{0:T(1024)S(1)}, /*index=5*/f32[1...) fusion(f32[1,16,16,1536]{3,2,1,0:T(8,128)S(1)} %get-tuple-eleme, ...), kind=kLoop, calls=%fused_computation.188 | loop fusion | flops 12168192 | bytes 4018177 | tf_op jit(solution)/shard_map/reduce_sum | solution.py:41
  103.2 0.0 copy-done.9
  103.2 0.0 copy-done.10
  103.3 0.0 copy-start.4
  103.3 0.5 concatenate.35
  103.8 0.0 copy-start.3
  103.8 1.3 all_to_all.14
  105.1 22.3 %all_to_all.21 = f32[64,1,1248]{2,1,0:T(1,128)S(1)} all-to-all(f32[64,1,1248]{2,1,0:T(1,128)} %all_to_all.14), channel_id=1, replica_groups=mesh['dp_hi'=2,'z'=12,'row'=2,'y'=8,'core'=2] {'dp_hi','row','y','core'}, dimensions={0} | all-to-all | bytes 638976 | tf_op jit(solution)/shard_map/all_to_all | solution.py:53
  127.4 0.2 reduce_sum.578
  127.7 19.3 %all_to_all.22 = f32[12,1,1248]{2,1,0:T(1,128)S(1)} all-to-all(f32[12,1,1248]{2,1,0:T(1,128)S(1)} %broadcast_in_dim.11), channel_id=1, replica_groups=mesh['dp_hi'=2,'z'=12,'row'=2,'y'=8,'core'=2] {'z'}, dimensions={0} | all-to-all | bytes 119808 | tf_op jit(solution)/shard_map/all_to_all | solution.py:59
  147.0 0.9 broadcast_in_dim.12
  147.9 8.0 %all-to-all-start.2 = ((f32[64,1,1248]{2,1,0:T(1,128)}), f32[64,1,1248]{2,1,0:T(1,128)S(1)}, u32[]{:S(2)}, u32[]{:S(2)}) async-start(f32[64,1,1248]{2,1,0:T(1,128)} %broadcast_in_dim.12), calls=%async_computation.3 | async-start | bytes 655360 | tf_op jit(solution)/shard_map/all_to_all | solution.py:59
  155.9 0.0 copy-done.4
  155.9 0.0 copy-done.3
  155.9 1.1 multiply_convert_fusion
  157.1 12.1 %all-to-all-done.2 = f32[64,1,1248]{2,1,0:T(1,128)S(1)} async-done(((f32[64,1,1248]{2,1,0:T(1,128)}), f32[64,1,1248]{2,1,0:T(1,128)S(1)}, u32[]{:S(2)}, u32[]{:S(2)}) %all-to-all-start.2) | async-done | bytes 319520 | tf_op jit(solution)/shard_map/all_to_all | solution.py:59
  169.1 0.8 reduce.56
  169.9 0.4 reshape_reshape.4
  170.3 0.6 slice.447
  170.9 0.8 reshape.354
  171.7 1.8 %bitcast_convert_fusion = f32[1,96,1536]{2,1,0:T(8,128)} fusion(bf16[96,1536]{1,0:T(8,128)(2,1)} %reduce-scatter.2.cloned.1.call-done), kind=kLoop, calls=%fused_computation.133 | loop fusion | flops 147456 | bytes 884736 | tf_op jit(solution)/shard_map/broadcast_in_dim | solution.py:114
  (55 shorter events, 0.4 us)
Async XLA Ops:
  7.2 59.4 %all-gather.2.cloned.1.call-start = ((), (), s32[]{:S(2)}) async-start(), calls=%async_computation.4 | async-start | bytes 5013504 | tf_op jit(solution)/shard_map/all_gather | solution.py:88
  7.9 163.8 %reduce-scatter.2.cloned.1.call-start = ((), (), s32[]{:S(2)}) async-start(), calls=%async_computation.5 | async-start | bytes 5013504 | tf_op jit(solution)/shard_map/reduce_scatter | solution.py:95
  7.9 10.7 %collective-permute-start = (bf16[1,8,16,1536]{3,2,1,0:T(8,128)(2,1)}, bf16[1,8,16,1536]{3,2,1,0:T(8,128)(2,1)S(1)}, u32[]{:S(2)}, u32[]{:S(2)}) collective-permute-start(bf16[1,8,16,1536]{3,2,1,0:T(8,128)(2,1)} %param.7), channel_id=1, source_target_pairs={{0,16},{16,0},{1,17},{17,1},{2,18},{18,2},{3,19},{19,3},{4,20},{20... | collective-permute-start | bytes 1179656 | tf_op jit(solution)/shard_map/ppermute | solution.py:75
  35.0 1.0 copy-start.6
  35.0 1.0 copy-start.11
  66.6 10.1 %copy-start.1 = (bf16[1,16,16,1536]{3,2,1,0:T(8,128)(2,1)S(1)}, bf16[1,16,16,1536]{3,2,1,0:T(8,128)(2,1)}, u32[]{:S(2)}) copy-start(bf16[1,16,16,1536]{3,2,1,0:T(8,128)(2,1)} %add_convert_fusion) | copy-start | bytes 2359300
  75.8 0.9 copy-start.5
  87.9 3.1 %copy-start = (f32[256,1536]{1,0:T(8,128)S(1)}, f32[256,1536]{1,0:T(8,128)}, u32[]{:S(2)}) copy-start(f32[256,1536]{1,0:T(8,128)} %get-tuple-element.125) | copy-start | bytes 4718596
  87.9 3.1 %copy-start.7 = (f32[1536]{0:T(1024)S(1)}, f32[1536]{0:T(1024)}, u32[]{:S(2)}) copy-start(f32[1536]{0:T(1024)} %param.10) | copy-start | bytes 18436
  87.9 3.2 %copy-start.8 = (f32[16,16]{1,0:T(8,128)S(1)}, f32[16,16]{1,0:T(8,128)}, u32[]{:S(2)}) copy-start(f32[16,16]{1,0:T(8,128)} %div.17) | copy-start | bytes 3076
  96.0 4.0 %copy-start.2 = (bf16[1,8,16,1536]{3,2,1,0:T(8,128)(2,1)S(1)}, bf16[1,8,16,1536]{3,2,1,0:T(8,128)(2,1)}, u32[]{:S(2)}) copy-start(bf16[1,8,16,1536]{3,2,1,0:T(8,128)(2,1)} %param.7) | copy-start | bytes 1179652
  99.9 3.3 %copy-start.9 = (f32[1,1536]{1,0:T(1,128)S(1)}, f32[1,1536]{1,0:T(1,128)}, u32[]{:S(2)}) copy-start(f32[1,1536]{1,0:T(1,128)} %stack.207) | copy-start | bytes 18436
  99.9 3.3 %copy-start.10 = (f32[1,1536]{1,0:T(1,128)S(1)}, f32[1,1536]{1,0:T(1,128)}, u32[]{:S(2)}) copy-start(f32[1,1536]{1,0:T(1,128)} %stack.206) | copy-start | bytes 18436
  103.3 52.6 %copy-start.4 = (f32[256,1536]{1,0:T(8,128)S(1)}, f32[256,1536]{1,0:T(8,128)}, u32[]{:S(2)}) copy-start(f32[256,1536]{1,0:T(8,128)} %get-tuple-element.124) | copy-start | bytes 4718596
  103.8 52.1 %copy-start.3 = (f32[256,1536]{1,0:T(8,128)S(1)}, f32[256,1536]{1,0:T(8,128)}, u32[]{:S(2)}) copy-start(f32[256,1536]{1,0:T(8,128)} %get-tuple-element.121) | copy-start | bytes 4718596
  147.9 21.3 %all-to-all-start.2 = ((f32[64,1,1248]{2,1,0:T(1,128)}), f32[64,1,1248]{2,1,0:T(1,128)S(1)}, u32[]{:S(2)}, u32[]{:S(2)}) async-start(f32[64,1,1248]{2,1,0:T(1,128)} %broadcast_in_dim.12), calls=%async_computation.3 | async-start | bytes 655360 | tf_op jit(solution)/shard_map/all_to_all | solution.py:59
Sparse Core Ops, SparseCore 0:
  10.4 56.1 all-gather.1
  80.4 70.8 reduce-scatter.1

commit v8 on v6

--- a/solution.py
+++ b/solution.py
@@ -100,10 +100,13 @@
         padded, unit_field, scale_inv, grad_normed.reshape(unit_field.shape), ln_gain
     )
     taps = kernel_part.shape[0] * kernel_part.shape[1]
-    packed = jnp.concatenate([kernel_part.reshape(taps, channels), vector_part], axis=0)
+    shards_of = lax.axis_size(("dp_hi", "row") + FSDP)
+    spare = -(taps + vector_part.shape[0]) % shards_of
+    padding = jnp.zeros((spare, channels), jnp.float32)
+    packed = jnp.concatenate([kernel_part.reshape(taps, channels), vector_part, padding], axis=0)
     packed = packed_sum(packed.reshape(-1)).reshape(packed.shape)
     grad_kernel = packed[:taps].reshape(kernel_part.shape)
-    grad_vectors = packed[taps:]
+    grad_vectors = packed[taps : taps + vector_part.shape[0]]
     return (hidden.reshape(cotangent.shape), grad_weight[None], grad_kernel, grad_vectors)
 
 

time: 178 us -> 180 us (1.011)
  no operation moved by 1% of the time
where the time goes in v8:
time: 180 us; the launch traced here: 179 us
  blocking collectives  51.5 us (29%)
  waiting for transfers between devices  48.1 us (27%)
  other arithmetic  32 us (18%)
  matrix products  17.9 us (10%)
  between operations  14.7 us (8%)
  starting transfers between devices  8.27 us (5%)
  local copies, waits for them, and re-layouts  6.68 us (4%)
    all_gather x1, waiting for transfers between devices, shards(): weights = lax.all_gather(w_up, FSDP, axis=0, tiled=True)  34 us
    all_to_all x1, blocking collectives, exchange_sum(): lax.all_to_all(values.reshape(count, -1), axes, 0, 0, tiled=True).sum(0)  24 us
    all_to_all x1, blocking collectives, exchange_gather(): return lax.all_to_all(copies, axes, 0, 0, tiled=True).reshape(-1)  19.2 us
    all_to_all x1, waiting for transfers between devices, exchange_gather(): return lax.all_to_all(copies, axes, 0, 0, tiled=True).reshape(-1)  13.4 us
    reduce_sum x1, other arithmetic, conv_norm(): centre = jnp.mean(conv_out, axis=-1, keepdims=True)  13.2 us
    dot_general x1, matrix products, shards(): pre_act = jnp.dot(flat, weights, preferred_element_type=jnp.float32)  9.2 us
    reduce_sum x2, other arithmetic, norm_conv_grads(): tap_sums.append(jnp.sum(window * grad_conv, axis=(0, 1, 2)))  8.79 us
    all_gather x1, blocking collectives, shards(): full_maps = lax.all_gather(images, 'row', axis=1, tiled=True)  8.27 us
  transfers between devices with their start and end apart: 3, of which 2 were waited for; matrix products, arithmetic and copies ran while one was open for 23% of the time, Pallas kernels for 0%

profile of v8, /device:TPU:1, one launch (start us, length us, event | category | flops | bytes accessed | tf_op | source)
XLA Modules:
  0.0 179.2 jit_solution(12449761319557272076)
XLA Ops:
  7.2 0.0 all-gather.2.cloned.1.call-start
  7.2 0.7 all-gather.2.cloned.1.call-update
  7.9 0.0 reduce-scatter.2.cloned.1.call-start
  7.9 0.0 copy-start.7
  8.0 8.3 %all_gather.6 = bf16[1,16,16,1536]{3,2,0,1:T(8,128)(2,1)S(1)} all-gather(bf16[1,8,16,1536]{3,2,0,1:T(8,128)(2,1)} %bitcast.29), channel_id=1, replica_groups=mesh['dp_hi'=2,'z'=12,'row'=2,'y'=8,'core'=2] {'row'}, dimensions={1}, use_global_device_ids=true | all-gather | bytes 1179648 | tf_op jit(solution)/shard_map/all_gather | solution.py:74
  16.2 0.0 copy-start.1
  16.2 0.2 convert_element_type.24
  16.4 0.0 copy-done.7
  16.4 0.2 slice_reduce_fusion.47
  16.6 0.3 slice_reduce_fusion.49
  16.9 0.3 slice_reduce_fusion.48
  17.3 0.0 copy-done.1
  17.3 13.2 %fusion.16 = (f32[16,16]{1,0:T(8,128)S(1)}, f32[1,16,16,1536]{3,2,0,1:T(8,128)S(1)}) fusion(f32[1536]{0:T(1024)S(1)} %get-tuple-element.117, f32[1536]{0:T(1024)S(1)} %get-tuple-element.118, f32[1536]{0:T(1024)S(1)} %get-tuple-element.71, f32[1536]{0:T(1024)S(1)} %get-tuple-element.72, f32[1536]{0:T(1024)S(1)} %get-tuple-element.73, ...), kind=kLoop, calls=%fused_computation.189 | loop fusion | flops 38928128 | bytes 3453952 | tf_op jit(solution)/shard_map/reduce_sum | solution.py:25
  30.5 0.0 copy-start.8
  30.5 0.0 copy-start.9
  30.6 0.3 multiply_reduce_fusion.52
  30.9 0.4 copy-done.8
  31.2 0.0 copy-done.9
  31.3 1.2 add_convert_fusion
  32.5 34.0 %all-gather.2.cloned.1.call-done = bf16[1536,1536]{1,0:T(8,128)(2,1)} async-done(((bf16[96,1536]{1,0:T(8,128)(2,1)}), bf16[1536,1536]{1,0:T(8,128)(2,1)}) %all-gather.2.cloned.1.call-update) | async-done | bytes 4718608 | tf_op jit(solution)/shard_map/all_gather | solution.py:81
  66.5 0.0 copy-start.3
  66.5 9.2 %fusion.5 = (bf16[256,1536]{1,0:T(8,128)(2,1)S(1)}, f32[256,1536]{1,0:T(8,128)}, f32[256,1536]{1,0:T(8,128)}) fusion(bf16[1,16,16,1536]{3,2,1,0:T(8,128)(2,1)} %param.13, bf16[256,1536]{1,0:T(8,128)(2,1)} %bitcast.26, bf16[1536,1536]{1,0:T(8,128)(2,1)} %all-gather.2.cloned.1.call-done), kind=kOutput, calls=%fused_computation.57 | convolution fusion | flops 1236664320 | bytes 10223616 | tf_op jit(solution)/shard_map/dot_general | solution.py:82
  75.7 0.0 copy-start.6
  75.7 0.9 copy-done.6
  76.6 0.0 copy-done.3
  76.6 3.5 %convolution_convert_fusion = bf16[1536,1536]{1,0:T(8,128)(2,1)} fusion(bf16[256,1536]{1,0:T(8,128)(2,1)S(1)} %bitcast.27, bf16[256,1536]{1,0:T(8,128)(2,1)S(1)} %get-tuple-element.120), kind=kOutput, calls=%fused_computation.48 | convolution fusion | flops 1210318848 | bytes 6291456 | tf_op jit(solution)/shard_map/dot_general | solution.py:89
  80.1 0.0 reduce-scatter.2.cloned.1.call-update
  80.1 5.2 %fusion.13 = (f32[1536]{0:T(1024)S(1)}, f32[256]{0:T(256)S(1)}, f32[256,1536]{1,0:T(8,128)}) fusion(f32[1536]{0:T(1024)S(1)} %copy-done.8, bf16[256,1536]{1,0:T(8,128)(2,1)} %copy-done.6, bf16[1536,1536]{1,0:T(8,128)(2,1)} %all-gather.2.cloned.1.call-done), kind=kOutput, calls=%fused_computation.187 | convolution fusion | flops 1209137408 | bytes 7091200 | tf_op jit(solution)/shard_map/dot_general | solution.py:96
  85.4 0.1 div.17
  85.4 0.0 copy-start
  85.4 2.5 %multiply_reduce_fusion = (f32[1536]{0:T(1024)S(1)}, f32[16,16]{1,0:T(8,128)S(1)}) fusion(f32[1,16,16,1536]{3,2,0,1:T(8,128)S(1)} %get-tuple-element.123, f32[16,16]{1,0:T(8,128)S(1)} %add_rsqrt_fusion, f32[16,16]{1,0:T(8,128)S(1)} %broadcast_multiply_fusion.1, f32[256,1536]{1,0:T(8,128)} %get-tuple-element.125, f32[1,16,16,1536]{3,2,0,1:T(8,128)} %bitcast.25, ...), kind=kLoop, calls=%fused_computation.60 | loop fusion | flops 2750720 | bytes 4733952 | tf_op jit(solution)/shard_map/reduce_sum | solution.py:35
  88.0 0.0 copy-done
  88.0 4.9 %multiply_reduce_fusion.1 = (f32[1536]{0:T(1024)S(1)}, f32[1536]{0:T(1024)S(1)}, f32[1536]{0:T(1024)S(1)}, f32[1536]{0:T(1024)S(1)}, f32[1536]{0:T(1024)S(1)}, /...) fusion(f32[1,16,16,1536]{3,2,0,1:T(8,128)S(1)} %convert_element, ...), kind=kLoop, calls=%fused_computation.61 | loop fusion | flops 16880640 | bytes 6412288 | tf_op jit(solution)/shard_map/reduce_sum | solution.py:46
  92.9 0.0 copy-start.2
  92.9 3.9 %multiply_reduce_fusion.19 = (f32[1536]{0:T(1024)S(1)}, f32[1536]{0:T(1024)S(1)}, f32[1536]{0:T(1024)S(1)}, f32[1536]{0:T(1024)S(1)}, f32[1536]{0:T(1024)S(1)}, ...) fusion(f32[1,16,16,1536]{3,2,0,1:T(8,128)S(1)} %get-tuple-eleme, ...), kind=kLoop, calls=%fused_computation.79 | loop fusion | flops 14128128 | bytes 3256320 | tf_op jit(solution)/shard_map/reduce_sum | solution.py:46
  97.1 0.0 copy-done.2
  97.1 2.5 %fusion.14 = (f32[1536]{0:T(1024)S(1)}, f32[1536]{0:T(1024)S(1)}, f32[1536]{0:T(1024)S(1)}, f32[1536]{0:T(1024)S(1)}, f32[1536]{0:T(1024)S(1)}, /*index=5*/f32[1...) fusion(f32[1,16,16,1536]{3,2,0,1:T(8,128)S(1)} %get-tuple-eleme, ...), kind=kLoop, calls=%fused_computation.188 | loop fusion | flops 10988544 | bytes 4018176 | tf_op jit(solution)/shard_map/reduce_sum | solution.py:41
  100.0 0.7 concatenate.3
  100.7 0.0 copy-start.4
  100.8 0.0 copy-start.5
  100.8 0.3 all_to_all.14
  101.0 24.0 %all_to_all.21 = f32[64,1,1536]{2,1,0:T(1,128)S(1)} all-to-all(f32[64,1,1536]{2,1,0:T(1,128)S(1)} %all_to_all.14), channel_id=1, replica_groups=mesh['dp_hi'=2,'z'=12,'row'=2,'y'=8,'core'=2] {'dp_hi','row','y','core'}, dimensions={0} | all-to-all | bytes 786432 | tf_op jit(solution)/shard_map/all_to_all | solution.py:53
  125.0 0.2 reduce_sum.578
  125.3 19.2 %all_to_all.22 = f32[12,1,1536]{2,1,0:T(1,128)S(1)} all-to-all(f32[12,1,1536]{2,1,0:T(1,128)S(1)} %broadcast_in_dim.14), channel_id=1, replica_groups=mesh['dp_hi'=2,'z'=12,'row'=2,'y'=8,'core'=2] {'z'}, dimensions={0} | all-to-all | bytes 147456 | tf_op jit(solution)/shard_map/all_to_all | solution.py:59
  144.5 0.1 reduce_sum.579
  144.6 0.9 broadcast_in_dim.15
  145.5 8.2 %all-to-all-start.2 = ((f32[64,1,1536]{2,1,0:T(1,128)}), f32[64,1,1536]{2,1,0:T(1,128)S(1)}, u32[]{:S(2)}, u32[]{:S(2)}) async-start(f32[64,1,1536]{2,1,0:T(1,128)} %broadcast_in_dim.15), calls=%async_computation.3 | async-start | bytes 786432 | tf_op jit(solution)/shard_map/all_to_all | solution.py:59
  153.7 0.0 copy-done.4
  153.8 0.0 copy-done.5
  153.8 1.1 multiply_convert_fusion
  154.9 13.4 %all-to-all-done.2 = f32[64,1,1536]{2,1,0:T(1,128)S(1)} async-done(((f32[64,1,1536]{2,1,0:T(1,128)}), f32[64,1,1536]{2,1,0:T(1,128)S(1)}, u32[]{:S(2)}, u32[]{:S(2)}) %all-to-all-start.2) | async-done | bytes 393248 | tf_op jit(solution)/shard_map/all_to_all | solution.py:59
  168.4 0.8 slice_reduce_fusion
  169.1 0.8 reshape.263
  169.9 0.6 copy.20
  170.5 0.0 reduce-scatter.2.cloned.1.call-done
  170.5 1.8 %bitcast_convert_fusion = f32[1,96,1536]{2,1,0:T(8,128)} fusion(bf16[96,1536]{1,0:T(8,128)(2,1)} %reduce-scatter.2.cloned.1.call-done), kind=kLoop, calls=%fused_computation.132 | loop fusion | flops 147456 | bytes 884736 | tf_op jit(solution)/shard_map/broadcast_in_dim | solution.py:110
  (59 shorter events, 0.4 us)
Async XLA Ops:
  7.2 59.3 %all-gather.2.cloned.1.call-start = ((), (), s32[]{:S(2)}) async-start(), calls=%async_computation.4 | async-start | bytes 5013504 | tf_op jit(solution)/shard_map/all_gather | solution.py:81
  7.9 162.6 %reduce-scatter.2.cloned.1.call-start = ((), (), s32[]{:S(2)}) async-start(), calls=%async_computation.5 | async-start | bytes 5013504 | tf_op jit(solution)/shard_map/reduce_scatter | solution.py:88
  7.9 8.5 %copy-start.7 = (f32[7,7,1536]{2,1,0:T(8,128)S(1)}, f32[7,7,1536]{2,1,0:T(8,128)}, u32[]{:S(2)}) copy-start(f32[7,7,1536]{2,1,0:T(8,128)} %param.8) | copy-start | bytes 903172
  16.2 1.0 copy-start.1
  30.5 0.7 copy-start.8
  30.5 0.7 copy-start.9
  66.5 10.1 %copy-start.3 = (bf16[1,16,16,1536]{3,2,0,1:T(8,128)(2,1)S(1)}, bf16[1,16,16,1536]{3,2,0,1:T(8,128)(2,1)}, u32[]{:S(2)}) copy-start(bf16[1,16,16,1536]{3,2,0,1:T(8,128)(2,1)} %add_convert_fusion) | copy-start | bytes 2359300
  75.7 0.9 copy-start.6
  85.4 2.5 %copy-start = (f32[256,1536]{1,0:T(8,128)S(1)}, f32[256,1536]{1,0:T(8,128)}, u32[]{:S(2)}) copy-start(f32[256,1536]{1,0:T(8,128)} %get-tuple-element.125) | copy-start | bytes 4718596
  92.9 4.2 %copy-start.2 = (bf16[1,16,16,1536]{3,2,0,1:T(8,128)(2,1)S(1)}, bf16[1,16,16,1536]{3,2,0,1:T(8,128)(2,1)}, u32[]{:S(2)}) copy-start(bf16[1,16,16,1536]{3,2,0,1:T(8,128)(2,1)} %copy-done.1) | copy-start | bytes 2359300
  100.7 53.0 %copy-start.4 = (f32[256,1536]{1,0:T(8,128)S(1)}, f32[256,1536]{1,0:T(8,128)}, u32[]{:S(2)}) copy-start(f32[256,1536]{1,0:T(8,128)} %get-tuple-element.121) | copy-start | bytes 4718596
  100.8 53.0 %copy-start.5 = (f32[256,1536]{1,0:T(8,128)S(1)}, f32[256,1536]{1,0:T(8,128)}, u32[]{:S(2)}) copy-start(f32[256,1536]{1,0:T(8,128)} %get-tuple-element.124) | copy-start | bytes 4718596
  145.5 22.8 %all-to-all-start.2 = ((f32[64,1,1536]{2,1,0:T(1,128)}), f32[64,1,1536]{2,1,0:T(1,128)S(1)}, u32[]{:S(2)}, u32[]{:S(2)}) async-start(f32[64,1,1536]{2,1,0:T(1,128)} %broadcast_in_dim.15), calls=%async_computation.3 | async-start | bytes 786432 | tf_op jit(solution)/shard_map/all_to_all | solution.py:59
Sparse Core Ops, SparseCore 0:
  10.4 56.0 all-gather.1
  80.3 72.0 reduce-scatter.1

commit v9 on v6

--- a/solution.py
+++ b/solution.py
@@ -60,10 +60,19 @@
 
 
 def packed_sum(values):
-    inner, outer = ("dp_hi", "row") + FSDP, "z"
+    cores = lax.axis_size("core")
+    bit = lax.axis_index("core") % 2
+    swap = [(i, i ^ 1) for i in range(cores)]
+    half = values.shape[0] // 2
+    keep = lax.dynamic_slice_in_dim(values, bit * half, half)
+    send = lax.dynamic_slice_in_dim(values, (1 - bit) * half, half)
+    values = keep + lax.ppermute(send, "core", swap)
+    inner, outer = ("dp_hi", "row", "y"), "z"
     values = exchange_sum(values, inner)
     values = exchange_gather(values, outer).reshape(lax.axis_size(outer), -1).sum(0)
-    return exchange_gather(values, inner)
+    values = exchange_gather(values, inner)
+    other = lax.ppermute(values, "core", swap)
+    return jnp.where(bit == 0, jnp.concatenate([values, other]), jnp.concatenate([other, values]))
 
 
 DP = ("dp_hi", "z")

time: 178 us -> 180 us (1.011)
  blocking collectives: 50.1 us -> 43.9 us
  starting transfers between devices: 7.93 us -> 14.1 us
  other arithmetic: 32.7 us -> 35.5 us
    ppermute x0 -> x2, starting transfers between devices: none -> 8.62 us  [the longest x1 6.34 us: packed_sum(): other = lax.ppermute(values, 'core', swap)]
    all_to_all x1, blocking collectives: 22.6 us -> 16.4 us  [exchange_sum(): lax.all_to_all(values.reshape(count, -1), axes, 0, 0, tiled=True).sum(0)]
    all_to_all x1, waiting for transfers between devices: 12.1 us -> 9.25 us  [exchange_gather(): return lax.all_to_all(copies, axes, 0, 0, tiled=True).reshape(-1)]
    all_to_all x1, starting transfers between devices: 7.85 us -> 5.43 us  [exchange_gather(): return lax.all_to_all(copies, axes, 0, 0, tiled=True).reshape(-1)]
  transfers between devices with their start and end apart: 3 -> 5, of which waited for: 2 -> 3; matrix products, arithmetic and copies ran while one was open for 23% -> 25% of each run, Pallas kernels for 0% -> 0%
where the time goes in v9:
time: 180 us; the launch traced here: 179 us
  waiting for transfers between devices  45.4 us (25%)
  blocking collectives  43.9 us (24%)
  other arithmetic  35.5 us (20%)
  matrix products  17.9 us (10%)
  between operations  14.7 us (8%)
  starting transfers between devices  14.1 us (8%)
  local copies, waits for them, and re-layouts  7.77 us (4%)
    all_gather x1, waiting for transfers between devices, shards(): weights = lax.all_gather(w_up, FSDP, axis=0, tiled=True)  34 us
    all_to_all x1, blocking collectives, exchange_gather(): return lax.all_to_all(copies, axes, 0, 0, tiled=True).reshape(-1)  19.3 us
    all_to_all x1, blocking collectives, exchange_sum(): lax.all_to_all(values.reshape(count, -1), axes, 0, 0, tiled=True).sum(0)  16.4 us
    reduce_sum x1, other arithmetic, conv_norm(): centre = jnp.mean(conv_out, axis=-1, keepdims=True)  13.2 us
    all_to_all x1, waiting for transfers between devices, exchange_gather(): return lax.all_to_all(copies, axes, 0, 0, tiled=True).reshape(-1)  9.25 us
    dot_general x1, matrix products, shards(): pre_act = jnp.dot(flat, weights, preferred_element_type=jnp.float32)  9.2 us
    reduce_sum x2, other arithmetic, norm_conv_grads(): tap_sums.append(jnp.sum(window * grad_conv, axis=(0, 1, 2)))  8.79 us
    all_gather x1, blocking collectives, shards(): full_maps = lax.all_gather(images, 'row', axis=1, tiled=True)  8.27 us
  transfers between devices with their start and end apart: 5, of which 3 were waited for; matrix products, arithmetic and copies ran while one was open for 25% of the time, Pallas kernels for 0%

profile of v9, /device:TPU:1, one launch (start us, length us, event | category | flops | bytes accessed | tf_op | source)
XLA Modules:
  0.0 179.4 jit_solution(6874179498710865527)
XLA Ops:
  7.2 0.0 all-gather.2.cloned.1.call-start
  7.2 0.7 all-gather.2.cloned.1.call-update
  7.9 0.0 reduce-scatter.2.cloned.1.call-start
  7.9 0.0 copy-start.7
  8.0 8.3 %all_gather.6 = bf16[1,16,16,1536]{3,2,0,1:T(8,128)(2,1)S(1)} all-gather(bf16[1,8,16,1536]{3,2,0,1:T(8,128)(2,1)} %bitcast.26), channel_id=1, replica_groups=mesh['dp_hi'=2,'z'=12,'row'=2,'y'=8,'core'=2] {'row'}, dimensions={1}, use_global_device_ids=true | all-gather | bytes 1179648 | tf_op jit(solution)/shard_map/all_gather | solution.py:83
  16.2 0.0 copy-start.1
  16.2 0.2 convert_element_type.24
  16.4 0.0 copy-done.7
  16.4 0.2 slice_reduce_fusion.46
  16.6 0.3 slice_reduce_fusion.48
  16.9 0.3 slice_reduce_fusion.47
  17.3 0.0 copy-done.1
  17.3 13.2 %fusion.18 = (f32[16,16]{1,0:T(8,128)S(1)}, f32[1,16,16,1536]{3,2,0,1:T(8,128)S(1)}) fusion(f32[1536]{0:T(1024)S(1)} %get-tuple-element.117, f32[1536]{0:T(1024)S(1)} %get-tuple-element.118, f32[1536]{0:T(1024)S(1)} %get-tuple-element.71, f32[1536]{0:T(1024)S(1)} %get-tuple-element.72, f32[1536]{0:T(1024)S(1)} %get-tuple-element.73, ...), kind=kLoop, calls=%fused_computation.194 | loop fusion | flops 38928128 | bytes 3453952 | tf_op jit(solution)/shard_map/reduce_sum | solution.py:25
  30.5 0.0 copy-start.8
  30.5 0.0 copy-start.9
  30.6 0.3 multiply_reduce_fusion.52
  30.9 0.4 copy-done.8
  31.2 0.0 copy-done.9
  31.3 1.2 add_convert_fusion
  32.5 34.0 %all-gather.2.cloned.1.call-done = bf16[1536,1536]{1,0:T(8,128)(2,1)} async-done(((bf16[96,1536]{1,0:T(8,128)(2,1)}), bf16[1536,1536]{1,0:T(8,128)(2,1)}) %all-gather.2.cloned.1.call-update) | async-done | bytes 4718608 | tf_op jit(solution)/shard_map/all_gather | solution.py:90
  66.5 0.0 copy-start.3
  66.5 9.2 %fusion.5 = (bf16[256,1536]{1,0:T(8,128)(2,1)S(1)}, f32[256,1536]{1,0:T(8,128)}, f32[256,1536]{1,0:T(8,128)}) fusion(bf16[1,16,16,1536]{3,2,1,0:T(8,128)(2,1)} %param.13, bf16[256,1536]{1,0:T(8,128)(2,1)} %bitcast.23, bf16[1536,1536]{1,0:T(8,128)(2,1)} %all-gather.2.cloned.1.call-done), kind=kOutput, calls=%fused_computation.57 | convolution fusion | flops 1236664320 | bytes 10223616 | tf_op jit(solution)/shard_map/dot_general | solution.py:91
  75.7 0.0 copy-start.6
  75.7 0.9 copy-done.6
  76.6 0.0 copy-done.3
  76.6 3.5 %convolution_convert_fusion = bf16[1536,1536]{1,0:T(8,128)(2,1)} fusion(bf16[256,1536]{1,0:T(8,128)(2,1)S(1)} %bitcast.24, bf16[256,1536]{1,0:T(8,128)(2,1)S(1)} %get-tuple-element.120), kind=kOutput, calls=%fused_computation.48 | convolution fusion | flops 1210318848 | bytes 6291456 | tf_op jit(solution)/shard_map/dot_general | solution.py:98
  80.1 0.0 reduce-scatter.2.cloned.1.call-update
  80.2 5.2 %fusion.15 = (f32[1536]{0:T(1024)S(1)}, f32[256]{0:T(256)S(1)}, f32[256,1536]{1,0:T(8,128)}) fusion(f32[1536]{0:T(1024)S(1)} %copy-done.8, bf16[256,1536]{1,0:T(8,128)(2,1)} %copy-done.6, bf16[1536,1536]{1,0:T(8,128)(2,1)} %all-gather.2.cloned.1.call-done), kind=kOutput, calls=%fused_computation.192 | convolution fusion | flops 1209137408 | bytes 7091200 | tf_op jit(solution)/shard_map/dot_general | solution.py:105
  85.4 0.1 div.17
  85.5 0.0 copy-start
  85.5 2.5 %multiply_reduce_fusion = (f32[1536]{0:T(1024)S(1)}, f32[16,16]{1,0:T(8,128)S(1)}) fusion(f32[1,16,16,1536]{3,2,0,1:T(8,128)S(1)} %get-tuple-element.123, f32[16,16]{1,0:T(8,128)S(1)} %add_rsqrt_fusion, f32[16,16]{1,0:T(8,128)S(1)} %broadcast_multiply_fusion.1, f32[256,1536]{1,0:T(8,128)} %get-tuple-element.125, f32[1,16,16,1536]{3,2,0,1:T(8,128)} %bitcast.22, ...), kind=kLoop, calls=%fused_computation.60 | loop fusion | flops 2750720 | bytes 4733952 | tf_op jit(solution)/shard_map/reduce_sum | solution.py:35
  88.0 0.0 copy-done
  88.0 4.9 %multiply_reduce_fusion.1 = (f32[1536]{0:T(1024)S(1)}, f32[1536]{0:T(1024)S(1)}, f32[1536]{0:T(1024)S(1)}, f32[1536]{0:T(1024)S(1)}, f32[1536]{0:T(1024)S(1)}, /...) fusion(f32[1,16,16,1536]{3,2,0,1:T(8,128)S(1)} %convert_element, ...), kind=kLoop, calls=%fused_computation.61 | loop fusion | flops 16880640 | bytes 6412288 | tf_op jit(solution)/shard_map/reduce_sum | solution.py:46
  92.9 0.0 copy-start.2
  92.9 3.9 %multiply_reduce_fusion.19 = (f32[1536]{0:T(1024)S(1)}, f32[1536]{0:T(1024)S(1)}, f32[1536]{0:T(1024)S(1)}, f32[1536]{0:T(1024)S(1)}, f32[1536]{0:T(1024)S(1)}, ...) fusion(f32[1,16,16,1536]{3,2,0,1:T(8,128)S(1)} %get-tuple-eleme, ...), kind=kLoop, calls=%fused_computation.79 | loop fusion | flops 14128128 | bytes 3256320 | tf_op jit(solution)/shard_map/reduce_sum | solution.py:46
  97.1 0.0 copy-done.2
  97.1 2.5 %fusion.16 = (f32[1536]{0:T(1024)S(1)}, f32[1536]{0:T(1024)S(1)}, f32[1536]{0:T(1024)S(1)}, f32[1536]{0:T(1024)S(1)}, f32[1536]{0:T(1024)S(1)}, /*index=5*/f32[1...) fusion(f32[1,16,16,1536]{3,2,0,1:T(8,128)S(1)} %get-tuple-eleme, ...), kind=kLoop, calls=%fused_computation.193 | loop fusion | flops 10988544 | bytes 4018176 | tf_op jit(solution)/shard_map/reduce_sum | solution.py:41
  100.0 0.5 concatenate.19
  100.6 0.0 copy-start.5
  100.6 0.0 copy-start.4
  100.6 0.7 dynamic_slice.7
  101.3 2.3 %collective-permute-start = (f32[39936]{0:T(1024)}, f32[39936]{0:T(1024)}, u32[]{:S(2)}, u32[]{:S(2)}) collective-permute-start(f32[39936]{0:T(1024)} %dynamic_slice.7), channel_id=1, source_target_pairs={{0,1},{1,0},{2,3},{3,2},{4,5},{5,4},{6,7},{7,6},{8,9},{9,8},{10,11... | collective-permute-start | bytes 479240 | tf_op jit(solution)/shard_map/ppermute | solution.py:69
  103.6 1.4 collective-permute-done
  105.1 1.6 dynamic-slice_add_fusion
  106.7 1.2 all_to_all.14
  107.8 16.4 %all_to_all.21 = f32[32,1,1248]{2,1,0:T(1,128)S(1)} all-to-all(f32[32,1,1248]{2,1,0:T(1,128)S(1)} %all_to_all.14), channel_id=1, replica_groups=mesh['dp_hi'=2,'z'=12,'row'=2,'y'=8,'core'=2] {'dp_hi','row','y'}, dimensions={0} | all-to-all | bytes 319488 | tf_op jit(solution)/shard_map/all_to_all | solution.py:53
  124.2 0.1 reduce_sum.578
  124.4 19.3 %all_to_all.22 = f32[12,1,1248]{2,1,0:T(1,128)S(1)} all-to-all(f32[12,1,1248]{2,1,0:T(1,128)S(1)} %broadcast_in_dim.11), channel_id=1, replica_groups=mesh['dp_hi'=2,'z'=12,'row'=2,'y'=8,'core'=2] {'z'}, dimensions={0} | all-to-all | bytes 119808 | tf_op jit(solution)/shard_map/all_to_all | solution.py:59
  143.7 0.8 broadcast_in_dim.12
  144.5 5.4 %all-to-all-start.2 = ((f32[32,1,1248]{2,1,0:T(1,128)}), f32[32,1,1248]{2,1,0:T(1,128)S(1)}, u32[]{:S(2)}, u32[]{:S(2)}) async-start(f32[32,1,1248]{2,1,0:T(1,128)} %broadcast_in_dim.12), calls=%async_computation.3 | async-start | bytes 327680 | tf_op jit(solution)/shard_map/all_to_all | solution.py:59
  149.9 9.3 %all-to-all-done.2 = f32[32,1,1248]{2,1,0:T(1,128)S(1)} async-done(((f32[32,1,1248]{2,1,0:T(1,128)}), f32[32,1,1248]{2,1,0:T(1,128)S(1)}, u32[]{:S(2)}, u32[]{:S(2)}) %all-to-all-start.2) | async-done | bytes 159776 | tf_op jit(solution)/shard_map/all_to_all | solution.py:59
  159.2 0.4 reduce.56
  159.6 0.1 reshape.281
  159.7 6.3 %collective-permute-start.1 = (f32[39936]{0:T(1024)S(1)}, f32[39936]{0:T(1024)}, u32[]{:S(2)}, u32[]{:S(2)}) collective-permute-start(f32[39936]{0:T(1024)S(1)} %reshape.281), channel_id=1, source_target_pairs={{0,1},{1,0},{2,3},{3,2},{4,5},{5,4},{6,7},{7,6},{8,9},{9,8},{10,11... | collective-permute-start | bytes 479240 | tf_op jit(solution)/shard_map/ppermute | solution.py:74
  166.0 0.0 copy-done.5
  166.1 0.0 copy-done.4
  166.1 1.1 multiply_convert_fusion
  167.2 0.2 concatenate.22
  167.4 0.0 collective-permute-done.1
  167.4 1.0 fusion.13
  168.4 0.8 reshape.282
  169.2 0.9 concatenate.23
  170.1 0.6 fusion.14
  170.8 1.8 %bitcast_convert_fusion = f32[1,96,1536]{2,1,0:T(8,128)} fusion(bf16[96,1536]{1,0:T(8,128)(2,1)} %reduce-scatter.2.cloned.1.call-done), kind=kLoop, calls=%fused_computation.134 | loop fusion | flops 147456 | bytes 884736 | tf_op jit(solution)/shard_map/broadcast_in_dim | solution.py:116
  (60 shorter events, 0.5 us)
Async XLA Ops:
  7.2 59.3 %all-gather.2.cloned.1.call-start = ((), (), s32[]{:S(2)}) async-start(), calls=%async_computation.4 | async-start | bytes 5013504 | tf_op jit(solution)/shard_map/all_gather | solution.py:90
  7.9 162.9 %reduce-scatter.2.cloned.1.call-start = ((), (), s32[]{:S(2)}) async-start(), calls=%async_computation.5 | async-start | bytes 5013504 | tf_op jit(solution)/shard_map/reduce_scatter | solution.py:97
  7.9 8.5 %copy-start.7 = (f32[7,7,1536]{2,1,0:T(8,128)S(1)}, f32[7,7,1536]{2,1,0:T(8,128)}, u32[]{:S(2)}) copy-start(f32[7,7,1536]{2,1,0:T(8,128)} %param.8) | copy-start | bytes 903172
  16.2 1.0 copy-start.1
  30.5 0.7 copy-start.8
  30.5 0.7 copy-start.9
  66.5 10.1 %copy-start.3 = (bf16[1,16,16,1536]{3,2,0,1:T(8,128)(2,1)S(1)}, bf16[1,16,16,1536]{3,2,0,1:T(8,128)(2,1)}, u32[]{:S(2)}) copy-start(bf16[1,16,16,1536]{3,2,0,1:T(8,128)(2,1)} %add_convert_fusion) | copy-start | bytes 2359300
  75.7 0.9 copy-start.6
  85.5 2.5 %copy-start = (f32[256,1536]{1,0:T(8,128)S(1)}, f32[256,1536]{1,0:T(8,128)}, u32[]{:S(2)}) copy-start(f32[256,1536]{1,0:T(8,128)} %get-tuple-element.125) | copy-start | bytes 4718596
  92.9 4.2 %copy-start.2 = (bf16[1,16,16,1536]{3,2,0,1:T(8,128)(2,1)S(1)}, bf16[1,16,16,1536]{3,2,0,1:T(8,128)(2,1)}, u32[]{:S(2)}) copy-start(bf16[1,16,16,1536]{3,2,0,1:T(8,128)(2,1)} %copy-done.1) | copy-start | bytes 2359300
  100.6 65.5 %copy-start.5 = (f32[256,1536]{1,0:T(8,128)S(1)}, f32[256,1536]{1,0:T(8,128)}, u32[]{:S(2)}) copy-start(f32[256,1536]{1,0:T(8,128)} %get-tuple-element.124) | copy-start | bytes 4718596
  100.6 65.4 %copy-start.4 = (f32[256,1536]{1,0:T(8,128)S(1)}, f32[256,1536]{1,0:T(8,128)}, u32[]{:S(2)}) copy-start(f32[256,1536]{1,0:T(8,128)} %get-tuple-element.121) | copy-start | bytes 4718596
  101.3 3.7 %collective-permute-start = (f32[39936]{0:T(1024)}, f32[39936]{0:T(1024)}, u32[]{:S(2)}, u32[]{:S(2)}) collective-permute-start(f32[39936]{0:T(1024)} %dynamic_slice.7), channel_id=1, source_target_pairs={{0,1},{1,0},{2,3},{3,2},{4,5},{5,4},{6,7},{7,6},{8,9},{9,8},{10,11... | collective-permute-start | bytes 479240 | tf_op jit(solution)/shard_map/ppermute | solution.py:69
  144.5 14.7 %all-to-all-start.2 = ((f32[32,1,1248]{2,1,0:T(1,128)}), f32[32,1,1248]{2,1,0:T(1,128)S(1)}, u32[]{:S(2)}, u32[]{:S(2)}) async-start(f32[32,1,1248]{2,1,0:T(1,128)} %broadcast_in_dim.12), calls=%async_computation.3 | async-start | bytes 327680 | tf_op jit(solution)/shard_map/all_to_all | solution.py:59
  159.7 7.7 %collective-permute-start.1 = (f32[39936]{0:T(1024)S(1)}, f32[39936]{0:T(1024)}, u32[]{:S(2)}, u32[]{:S(2)}) collective-permute-start(f32[39936]{0:T(1024)S(1)} %reshape.281), channel_id=1, source_target_pairs={{0,1},{1,0},{2,3},{3,2},{4,5},{5,4},{6,7},{7,6},{8,9},{9,8},{10,11... | collective-permute-start | bytes 479240 | tf_op jit(solution)/shard_map/ppermute | solution.py:74
Sparse Core Ops, SparseCore 0:
  10.4 56.0 all-gather.1
  80.3 67.6 reduce-scatter.1

commit v10 on v6

--- a/solution.py
+++ b/solution.py
@@ -60,7 +60,7 @@
 
 
 def packed_sum(values):
-    inner, outer = ("dp_hi", "row") + FSDP, "z"
+    inner, outer = ("dp_hi", "z", "row", "core"), "y"
     values = exchange_sum(values, inner)
     values = exchange_gather(values, outer).reshape(lax.axis_size(outer), -1).sum(0)
     return exchange_gather(values, inner)

time: 178 us -> 194 us (1.090)
  waiting for transfers between devices: 46.8 us -> 55 us
  local copies, waits for them, and re-layouts: 7.05 us -> 11.4 us
  blocking collectives: 50.1 us -> 53.9 us
    all_to_all x1, blocking collectives: 22.6 us -> 35.1 us  [exchange_sum(): lax.all_to_all(values.reshape(count, -1), axes, 0, 0, tiled=True).sum(0)]
    all_to_all x1, blocking collectives: 19.2 us -> 10.5 us  [exchange_gather(): return lax.all_to_all(copies, axes, 0, 0, tiled=True).reshape(-1)]
    all_to_all x1, waiting for transfers between devices: 12.1 us -> 20.3 us  [exchange_gather(): return lax.all_to_all(copies, axes, 0, 0, tiled=True).reshape(-1)]
    concatenate x1, local copies, waits for them, and re-layouts: 0.55 us -> 4.81 us  [shards(): jnp.concatenate([kernel_part.reshape(taps, channels), vector_part], axis=0)]
  transfers between devices with their start and end apart: 3 -> 3, of which waited for: 2 -> 2; matrix products, arithmetic and copies ran while one was open for 23% -> 24% of each run, Pallas kernels for 0% -> 0%
where the time goes in v10:
time: 194 us; the launch traced here: 193 us
  waiting for transfers between devices  55 us (28%)
  blocking collectives  53.9 us (28%)
  other arithmetic  33.8 us (17%)
  matrix products  17.9 us (9%)
  between operations  14.7 us (8%)
  local copies, waits for them, and re-layouts  11.4 us (6%)
  starting transfers between devices  6.71 us (3%)
    all_to_all x1, blocking collectives, exchange_sum(): lax.all_to_all(values.reshape(count, -1), axes, 0, 0, tiled=True).sum(0)  35.1 us
    all_gather x1, waiting for transfers between devices, shards(): weights = lax.all_gather(w_up, FSDP, axis=0, tiled=True)  34 us
    all_to_all x1, waiting for transfers between devices, exchange_gather(): return lax.all_to_all(copies, axes, 0, 0, tiled=True).reshape(-1)  20.3 us
    reduce_sum x1, other arithmetic, conv_norm(): centre = jnp.mean(conv_out, axis=-1, keepdims=True)  13.2 us
    all_to_all x1, blocking collectives, exchange_gather(): return lax.all_to_all(copies, axes, 0, 0, tiled=True).reshape(-1)  10.5 us
    dot_general x1, matrix products, shards(): pre_act = jnp.dot(flat, weights, preferred_element_type=jnp.float32)  9.19 us
    reduce_sum x2, other arithmetic, norm_conv_grads(): tap_sums.append(jnp.sum(window * grad_conv, axis=(0, 1, 2)))  8.78 us
    all_gather x1, blocking collectives, shards(): full_maps = lax.all_gather(images, 'row', axis=1, tiled=True)  8.27 us
  transfers between devices with their start and end apart: 3, of which 2 were waited for; matrix products, arithmetic and copies ran while one was open for 24% of the time, Pallas kernels for 0%

profile of v10, /device:TPU:1, one launch (start us, length us, event | category | flops | bytes accessed | tf_op | source)
XLA Modules:
  0.0 193.4 jit_solution(6787578603070701705)
XLA Ops:
  7.2 0.0 all-gather.2.cloned.1.call-start
  7.2 0.7 all-gather.2.cloned.1.call-update
  7.9 0.0 reduce-scatter.2.cloned.1.call-start
  7.9 0.0 copy-start.7
  8.0 8.3 %all_gather.6 = bf16[1,16,16,1536]{3,2,0,1:T(8,128)(2,1)S(1)} all-gather(bf16[1,8,16,1536]{3,2,0,1:T(8,128)(2,1)} %bitcast.28), channel_id=1, replica_groups=mesh['dp_hi'=2,'z'=12,'row'=2,'y'=8,'core'=2] {'row'}, dimensions={1}, use_global_device_ids=true | all-gather | bytes 1179648 | tf_op jit(solution)/shard_map/all_gather | solution.py:74
  16.2 0.0 copy-start.1
  16.2 0.2 convert_element_type.24
  16.4 0.0 copy-done.7
  16.4 0.2 slice_reduce_fusion.46
  16.6 0.3 slice_reduce_fusion.48
  16.9 0.3 slice_reduce_fusion.47
  17.3 0.0 copy-done.1
  17.3 13.2 %fusion.16 = (f32[16,16]{1,0:T(8,128)S(1)}, f32[1,16,16,1536]{3,2,0,1:T(8,128)S(1)}) fusion(f32[1536]{0:T(1024)S(1)} %get-tuple-element.117, f32[1536]{0:T(1024)S(1)} %get-tuple-element.118, f32[1536]{0:T(1024)S(1)} %get-tuple-element.71, f32[1536]{0:T(1024)S(1)} %get-tuple-element.72, f32[1536]{0:T(1024)S(1)} %get-tuple-element.73, ...), kind=kLoop, calls=%fused_computation.187 | loop fusion | flops 38928128 | bytes 3453952 | tf_op jit(solution)/shard_map/reduce_sum | solution.py:25
  30.5 0.0 copy-start.8
  30.5 0.0 copy-start.9
  30.6 0.3 multiply_reduce_fusion.52
  30.9 0.4 copy-done.8
  31.2 0.0 copy-done.9
  31.3 1.2 add_convert_fusion
  32.5 34.0 %all-gather.2.cloned.1.call-done = bf16[1536,1536]{1,0:T(8,128)(2,1)} async-done(((bf16[96,1536]{1,0:T(8,128)(2,1)}), bf16[1536,1536]{1,0:T(8,128)(2,1)}) %all-gather.2.cloned.1.call-update) | async-done | bytes 4718608 | tf_op jit(solution)/shard_map/all_gather | solution.py:81
  66.5 0.0 copy-start.3
  66.5 9.2 %fusion.5 = (bf16[256,1536]{1,0:T(8,128)(2,1)S(1)}, f32[256,1536]{1,0:T(8,128)}, f32[256,1536]{1,0:T(8,128)}) fusion(bf16[1,16,16,1536]{3,2,1,0:T(8,128)(2,1)} %param.13, bf16[256,1536]{1,0:T(8,128)(2,1)} %bitcast.24, bf16[1536,1536]{1,0:T(8,128)(2,1)} %all-gather.2.cloned.1.call-done), kind=kOutput, calls=%fused_computation.57 | convolution fusion | flops 1236664320 | bytes 10223616 | tf_op jit(solution)/shard_map/dot_general | solution.py:82
  75.7 0.0 copy-start.6
  75.7 0.9 copy-done.6
  76.6 0.0 copy-done.3
  76.6 3.5 %convolution_convert_fusion = bf16[1536,1536]{1,0:T(8,128)(2,1)} fusion(bf16[256,1536]{1,0:T(8,128)(2,1)S(1)} %bitcast.25, bf16[256,1536]{1,0:T(8,128)(2,1)S(1)} %get-tuple-element.120), kind=kOutput, calls=%fused_computation.48 | convolution fusion | flops 1210318848 | bytes 6291456 | tf_op jit(solution)/shard_map/dot_general | solution.py:89
  80.1 0.0 reduce-scatter.2.cloned.1.call-update
  80.1 5.2 %fusion.13 = (f32[1536]{0:T(1024)S(1)}, f32[256]{0:T(256)S(1)}, f32[256,1536]{1,0:T(8,128)}) fusion(f32[1536]{0:T(1024)S(1)} %copy-done.8, bf16[256,1536]{1,0:T(8,128)(2,1)} %copy-done.6, bf16[1536,1536]{1,0:T(8,128)(2,1)} %all-gather.2.cloned.1.call-done), kind=kOutput, calls=%fused_computation.185 | convolution fusion | flops 1209137408 | bytes 7091200 | tf_op jit(solution)/shard_map/dot_general | solution.py:96
  85.3 0.1 div.17
  85.4 0.0 copy-start
  85.4 2.5 %multiply_reduce_fusion = (f32[1536]{0:T(1024)S(1)}, f32[16,16]{1,0:T(8,128)S(1)}) fusion(f32[1,16,16,1536]{3,2,0,1:T(8,128)S(1)} %get-tuple-element.123, f32[16,16]{1,0:T(8,128)S(1)} %add_rsqrt_fusion, f32[16,16]{1,0:T(8,128)S(1)} %broadcast_multiply_fusion.1, f32[256,1536]{1,0:T(8,128)} %get-tuple-element.125, f32[1,16,16,1536]{3,2,0,1:T(8,128)} %bitcast.23, ...), kind=kLoop, calls=%fused_computation.60 | loop fusion | flops 2750720 | bytes 4733952 | tf_op jit(solution)/shard_map/reduce_sum | solution.py:35
  88.0 0.0 copy-done
  88.0 4.9 %multiply_reduce_fusion.1 = (f32[1536]{0:T(1024)S(1)}, f32[1536]{0:T(1024)S(1)}, f32[1536]{0:T(1024)S(1)}, f32[1536]{0:T(1024)S(1)}, f32[1536]{0:T(1024)S(1)}, /...) fusion(f32[1,16,16,1536]{3,2,0,1:T(8,128)S(1)} %convert_element, ...), kind=kLoop, calls=%fused_computation.61 | loop fusion | flops 16880640 | bytes 6412288 | tf_op jit(solution)/shard_map/reduce_sum | solution.py:46
  92.9 0.0 copy-start.2
  92.9 3.9 %multiply_reduce_fusion.19 = (f32[1536]{0:T(1024)S(1)}, f32[1536]{0:T(1024)S(1)}, f32[1536]{0:T(1024)S(1)}, f32[1536]{0:T(1024)S(1)}, f32[1536]{0:T(1024)S(1)}, ...) fusion(f32[1,16,16,1536]{3,2,0,1:T(8,128)S(1)} %get-tuple-eleme, ...), kind=kLoop, calls=%fused_computation.79 | loop fusion | flops 14128128 | bytes 3256320 | tf_op jit(solution)/shard_map/reduce_sum | solution.py:46
  96.8 0.0 copy-done.2
  96.8 2.5 %fusion.14 = (f32[1536]{0:T(1024)S(1)}, f32[1536]{0:T(1024)S(1)}, f32[1536]{0:T(1024)S(1)}, f32[1536]{0:T(1024)S(1)}, f32[1536]{0:T(1024)S(1)}, /*index=5*/f32[1...) fusion(f32[1,16,16,1536]{3,2,0,1:T(8,128)S(1)} %get-tuple-eleme, ...), kind=kLoop, calls=%fused_computation.186 | loop fusion | flops 10988544 | bytes 4018176 | tf_op jit(solution)/shard_map/reduce_sum | solution.py:41
  100.0 0.0 copy-start.5
  100.0 4.8 %concatenate.3 = f32[52,1536]{1,0:T(8,128)} concatenate(f32[1,1536]{1,0:T(1,128)S(1)} %stack.156, f32[1,1536]{1,0:T(1,128)S(1)} %stack.157, f32[1,1536]{1,0:T(1,128)S(1)} %stack.158, f32[1,1536]{1,0:T(1,128)S(1)} %stack.159, f32[1,1536]{1,0:T(1,128)S(1)} %stack.160, f32[1,1536]{1,0:T(1,128)S(1)} %stack.161, f32[1,1536]{1,0:T(1,128)S(1)} %stack.162, f32[1,1536]{1,0:T(1,128)S(1)} %stack.163, ...), dimensions={0} | concatenate | bytes 638976 | tf_op jit(solution)/shard_map/concatenate | solution.py:103
  104.8 0.0 copy-start.4
  104.8 1.5 all_to_all.14
  106.4 35.1 %all_to_all.21 = f32[96,1,832]{2,1,0:T(1,128)} all-to-all(f32[96,1,832]{2,1,0:T(1,128)S(1)} %all_to_all.14), channel_id=1, replica_groups=mesh['dp_hi'=2,'z'=12,'row'=2,'y'=8,'core'=2] {'dp_hi','z','row','core'}, dimensions={0} | all-to-all | bytes 638976 | tf_op jit(solution)/shard_map/all_to_all | solution.py:53
  141.4 1.2 reduce_sum.578
  142.7 10.5 %all_to_all.22 = f32[8,1,832]{2,1,0:T(1,128)S(1)} all-to-all(f32[8,1,832]{2,1,0:T(1,128)S(1)} %broadcast_in_dim.11), channel_id=1, replica_groups=mesh['dp_hi'=2,'z'=12,'row'=2,'y'=8,'core'=2] {'y'}, dimensions={0} | all-to-all | bytes 53248 | tf_op jit(solution)/shard_map/all_to_all | solution.py:59
  153.3 0.9 broadcast_in_dim.12
  154.2 6.6 %all-to-all-start.2 = ((f32[96,1,832]{2,1,0:T(1,128)}), f32[96,1,832]{2,1,0:T(1,128)S(1)}, u32[]{:S(2)}, u32[]{:S(2)}) async-start(f32[96,1,832]{2,1,0:T(1,128)} %broadcast_in_dim.12), calls=%async_computation.3 | async-start | bytes 688128 | tf_op jit(solution)/shard_map/all_to_all | solution.py:59
  160.8 0.0 copy-done.5
  160.8 0.0 copy-done.4
  160.8 1.1 multiply_convert_fusion
  162.0 20.3 %all-to-all-done.2 = f32[96,1,832]{2,1,0:T(1,128)S(1)} async-done(((f32[96,1,832]{2,1,0:T(1,128)}), f32[96,1,832]{2,1,0:T(1,128)S(1)}, u32[]{:S(2)}, u32[]{:S(2)}) %all-to-all-start.2) | async-done | bytes 319520 | tf_op jit(solution)/shard_map/all_to_all | solution.py:59
  182.3 0.8 reduce.56
  183.1 0.2 reshape_reshape.4
  183.3 0.6 slice.447
  183.9 0.8 reshape.262
  184.7 0.0 reduce-scatter.2.cloned.1.call-done
  184.7 1.8 bitcast_convert_fusion
  (58 shorter events, 0.4 us)
Async XLA Ops:
  7.2 59.3 %all-gather.2.cloned.1.call-start = ((), (), s32[]{:S(2)}) async-start(), calls=%async_computation.4 | async-start | bytes 5013504 | tf_op jit(solution)/shard_map/all_gather | solution.py:81
  7.9 176.8 %reduce-scatter.2.cloned.1.call-start = ((), (), s32[]{:S(2)}) async-start(), calls=%async_computation.5 | async-start | bytes 5013504 | tf_op jit(solution)/shard_map/reduce_scatter | solution.py:88
  7.9 8.5 %copy-start.7 = (f32[7,7,1536]{2,1,0:T(8,128)S(1)}, f32[7,7,1536]{2,1,0:T(8,128)}, u32[]{:S(2)}) copy-start(f32[7,7,1536]{2,1,0:T(8,128)} %param.8) | copy-start | bytes 903172
  16.2 1.0 copy-start.1
  30.5 0.7 copy-start.8
  30.5 0.7 copy-start.9
  66.5 10.1 %copy-start.3 = (bf16[1,16,16,1536]{3,2,0,1:T(8,128)(2,1)S(1)}, bf16[1,16,16,1536]{3,2,0,1:T(8,128)(2,1)}, u32[]{:S(2)}) copy-start(bf16[1,16,16,1536]{3,2,0,1:T(8,128)(2,1)} %add_convert_fusion) | copy-start | bytes 2359300
  75.7 0.9 copy-start.6
  85.4 2.6 %copy-start = (f32[256,1536]{1,0:T(8,128)S(1)}, f32[256,1536]{1,0:T(8,128)}, u32[]{:S(2)}) copy-start(f32[256,1536]{1,0:T(8,128)} %get-tuple-element.125) | copy-start | bytes 4718596
  92.9 4.0 %copy-start.2 = (bf16[1,16,16,1536]{3,2,0,1:T(8,128)(2,1)S(1)}, bf16[1,16,16,1536]{3,2,0,1:T(8,128)(2,1)}, u32[]{:S(2)}) copy-start(bf16[1,16,16,1536]{3,2,0,1:T(8,128)(2,1)} %copy-done.1) | copy-start | bytes 2359300
  100.0 60.8 %copy-start.5 = (f32[256,1536]{1,0:T(8,128)S(1)}, f32[256,1536]{1,0:T(8,128)}, u32[]{:S(2)}) copy-start(f32[256,1536]{1,0:T(8,128)} %get-tuple-element.124) | copy-start | bytes 4718596
  104.8 56.0 %copy-start.4 = (f32[256,1536]{1,0:T(8,128)S(1)}, f32[256,1536]{1,0:T(8,128)}, u32[]{:S(2)}) copy-start(f32[256,1536]{1,0:T(8,128)} %get-tuple-element.121) | copy-start | bytes 4718596
  154.2 28.1 %all-to-all-start.2 = ((f32[96,1,832]{2,1,0:T(1,128)}), f32[96,1,832]{2,1,0:T(1,128)S(1)}, u32[]{:S(2)}, u32[]{:S(2)}) async-start(f32[96,1,832]{2,1,0:T(1,128)} %broadcast_in_dim.12), calls=%async_computation.3 | async-start | bytes 688128 | tf_op jit(solution)/shard_map/all_to_all | solution.py:59
Sparse Core Ops, SparseCore 0:
  10.4 56.0 all-gather.1
  80.2 66.7 reduce-scatter.1
